TPU v7x, 128 devices: a whole 4x4x4 slice. The times are simulated.
128 devices in a mesh: gx: 4 (over x), gy: 16 (over z, y), wa: 2 (over core).
Axes of the slice: x: 4, y: 4, z: 4, core: 2. Of those that a mesh axis runs over, the one named last changes fastest.
Arguments:
- pressure: float32 [24, 256, 512], P(None, ('gy', 'wa'), 'gx'), may hold values from -6 to 6
- saturation: float32 [24, 256, 512], P(None, ('gy', 'wa'), 'gx'), may hold values from 0.1 to 0.9
- sat_old: float32 [24, 256, 512], P(None, ('gy', 'wa'), 'gx'), may hold values from 0.1 to 0.9
- pore: float32 [24, 256, 512], P(None, ('gy', 'wa'), 'gx'), may hold values from 0.5 to 2
- trans_x: float32 [24, 256, 512], P(None, ('gy', 'wa'), 'gx'), may hold values from 0.3 to 3
- trans_y: float32 [24, 256, 512], P(None, ('gy', 'wa'), 'gx'), may hold values from 0.3 to 3
- trans_z: float32 [24, 256, 512], P(None, ('gy', 'wa'), 'gx'), may hold values from 0.3 to 3
- upwind_x: int32 [24, 256, 512], P(None, ('gy', 'wa'), 'gx'), may hold values 0 or 1
- upwind_y: int32 [24, 256, 512], P(None, ('gy', 'wa'), 'gx'), may hold values 0 or 1
- upwind_z: int32 [24, 256, 512], P(None, ('gy', 'wa'), 'gx'), may hold values 0 or 1
- directions: float32 [4, 2, 24, 256, 512], P(None, None, None, ('gy', 'wa'), 'gx'), may hold values from -6 to 6
- adjoint_weights: float32 [4, 2, 24, 256, 512], P(None, None, None, ('gy', 'wa'), 'gx'), may hold values from -6 to 6
- perf_well: int32 [4096], P(('gx', 'gy', 'wa')), may hold values from 0 to 2047, as said below
- perf_col: int32 [4096], P(('gx', 'gy', 'wa')), may hold values from 0 to 1023
- perf_top: int32 [4096], P(('gx', 'gy', 'wa')), may hold values from 0 to 11
- perf_span: int32 [4096], P(('gx', 'gy', 'wa')), may hold values from 1 to 12
- perf_index: float32 [4096], P(('gx', 'gy', 'wa')), may hold values from 0.5 to 2
- bhp: float32 [2048], replicated, may hold values from -6 to 6
- target: float32 [2048], replicated, may hold values from -4 to 4
Outputs:
- reduced_residual: float32 [2, 24, 256, 512], P(None, None, ('gy', 'wa'), 'gx')
- forward_products: float32 [4, 2, 24, 256, 512], P(None, None, None, ('gy', 'wa'), 'gx')
- adjoint_products: float32 [4, 2, 24, 256, 512], P(None, None, None, ('gy', 'wa'), 'gx')
Inputs may be any that keep to these rules, and one draw needn't show every extreme that they name: `perf_well`: every well is named by at least one perforation row; well w is owned by device w // 16 of the axes gx+gy+wa.
All inputs are finite; a program needn't handle non-finite values. No bound on the sum of `upwind_x` or of `upwind_y` or of `upwind_z` on one device may be relied on, other than what follows from the above.
Results may differ from a plain program's by a relative error of at most 0.0002.
Values sent between devices are 32-bit elements; how exact they have to be, the bound alone decides.
No kernel may reach another device: no remote copies, remote signals or barrier semaphores. Data moves between devices by JAX's collectives and lax.ppermute only.
A program may use at most 64 MiB of HBM per device.

v0:
```python
import functools

import jax
import jax.numpy as jnp
from jax import lax
from jax.sharding import Mesh
from jax.sharding import PartitionSpec as P

GY_WA = ("gy_0", "gy_1", "wa")
GX_GY_WA = ("gx", "gy_0", "gy_1", "wa")


water_visc = 0.5
oil_visc = 2.0
water_head = 0.3
oil_head = 0.2


def extended(shard, sides, width):
    edges = {}
    for axis, dim in sides:
        peers, length = (lax.axis_size(axis), shard.shape[dim])
        up = [(i, (i + 1) % peers) for i in range(peers - 1)]
        last = lax.slice_in_dim(shard, length - width, length, axis=dim)
        initial = lax.slice_in_dim(shard, 0, width, axis=dim)
        edges[dim] = (
            lax.ppermute(last, axis, up),
            lax.ppermute(initial, axis, [(b, a) for a, b in up]),
        )
    done = []
    for _, dim in sides:
        low, high = edges[dim]
        around = [(width, width) if d in done else (0, 0) for d in range(shard.ndim)]
        shard = jnp.concatenate([jnp.pad(low, around), shard, jnp.pad(high, around)], axis=dim)
        done.append(dim)
    return shard


def one_axis_at_a_time(shard, axes):
    return functools.reduce(lax.psum, axes, shard)


def mobility(sat):
    return jnp.stack([sat * sat / water_visc, (1.0 - sat) * (1.0 - sat) / oil_visc])


def mobility_slope(sat):
    return jnp.stack([2.0 * sat / water_visc, -2.0 * (1.0 - sat) / oil_visc])


def face_flux(trans, lower_up, first, second, heads):
    sat_up = jnp.where(lower_up, first[1], second[1])
    drop = first[0] - second[0]
    potential = jnp.stack([drop + heads[0], drop + heads[1]])
    return trans * mobility(sat_up) * potential


def well_factors(sums, goal):
    return jnp.concatenate([((sums[1] - goal) / sums[0])[None], sums[2:] / sums[0][None]], axis=0)


def body(
    pressure,
    saturation,
    sat_old,
    pore,
    trans_x,
    trans_y,
    trans_z,
    upwind_x,
    upwind_y,
    upwind_z,
    directions,
    adjoint_weights,
    perf_well,
    perf_col,
    perf_top,
    perf_span,
    perf_index,
    bhp,
    target,
):
    state = jnp.stack([pressure, saturation])
    layers, rows, cols = pressure.shape
    spatial = (layers, rows, cols)
    ndir = directions.shape[0]
    nwells = target.shape[0]
    last_x = lax.axis_index("gx") == lax.axis_size("gx") - 1
    last_y = lax.axis_index(GY_WA) == lax.axis_size(GY_WA) - 1
    col_keep = jnp.where(jnp.logical_and(last_x, jnp.arange(cols) == cols - 1), 0.0, 1.0)
    row_keep = jnp.where(jnp.logical_and(last_y, jnp.arange(rows) == rows - 1), 0.0, 1.0)
    trans_xe = trans_x * col_keep[None, None, :]
    trans_ye = trans_y * row_keep[None, :, None]
    flag_x = upwind_x.astype(jnp.float32)
    flag_y = upwind_y.astype(jnp.float32)
    count = 2 + 4 * ndir
    cell_data = jnp.concatenate(
        [
            state,
            directions.reshape((2 * ndir,) + spatial),
            adjoint_weights.reshape((2 * ndir,) + spatial),
        ],
        axis=0,
    )
    stacked = jnp.concatenate([cell_data, jnp.stack([trans_xe, trans_ye, flag_x, flag_y])], axis=0)
    padded = extended(stacked, ((GY_WA, 2), ("gx", 3)), 1)
    cells_pad = padded[:count]
    tx_face = padded[count, :, 1:-1, :-1]
    ty_face = padded[count + 1, :, :-1, 1:-1]
    ux_face = padded[count + 2, :, 1:-1, :-1]
    uy_face = padded[count + 3, :, :-1, 1:-1]
    state_pad = cells_pad[:2]
    dir_pad = cells_pad[2 : 2 + 2 * ndir].reshape((ndir, 2) + cells_pad.shape[1:])
    wts_pad = cells_pad[2 + 2 * ndir :].reshape((ndir, 2) + cells_pad.shape[1:])
    lower_x = ux_face > 0.5
    lower_y = uy_face > 0.5
    lower_z = upwind_z[:-1] == 1
    trans_zf = trans_z[:-1]

    def divergence(padded_state):
        fx = face_flux(
            tx_face,
            lower_x,
            padded_state[:, :, 1:-1, :-1],
            padded_state[:, :, 1:-1, 1:],
            (0.0, 0.0),
        )
        div = jnp.pad(fx, ((0, 0), (0, 0), (1, 1), (0, 1))) - jnp.pad(
            fx, ((0, 0), (0, 0), (1, 1), (1, 0))
        )
        fy = face_flux(
            ty_face,
            lower_y,
            padded_state[:, :, :-1, 1:-1],
            padded_state[:, :, 1:, 1:-1],
            (0.0, 0.0),
        )
        div = (
            div
            + jnp.pad(fy, ((0, 0), (0, 0), (0, 1), (1, 1)))
            - jnp.pad(fy, ((0, 0), (0, 0), (1, 0), (1, 1)))
        )
        inner = padded_state[:, :, 1:-1, 1:-1]
        fz = face_flux(trans_zf, lower_z, inner[:, :-1], inner[:, 1:], (water_head, oil_head))
        vertical = jnp.pad(fz, ((0, 0), (0, 1), (0, 0), (0, 0))) - jnp.pad(
            fz, ((0, 0), (1, 0), (0, 0), (0, 0))
        )
        return div + jnp.pad(vertical, ((0, 0), (0, 0), (1, 1), (1, 1)))

    flux_div, pullback = jax.vjp(divergence, state_pad)

    def pulled(cot):
        return pullback(cot)[0]

    unused, pushback = jax.vjp(pulled, jnp.zeros_like(flux_div))
    forward_flux = jax.vmap(lambda item: pushback(item)[0])(dir_pad)[..., 1:-1, 1:-1]
    adjoint_flux = jax.vmap(pulled)(wts_pad)[..., 1:-1, 1:-1]
    change = saturation - sat_old
    accum = jnp.stack([pore * change, -pore * change])
    forward_acc = jnp.stack([pore * directions[:, 1], -pore * directions[:, 1]], axis=1)
    adjoint_acc = jnp.stack(
        [
            jnp.zeros_like(adjoint_weights[:, 0]),
            pore * (adjoint_weights[:, 0] - adjoint_weights[:, 1]),
        ],
        axis=1,
    )
    flat_count = rows * cols
    perf_rows = perf_col.shape[0]

    def at_perfs(field):
        return jnp.take(field.reshape(field.shape[:-2] + (flat_count,)), perf_col, axis=-1)

    p_cells = at_perfs(pressure)
    s_cells = at_perfs(saturation)
    depth = jnp.arange(layers)[:, None]
    open_layer = jnp.logical_and(
        depth >= perf_top[None, :], depth < (perf_top + perf_span)[None, :]
    )
    weight = jnp.where(open_layer, perf_index[None, :], 0.0)
    row_bhp = jnp.take(bhp, perf_well)
    drive = p_cells - row_bhp
    mob = mobility(s_cells)
    slope = mobility_slope(s_cells)
    mob_total = mob[0] + mob[1]
    slope_total = slope[0] + slope[1]
    rates = weight * mob * drive
    dir_cells = at_perfs(directions)
    wts_cells = at_perfs(adjoint_weights)
    rate_tangent = weight * (mob * dir_cells[:, 0:1] + slope * drive * dir_cells[:, 1:2])
    grad_p = weight * (mob[0] * wts_cells[:, 0] + mob[1] * wts_cells[:, 1])
    grad_s = weight * drive * (slope[0] * wts_cells[:, 0] + slope[1] * wts_cells[:, 1])
    row_sums = jnp.concatenate(
        [
            jnp.sum(weight * mob_total, axis=0)[None],
            jnp.sum(rates[0] + rates[1], axis=0)[None],
            jnp.sum(rate_tangent[:, 0] + rate_tangent[:, 1], axis=1),
            jnp.sum(grad_p, axis=1),
        ],
        axis=0,
    )
    to_slots = (perf_well[:, None] == jnp.arange(nwells)[None, :]).astype(jnp.float32)
    totals = jnp.dot(row_sums, to_slots, precision=lax.Precision.HIGHEST)
    factors = well_factors(one_axis_at_a_time(totals, GX_GY_WA), target)
    row_factors = jnp.take(factors, perf_well, axis=1)
    wells_res = rates - weight * mob * row_factors[0]
    wells_fwd = rate_tangent - (weight * mob)[None] * row_factors[1 : 1 + ndir][:, None, None, :]
    out_f = row_factors[1 + ndir :][:, None, :]
    wells_adj = jnp.stack(
        [grad_p - weight * mob_total * out_f, grad_s - weight * slope_total * drive * out_f], axis=1
    )
    combined = jnp.concatenate([wells_res[None], wells_fwd, wells_adj], axis=0)
    from_perfs = (perf_col[:, None] == jnp.arange(flat_count)[None, :]).astype(jnp.float32)
    spread = jnp.dot(
        combined.reshape(-1, perf_rows), from_perfs, precision=lax.Precision.HIGHEST
    ).reshape((1 + 2 * ndir, 2) + spatial)
    reduced_residual = flux_div[:, :, 1:-1, 1:-1] + accum + spread[0]
    forward_products = forward_flux + forward_acc + spread[1 : 1 + ndir]
    adjoint_products = adjoint_flux + adjoint_acc + spread[1 + ndir :]
    return (reduced_residual, forward_products, adjoint_products)


def solution(mesh):
    split = Mesh(
        mesh.devices.reshape(mesh.shape["gx"], 4, 4, mesh.shape["wa"]), ("gx", "gy_0", "gy_1", "wa")
    )
    return jax.shard_map(
        body,
        mesh=split,
        in_specs=(
            P(None, GY_WA, "gx"),
            P(None, GY_WA, "gx"),
            P(None, GY_WA, "gx"),
            P(None, GY_WA, "gx"),
            P(None, GY_WA, "gx"),
            P(None, GY_WA, "gx"),
            P(None, GY_WA, "gx"),
            P(None, GY_WA, "gx"),
            P(None, GY_WA, "gx"),
            P(None, GY_WA, "gx"),
            P(None, None, None, GY_WA, "gx"),
            P(None, None, None, GY_WA, "gx"),
            P(GX_GY_WA),
            P(GX_GY_WA),
            P(GX_GY_WA),
            P(GX_GY_WA),
            P(GX_GY_WA),
            P(),
            P(),
        ),
        out_specs=(
            P(None, None, GY_WA, "gx"),
            P(None, None, None, GY_WA, "gx"),
            P(None, None, None, GY_WA, "gx"),
        ),
        check_vma=False,
    )
```

profile of v0, /device:TPU:27, one launch (start us, length us, event | category | flops | bytes accessed | tf_op | source)
XLA Modules:
  0.0 245.5 jit_solution(8731900309420484959)
XLA Ops:
  8.2 2.2 copy.192
  14.0 3.8 %collective-permute-start.1 = (f32[22,24,1,128]{3,1,2,0:T(8,128)}, f32[22,24,1,128]{3,1,2,0:T(8,128)S(1)}, u32[]{:S(2)}, u32[]{:S(2)}) collective-permute-start(f32[22,24,1,128]{3,1,2,0:T(8,128)} %get-tuple-element.63), channel_id=1, source_target_pairs={{0,1},{1,2},{2,3},{3,4},{4,5},{5,6},{6,7},{7,8},{8,9},{9,10},{10,1... | collective-permute-start | bytes 811016 | tf_op jit(solution)/shard_map/ppermute | solution.py:27
  17.7 1.9 collective-permute-start.2
  19.7 2.8 %fusion.77 = (f32[22,24,8,1]{3,1,2,0:T(8,128)}, f32[22,24,8,1]{3,1,2,0:T(8,128)}) fusion(f32[22,24,8,128]{3,1,2,0:T(8,128)S(1)} %bitcast_dynamic-update-slice_fusion), kind=kLoop, calls=%fused_computation.269 | loop fusion | bytes 67584 | tf_op jit(solution)/shard_map/slice | solution.py:24
  22.4 3.3 %copy.198 = f32[22,24,8,1]{1,2,3,0:T(8,128)} copy(f32[22,24,8,1]{3,1,2,0:T(8,128)} %get-tuple-element.61) | data formatting | bytes 33792 | tf_op jit(solution)/shard_map/slice | solution.py:24
  25.8 3.1 %collective-permute-start = (f32[22,24,8,1]{1,2,3,0:T(8,128)}, f32[22,24,8,1]{1,2,3,0:T(8,128)}, u32[]{:S(2)}, u32[]{:S(2)}) collective-permute-start(f32[22,24,8,1]{1,2,3,0:T(8,128)} %copy.198), channel_id=1, source_target_pairs={{0,32},{32,64},{64,96},{1,33},{33,65},{65,97},{2,34},{34,66},{66,9... | collective-permute-start | bytes 50696 | tf_op jit(solution)/shard_map/ppermute | solution.py:27
  28.9 3.3 %copy.200 = f32[22,24,8,1]{1,2,3,0:T(8,128)} copy(f32[22,24,8,1]{3,1,2,0:T(8,128)} %get-tuple-element.62) | data formatting | bytes 33792 | tf_op jit(solution)/shard_map/slice | solution.py:25
  32.2 2.9 %collective-permute-start.3 = (f32[22,24,8,1]{1,2,3,0:T(8,128)}, f32[22,24,8,1]{1,2,3,0:T(8,128)}, u32[]{:S(2)}, u32[]{:S(2)}) collective-permute-start(f32[22,24,8,1]{1,2,3,0:T(8,128)} %copy.200), channel_id=1, source_target_pairs={{32,0},{64,32},{96,64},{33,1},{65,33},{97,65},{34,2},{66,34},{98,6... | collective-permute-start | bytes 50696 | tf_op jit(solution)/shard_map/ppermute | solution.py:28
  35.2 3.6 %copy.211 = f32[4,2,24,8,128]{2,0,4,3,1:T(4,128)} copy(f32[4,2,24,8,128]{4,3,2,1,0:T(8,128)} %param.33) | data formatting | bytes 1572864 | tf_op args[10]
  38.8 2.7 %copy.213 = f32[4,2,24,8,128]{2,0,4,3,1:T(4,128)} copy(f32[4,2,24,8,128]{4,3,2,1,0:T(8,128)S(1)} %copy-done.4) | data formatting | bytes 1572864 | tf_op args[11]
  41.6 1.9 copy.208
  43.5 1.9 copy.209
  45.4 3.5 %gather_fusion.4 = f32[32,4,2,24]{3,1,2,0:T(4,128)} fusion(f32[4,2,24,1024]{2,0,3,1:T(4,128)} %bitcast.243, s32[1024]{0:T(1024)S(1)} %get-tuple-element.129), kind=kCustom, calls=%fused_computation.1.clone | custom fusion | bytes 49280 | tf_op jit(solution)/shard_map/jit(_take)/gather | solution.py:172
  48.9 3.5 %gather_fusion.5 = f32[32,4,2,24]{3,1,2,0:T(4,128)} fusion(f32[4,2,24,1024]{2,0,3,1:T(4,128)} %bitcast.244, s32[1024]{0:T(1024)S(1)} %get-tuple-element.129), kind=kCustom, calls=%fused_computation.3.clone | custom fusion | bytes 49280 | tf_op jit(solution)/shard_map/jit(_take)/gather | solution.py:172
  52.4 2.2 gather_fusion.2
  71.7 35.6 %all-reduce.50.cloned.1.call-done = f32[10,2048]{1,0:T(8,128)} async-done(((f32[10,2048]{1,0:T(8,128)}), f32[10,2048]{1,0:T(8,128)}) %all-reduce.50.cloned.1.call-update) | async-done | bytes 81936 | tf_op jit(solution)/shard_map/psum | solution.py:40
  108.4 44.2 %all-reduce.52.cloned.1.call-done = f32[10,2048]{1,0:T(8,128)} async-done(((f32[10,2048]{1,0:T(8,128)}), f32[10,2048]{1,0:T(8,128)}) %all-reduce.52.cloned.1.call-update) | async-done | bytes 81936 | tf_op jit(solution)/shard_map/psum | solution.py:40
  155.0 3.3 %copy.199 = f32[22,24,8,1]{3,1,2,0:T(8,128)} copy(f32[22,24,8,1]{1,2,3,0:T(8,128)} %collective-permute-done) | data formatting | bytes 33792 | tf_op jit(solution)/shard_map/ppermute | solution.py:27
  158.3 3.3 %pad.215 = f32[22,24,10,1]{3,1,2,0:T(8,128)} pad(f32[22,24,8,1]{3,1,2,0:T(8,128)} %copy.199, f32[]{:T(128)} %constant.114.clone.1), padding=0_0x0_0x1_1x0_0 | pad | bytes 38020 | tf_op jit(solution)/shard_map/jit(_pad)/pad | solution.py:34
  161.6 3.4 %copy.201 = f32[22,24,8,1]{3,1,2,0:T(8,128)} copy(f32[22,24,8,1]{1,2,3,0:T(8,128)} %collective-permute-done.3) | data formatting | bytes 33792 | tf_op jit(solution)/shard_map/ppermute | solution.py:28
  165.0 3.4 %pad.216 = f32[22,24,10,1]{3,1,2,0:T(8,128)} pad(f32[22,24,8,1]{3,1,2,0:T(8,128)} %copy.201, f32[]{:T(128)} %constant.114.clone.1), padding=0_0x0_0x1_1x0_0 | pad | bytes 38020 | tf_op jit(solution)/shard_map/jit(_pad)/pad | solution.py:34
  168.4 27.2 %all-reduce.54.cloned.1.call-done = f32[10,2048]{1,0:T(8,128)} async-done(((f32[10,2048]{1,0:T(8,128)}), f32[10,2048]{1,0:T(8,128)}) %all-reduce.54.cloned.1.call-update) | async-done | bytes 81936 | tf_op jit(solution)/shard_map/psum | solution.py:40
  195.6 3.7 %pad_maximum_fusion = (f32[8,24,10,130]{3,1,2,0:T(8,128)S(1)}, f32[8,24,10,130]{3,1,2,0:T(8,128)S(1)}) fusion(f32[22,24,10,1]{3,1,2,0:T(8,128)} %pad.216, f32[22,24,10,1]{3,1,2,0:T(8,128)} %pad.215, f32[22,24,1,128]{3,1,2,0:T(8,128)S(1)} %collective-permute-done.2, f32[22,24,8,128]{3,1,2,0:T(8,128)S(1)} %bitcast_dynamic-update-slice_fusion, ...), kind=kLoop, calls=%fused_computation.6 | loop fusion | flops 1996800 | bytes 4742400 | tf_op jit(solution)/shard_map/concatenate | solution.py:34
  215.7 9.8 %all-reduce.56.cloned.1.call-done = f32[10,2048]{1,0:T(8,128)} async-done(((f32[10,2048]{1,0:T(8,128)}), f32[10,2048]{1,0:T(8,128)}) %all-reduce.56.cloned.1.call-update) | async-done | bytes 81936 | tf_op jit(solution)/shard_map/psum | solution.py:40
  (248 shorter events, 54.0 us)
Async XLA Ops:
  7.2 47.4 %copy-start = (f32[2048]{0:T(1024)S(1)}, f32[2048]{0:T(1024)}, u32[]{:S(2)}) copy-start(f32[2048]{0:T(1024)} %param.40) | copy-start | bytes 24580
  7.2 100.0 %all-reduce.50.cloned.1.call-start = ((), (), s32[]{:S(2)}) async-start(), calls=%async_computation | async-start | bytes 262144 | tf_op jit(solution)/shard_map/psum | solution.py:40
  14.0 181.6 %collective-permute-start.1 = (f32[22,24,1,128]{3,1,2,0:T(8,128)}, f32[22,24,1,128]{3,1,2,0:T(8,128)S(1)}, u32[]{:S(2)}, u32[]{:S(2)}) collective-permute-start(f32[22,24,1,128]{3,1,2,0:T(8,128)} %get-tuple-element.63), channel_id=1, source_target_pairs={{0,1},{1,2},{2,3},{3,4},{4,5},{5,6},{6,7},{7,8},{8,9},{9,10},{10,1... | collective-permute-start | bytes 811016 | tf_op jit(solution)/shard_map/ppermute | solution.py:27
  17.7 177.9 %collective-permute-start.2 = (f32[22,24,1,128]{3,1,2,0:T(8,128)}, f32[22,24,1,128]{3,1,2,0:T(8,128)S(1)}, u32[]{:S(2)}, u32[]{:S(2)}) collective-permute-start(f32[22,24,1,128]{3,1,2,0:T(8,128)} %get-tuple-element.64), channel_id=1, source_target_pairs={{1,0},{2,1},{3,2},{4,3},{5,4},{6,5},{7,6},{8,7},{9,8},{10,9},{11,1... | collective-permute-start | bytes 811016 | tf_op jit(solution)/shard_map/ppermute | solution.py:28
  25.8 129.2 %collective-permute-start = (f32[22,24,8,1]{1,2,3,0:T(8,128)}, f32[22,24,8,1]{1,2,3,0:T(8,128)}, u32[]{:S(2)}, u32[]{:S(2)}) collective-permute-start(f32[22,24,8,1]{1,2,3,0:T(8,128)} %copy.198), channel_id=1, source_target_pairs={{0,32},{32,64},{64,96},{1,33},{33,65},{65,97},{2,34},{34,66},{66,9... | collective-permute-start | bytes 50696 | tf_op jit(solution)/shard_map/ppermute | solution.py:27
  32.2 129.3 %collective-permute-start.3 = (f32[22,24,8,1]{1,2,3,0:T(8,128)}, f32[22,24,8,1]{1,2,3,0:T(8,128)}, u32[]{:S(2)}, u32[]{:S(2)}) collective-permute-start(f32[22,24,8,1]{1,2,3,0:T(8,128)} %copy.200), channel_id=1, source_target_pairs={{32,0},{64,32},{96,64},{33,1},{65,33},{97,65},{34,2},{66,34},{98,6... | collective-permute-start | bytes 50696 | tf_op jit(solution)/shard_map/ppermute | solution.py:28
  41.5 17.0 %copy-start.54 = (s32[32]{0:T(128)S(1)}, s32[32]{0:T(128)}, u32[]{:S(2)}) copy-start(s32[32]{0:T(128)} %param.37) | copy-start | bytes 388
  41.6 17.0 %copy-start.59 = (s32[32]{0:T(128)S(1)}, s32[32]{0:T(128)}, u32[]{:S(2)}) copy-start(s32[32]{0:T(128)} %param.38) | copy-start | bytes 388
  41.6 17.0 %copy-start.53 = (f32[32]{0:T(128)S(1)}, f32[32]{0:T(128)}, u32[]{:S(2)}) copy-start(f32[32]{0:T(128)} %param.39) | copy-start | bytes 388
  66.4 86.2 %all-reduce.52.cloned.1.call-start = ((), (), s32[]{:S(2)}) async-start(), calls=%async_computation.1 | async-start | bytes 262144 | tf_op jit(solution)/shard_map/psum | solution.py:40
  107.3 88.3 %all-reduce.54.cloned.1.call-start = ((), (), s32[]{:S(2)}) async-start(), calls=%async_computation.2 | async-start | bytes 262144 | tf_op jit(solution)/shard_map/psum | solution.py:40
  152.6 72.8 %all-reduce.56.cloned.1.call-start = ((), (), s32[]{:S(2)}) async-start(), calls=%async_computation.3 | async-start | bytes 262144 | tf_op jit(solution)/shard_map/psum | solution.py:40
  215.4 13.2 %copy-start.36 = (f32[24,32]{0,1:T(8,128)S(1)}, f32[24,32]{0,1:T(8,128)}, u32[]{:S(2)}) copy-start(f32[24,32]{0,1:T(8,128)} %copy-done.35) | copy-start | bytes 9220
  215.4 13.3 %copy-start.23 = (f32[4,24,32]{1,0,2:T(4,128)S(1)}, f32[4,24,32]{1,0,2:T(4,128)}, u32[]{:S(2)}) copy-start(f32[4,24,32]{1,0,2:T(4,128)} %copy-done.22) | copy-start | bytes 36868
  215.4 13.3 %copy-start.25 = (f32[4,24,32]{1,0,2:T(4,128)S(1)}, f32[4,24,32]{1,0,2:T(4,128)}, u32[]{:S(2)}) copy-start(f32[4,24,32]{1,0,2:T(4,128)} %copy-done.24) | copy-start | bytes 36868
  215.5 13.3 %copy-start.32 = (f32[2,24,32]{1,0,2:T(2,128)S(1)}, f32[2,24,32]{1,0,2:T(2,128)}, u32[]{:S(2)}) copy-start(f32[2,24,32]{1,0,2:T(2,128)} %copy-done.31) | copy-start | bytes 18436
  215.5 13.3 %copy-start.34 = (f32[2,24,32]{1,0,2:T(2,128)S(1)}, f32[2,24,32]{1,0,2:T(2,128)}, u32[]{:S(2)}) copy-start(f32[2,24,32]{1,0,2:T(2,128)} %copy-done.33) | copy-start | bytes 18436
  215.5 13.3 %copy-start.42 = (f32[2,24,32]{1,0,2:T(2,128)S(1)}, f32[2,24,32]{1,0,2:T(2,128)}, u32[]{:S(2)}) copy-start(f32[2,24,32]{1,0,2:T(2,128)} %copy.217) | copy-start | bytes 18436
  215.5 13.4 %copy-start.17 = (f32[4,2,24,32]{2,0,1,3:T(4,128)S(1)}, f32[4,2,24,32]{2,0,1,3:T(4,128)}, u32[]{:S(2)}) copy-start(f32[4,2,24,32]{2,0,1,3:T(4,128)} %copy-done.16) | copy-start | bytes 73732
  215.5 13.4 %copy-start.39 = (f32[24,32]{0,1:T(8,128)S(1)}, f32[24,32]{0,1:T(8,128)}, u32[]{:S(2)}) copy-start(f32[24,32]{0,1:T(8,128)} %copy-done.38) | copy-start | bytes 9220
  215.5 13.4 %copy-start.41 = (f32[24,32]{0,1:T(8,128)S(1)}, f32[24,32]{0,1:T(8,128)}, u32[]{:S(2)}) copy-start(f32[24,32]{0,1:T(8,128)} %copy-done.40) | copy-start | bytes 9220
  215.5 13.4 %copy-start.49 = (f32[24,32]{0,1:T(8,128)S(1)}, f32[24,32]{0,1:T(8,128)}, u32[]{:S(2)}) copy-start(f32[24,32]{0,1:T(8,128)} %get-tuple-element.36) | copy-start | bytes 9220
  215.5 13.4 %copy-start.50 = (f32[24,32]{0,1:T(8,128)S(1)}, f32[24,32]{0,1:T(8,128)}, u32[]{:S(2)}) copy-start(f32[24,32]{0,1:T(8,128)} %get-tuple-element.31) | copy-start | bytes 9220
  215.5 13.4 %copy-start.51 = (f32[24,32]{0,1:T(8,128)S(1)}, f32[24,32]{0,1:T(8,128)}, u32[]{:S(2)}) copy-start(f32[24,32]{0,1:T(8,128)} %get-tuple-element.113) | copy-start | bytes 9220
  (47 other events, 119.7 us)
Sparse Core Ops, SparseCore 0:
  66.5 40.6 all-reduce.49
  109.6 43.0 all-reduce.51
  154.9 40.6 all-reduce.53
  197.9 27.5 all-reduce.55
where the time goes:
time: 248 us; the launch traced here: 246 us
  waiting for transfers between devices  117 us (47%)
  local copies, waits for them, and re-layouts  65.8 us (27%)
  other arithmetic  32.4 us (13%)
  between operations  14.9 us (6%)
  starting transfers between devices  12 us (5%)
  matrix products  3.52 us (1%)
    psum x4, waiting for transfers between devices, one_axis_at_a_time(): return functools.reduce(lax.psum, axes, shard)  117 us
    unnamed x139, local copies, waits for them, and re-layouts  24.2 us
    gather x4, local copies, waits for them, and re-layouts, at_perfs(): jnp.take(field.reshape(field.shape[:-2] + (flat_count,)), perf_col, axis=-1)  10.8 us
    slice x3, local copies, waits for them, and re-layouts, extended(): last = lax.slice_in_dim(shard, length - width, length, axis=dim)  6.98 us
    ppermute x2, starting transfers between devices, extended(): lax.ppermute(last, axis, up)  6.86 us
  transfers between devices with their start and end apart: 8, of which 4 were waited for; matrix products, arithmetic and copies ran while one was open for 33% of the time, Pallas kernels for 0%

commit v1 on v0

--- a/solution.py
+++ b/solution.py
@@ -36,8 +36,16 @@
     return shard
 
 
-def one_axis_at_a_time(shard, axes):
-    return functools.reduce(lax.psum, axes, shard)
+def gather_everywhere(block):
+    held = block[None]
+    for axis in ("wa", "gx", "gy_1", "gy_0"):
+        size = lax.axis_size(axis)
+        step = 1
+        while step < size:
+            other = lax.ppermute(held, axis, [(i, i ^ step) for i in range(size)])
+            held = jnp.concatenate([held, other], axis=0)
+            step *= 2
+    return held
 
 
 def mobility(sat):
@@ -199,10 +207,14 @@
         ],
         axis=0,
     )
-    to_slots = (perf_well[:, None] == jnp.arange(nwells)[None, :]).astype(jnp.float32)
-    totals = jnp.dot(row_sums, to_slots, precision=lax.Precision.HIGHEST)
-    factors = well_factors(one_axis_at_a_time(totals, GX_GY_WA), target)
-    row_factors = jnp.take(factors, perf_well, axis=1)
+    packed = jnp.concatenate([row_sums, perf_well.astype(jnp.float32)[None]], axis=0)
+    everyone = gather_everywhere(packed)
+    all_sums = jnp.moveaxis(everyone[:, :-1], 1, 0).reshape(row_sums.shape[0], -1)
+    all_wells = everyone[:, -1].reshape(-1)
+    same_well = (perf_well.astype(jnp.float32)[:, None] == all_wells[None, :]).astype(jnp.float32)
+    row_totals = jnp.dot(all_sums, same_well.T, precision=lax.Precision.HIGHEST)
+    row_target = jnp.take(target, perf_well)
+    row_factors = well_factors(row_totals, row_target)
     wells_res = rates - weight * mob * row_factors[0]
     wells_fwd = rate_tangent - (weight * mob)[None] * row_factors[1 : 1 + ndir][:, None, None, :]
     out_f = row_factors[1 + ndir :][:, None, :]

time: 248 us -> 164 us (0.66)
  the two profiles are of different devices: /device:TPU:27 before, /device:TPU:0 now
where the time goes in v1:
time: 164 us; the launch traced here: 162 us
  local copies, waits for them, and re-layouts  94.5 us (58%)
  starting transfers between devices  29.9 us (18%)
  other arithmetic  27.9 us (17%)
  waiting for transfers between devices  5.95 us (4%)
  matrix products  2.28 us (1%)
    unnamed x121, local copies, waits for them, and re-layouts  25.1 us
    ppermute x7, starting transfers between devices, gather_everywhere(): other = lax.ppermute(held, axis, [(i, i ^ step) for i in range(size)])  21.3 us
    gather x4, local copies, waits for them, and re-layouts, at_perfs(): jnp.take(field.reshape(field.shape[:-2] + (flat_count,)), perf_col, axis=-1)  10.8 us
    concatenate x4, local copies, waits for them, and re-layouts, gather_everywhere(): held = jnp.concatenate([held, other], axis=0)  9.2 us
    ppermute x7, local copies, waits for them, and re-layouts, gather_everywhere(): other = lax.ppermute(held, axis, [(i, i ^ step) for i in range(size)])  7.81 us
    slice x3, local copies, waits for them, and re-layouts, extended(): last = lax.slice_in_dim(shard, length - width, length, axis=dim)  6.99 us
    ppermute x7, waiting for transfers between devices, gather_everywhere(): other = lax.ppermute(held, axis, [(i, i ^ step) for i in range(size)])  5.94 us
    ppermute x2, starting transfers between devices, extended(): lax.ppermute(last, axis, up)  5.88 us
  transfers between devices with their start and end apart: 11, of which 3 were waited for; matrix products, arithmetic and copies ran while one was open for 62% of the time, Pallas kernels for 0%

profile of v1, /device:TPU:0, one launch (start us, length us, event | category | flops | bytes accessed | tf_op | source)
XLA Modules:
  0.0 162.1 jit_solution(758601831800508028)
XLA Ops:
  1.7 2.2 %copy.285 = f32[4,2,24,8,128]{4,2,3,1,0:T(8,128)} copy(f32[4,2,24,8,128]{4,3,2,1,0:T(8,128)} %param.35) | data formatting | bytes 1572864 | tf_op args[10]
  10.0 2.8 %fusion.73 = (f32[22,24,8,1]{3,1,2,0:T(8,128)}, f32[22,24,8,1]{3,1,2,0:T(8,128)}) fusion(f32[22,24,8,128]{3,1,2,0:T(8,128)S(1)} %bitcast_dynamic-update-slice_fusion), kind=kLoop, calls=%fused_computation.267 | loop fusion | bytes 67584 | tf_op jit(solution)/shard_map/slice | solution.py:24
  12.8 3.3 %copy.291 = f32[22,24,8,1]{1,2,3,0:T(8,128)} copy(f32[22,24,8,1]{3,1,2,0:T(8,128)} %get-tuple-element.63) | data formatting | bytes 33792 | tf_op jit(solution)/shard_map/slice | solution.py:24
  16.1 4.6 %collective-permute-start = (f32[22,24,8,1]{1,2,3,0:T(8,128)}, f32[22,24,8,1]{1,2,3,0:T(8,128)}, u32[]{:S(2)}, u32[]{:S(2)}) collective-permute-start(f32[22,24,8,1]{1,2,3,0:T(8,128)} %copy.291), channel_id=1, source_target_pairs={{0,32},{32,64},{64,96},{1,33},{33,65},{65,97},{2,34},{34,66},{66,9... | collective-permute-start | bytes 50696 | tf_op jit(solution)/shard_map/ppermute | solution.py:27
  20.7 3.3 %copy.293 = f32[22,24,8,1]{1,2,3,0:T(8,128)} copy(f32[22,24,8,1]{3,1,2,0:T(8,128)} %get-tuple-element.64) | data formatting | bytes 33792 | tf_op jit(solution)/shard_map/slice | solution.py:25
  25.5 3.6 %copy.304 = f32[4,2,24,8,128]{2,0,4,3,1:T(4,128)} copy(f32[4,2,24,8,128]{4,3,2,1,0:T(8,128)} %param.35) | data formatting | bytes 1572864 | tf_op args[10]
  29.2 2.7 %copy.306 = f32[4,2,24,8,128]{2,0,4,3,1:T(4,128)} copy(f32[4,2,24,8,128]{4,3,2,1,0:T(8,128)S(1)} %copy-done.5) | data formatting | bytes 1572864 | tf_op args[11]
  36.3 3.5 %gather_fusion.3 = f32[32,4,2,24]{3,1,2,0:T(4,128)} fusion(f32[4,2,24,1024]{2,0,3,1:T(4,128)} %bitcast.256, s32[1024]{0:T(1024)S(1)} %get-tuple-element.126), kind=kCustom, calls=%fused_computation.2.clone | custom fusion | bytes 49280 | tf_op jit(solution)/shard_map/jit(_take)/gather | solution.py:180
  39.8 3.5 %gather_fusion.4 = f32[32,4,2,24]{3,1,2,0:T(4,128)} fusion(f32[4,2,24,1024]{2,0,3,1:T(4,128)} %bitcast.257, s32[1024]{0:T(1024)S(1)} %get-tuple-element.126), kind=kCustom, calls=%fused_computation.5.clone | custom fusion | bytes 49280 | tf_op jit(solution)/shard_map/jit(_take)/gather | solution.py:180
  43.3 2.2 %gather_fusion = f32[32,24]{1,0:T(8,128)} fusion(f32[24,1024]{0,1:T(8,128)} %bitcast.267, s32[1024]{0:T(1024)S(1)} %get-tuple-element.126), kind=kCustom, calls=%fused_computation.clone | custom fusion | bytes 6272 | tf_op jit(solution)/shard_map/jit(_take)/gather | solution.py:180
  60.7 2.2 %collective-permute-start.4 = (f32[1,11,32]{1,2,0:T(8,128)}, f32[1,11,32]{1,2,0:T(8,128)}, u32[]{:S(2)}, u32[]{:S(2)}) collective-permute-start(f32[1,11,32]{1,2,0:T(8,128)} %bitcast.274), channel_id=1, source_target_pairs={{0,1},{1,0},{2,3},{3,2},{4,5},{5,4},{6,7},{7,6},{8,9},{9,8},{10,11... | collective-permute-start | bytes 4232 | tf_op jit(solution)/shard_map/ppermute | solution.py:45
  68.2 2.4 %collective-permute-start.5 = (f32[2,11,32]{2,0,1:T(2,128)S(1)}, f32[2,11,32]{2,0,1:T(2,128)S(1)}, u32[]{:S(2)}, u32[]{:S(2)}) collective-permute-start(f32[2,11,32]{2,0,1:T(2,128)S(1)} %pad_maximum_fusion.20), channel_id=1, source_target_pairs={{0,32},{32,0},{64,96},{96,64},{1,33},{33,1},{65,97},{97,65},{2,34}... | collective-permute-start | bytes 8456 | tf_op jit(solution)/shard_map/ppermute | solution.py:45
  70.6 2.3 %copy_multiply_fusion.1 = (f32[4,1,24,8,128]{4,2,3,0,1:T(8,128)}, f32[4,1,24,8,128]{4,2,3,0,1:T(8,128)}, f32[4,1,24,8,128]{4,2,3,0,1:T(8,128)}) fusion(f32[4,1,24,8,128]{4,3,2,1,0:T(8,128)S(1)} %slice.277, f32[24,8,128]{2,0,1:T(8,128)S(1)} %get-tuple-element.107, f32[24,8,128]{2,0,1:T(8,128)S(1)} %get-tuple-element.109, ...), kind=kLoop, calls=%fused_computation.122 | loop fusion | flops 393216 | bytes 2555904 | tf_op jit(solution)/shard_map/mul | solution.py:168
  72.9 2.8 %collective-permute-start.6 = (f32[4,11,32]{2,0,1:T(4,128)S(1)}, f32[4,11,32]{2,0,1:T(4,128)S(1)}, u32[]{:S(2)}, u32[]{:S(2)}) collective-permute-start(f32[4,11,32]{2,0,1:T(4,128)S(1)} %pad_maximum_fusion.19), channel_id=1, source_target_pairs={{0,64},{32,96},{64,0},{96,32},{1,65},{33,97},{65,1},{97,33},{2,66}... | collective-permute-start | bytes 16904 | tf_op jit(solution)/shard_map/ppermute | solution.py:45
  78.4 2.3 %collective-permute-start.7 = (f32[8,11,32]{2,0,1:T(8,128)S(1)}, f32[8,11,32]{2,0,1:T(8,128)S(1)}, u32[]{:S(2)}, u32[]{:S(2)}) collective-permute-start(f32[8,11,32]{2,0,1:T(8,128)S(1)} %pad_maximum_fusion.17), channel_id=1, source_target_pairs={{0,2},{2,0},{4,6},{6,4},{1,3},{3,1},{5,7},{7,5},{8,10},{10,8},{12,... | collective-permute-start | bytes 33800 | tf_op jit(solution)/shard_map/ppermute | solution.py:45
  83.9 3.6 %collective-permute-start.8 = (f32[16,11,32]{2,0,1:T(8,128)}, f32[16,11,32]{2,0,1:T(8,128)}, u32[]{:S(2)}, u32[]{:S(2)}) collective-permute-start(f32[16,11,32]{2,0,1:T(8,128)} %concatenate.98), channel_id=1, source_target_pairs={{0,4},{2,6},{4,0},{6,2},{1,5},{3,7},{5,1},{7,3},{8,12},{10,14},{12... | collective-permute-start | bytes 67592 | tf_op jit(solution)/shard_map/ppermute | solution.py:45
  90.4 3.5 %concatenate.99 = f32[32,11,32]{2,0,1:T(8,128)} concatenate(f32[1,11,32]{2,0,1:T(1,128)S(1)} %copy.310, f32[1,11,32]{2,0,1:T(1,128)S(1)} %copy.311, f32[2,11,32]{2,0,1:T(2,128)} %copy-done.33, f32[4,11,32]{2,0,1:T(4,128)S(1)} %collective-permute-done.6, f32[8,11,32]{2,0,1:T(8,128)S(1)} %collective-permute-done.7, f32[16,11,32]{2,0,1:T(8,128)} %collective-permute-done.8), dimensions={0} | concatenate | bytes 90112 | tf_op jit(solution)/shard_map/concatenate | solution.py:46
  93.9 4.4 %collective-permute-start.9 = (f32[32,11,32]{2,0,1:T(8,128)}, f32[32,11,32]{2,0,1:T(8,128)}, u32[]{:S(2)}, u32[]{:S(2)}) collective-permute-start(f32[32,11,32]{2,0,1:T(8,128)} %concatenate.99), channel_id=1, source_target_pairs={{0,8},{8,0},{16,24},{24,16},{1,9},{9,1},{17,25},{25,17},{2,10},{10... | collective-permute-start | bytes 135176 | tf_op jit(solution)/shard_map/ppermute | solution.py:45
  109.3 3.6 %collective-permute-start.10 = (f32[64,11,32]{0,2,1:T(8,128)}, f32[64,11,32]{0,2,1:T(8,128)}, u32[]{:S(2)}, u32[]{:S(2)}) collective-permute-start(f32[64,11,32]{0,2,1:T(8,128)} %concatenate.100), channel_id=1, source_target_pairs={{0,16},{8,24},{16,0},{24,8},{1,17},{9,25},{17,1},{25,9},{2,18},{10... | collective-permute-start | bytes 270344 | tf_op jit(solution)/shard_map/ppermute | solution.py:45
  117.4 3.3 %copy.292 = f32[22,24,8,1]{3,1,2,0:T(8,128)} copy(f32[22,24,8,1]{1,2,3,0:T(8,128)} %collective-permute-done) | data formatting | bytes 33792 | tf_op jit(solution)/shard_map/ppermute | solution.py:27
  120.7 3.3 %pad.215 = f32[22,24,10,1]{3,1,2,0:T(8,128)} pad(f32[22,24,8,1]{3,1,2,0:T(8,128)} %copy.292, f32[]{:T(128)} %constant.94.clone.1), padding=0_0x0_0x1_1x0_0 | pad | bytes 38020 | tf_op jit(solution)/shard_map/jit(_pad)/pad | solution.py:34
  124.0 3.4 %copy.294 = f32[22,24,8,1]{3,1,2,0:T(8,128)} copy(f32[22,24,8,1]{1,2,3,0:T(8,128)} %collective-permute-done.3) | data formatting | bytes 33792 | tf_op jit(solution)/shard_map/ppermute | solution.py:28
  127.4 3.4 %pad.216 = f32[22,24,10,1]{3,1,2,0:T(8,128)} pad(f32[22,24,8,1]{3,1,2,0:T(8,128)} %copy.294, f32[]{:T(128)} %constant.94.clone.1), padding=0_0x0_0x1_1x0_0 | pad | bytes 38020 | tf_op jit(solution)/shard_map/jit(_pad)/pad | solution.py:34
  130.7 2.3 %concatenate.101 = f32[128,11,32]{0,2,1:T(8,128)} concatenate(f32[1,11,32]{0,2,1:T(8,128)S(1)} %copy.327, f32[1,11,32]{0,2,1:T(8,128)S(1)} %copy.328, f32[2,11,32]{0,2,1:T(8,128)S(1)} %copy.329, f32[4,11,32]{0,2,1:T(8,128)S(1)} %copy.330, f32[8,11,32]{0,2,1:T(8,128)} %copy.331, f32[16,11,32]{0,2,1:T(8,128)} %copy.332, f32[32,11,32]{0,2,1:T(8,128)} %copy.333, ...), dimensions={0} | concatenate | bytes 360448 | tf_op jit(solution)/shard_map/concatenate | solution.py:46
  (254 shorter events, 86.1 us)
Async XLA Ops:
  0.6 44.8 %copy-start = (f32[2048]{0:T(1024)S(1)}, f32[2048]{0:T(1024)}, u32[]{:S(2)}) copy-start(f32[2048]{0:T(1024)} %param.42) | copy-start | bytes 24580
  7.4 136.8 %collective-permute-start.1 = (f32[22,24,1,128]{3,1,2,0:T(8,128)}, f32[22,24,1,128]{3,1,2,0:T(8,128)S(1)}, u32[]{:S(2)}, u32[]{:S(2)}) collective-permute-start(f32[22,24,1,128]{3,1,2,0:T(8,128)} %get-tuple-element.65), channel_id=1, source_target_pairs={{0,1},{1,2},{2,3},{3,4},{4,5},{5,6},{6,7},{7,8},{8,9},{9,10},{10,1... | collective-permute-start | bytes 811016 | tf_op jit(solution)/shard_map/ppermute | solution.py:27
  8.7 135.5 %collective-permute-start.2 = (f32[22,24,1,128]{3,1,2,0:T(8,128)}, f32[22,24,1,128]{3,1,2,0:T(8,128)S(1)}, u32[]{:S(2)}, u32[]{:S(2)}) collective-permute-start(f32[22,24,1,128]{3,1,2,0:T(8,128)} %get-tuple-element.66), channel_id=1, source_target_pairs={{1,0},{2,1},{3,2},{4,3},{5,4},{6,5},{7,6},{8,7},{9,8},{10,9},{11,1... | collective-permute-start | bytes 811016 | tf_op jit(solution)/shard_map/ppermute | solution.py:28
  16.1 101.2 %collective-permute-start = (f32[22,24,8,1]{1,2,3,0:T(8,128)}, f32[22,24,8,1]{1,2,3,0:T(8,128)}, u32[]{:S(2)}, u32[]{:S(2)}) collective-permute-start(f32[22,24,8,1]{1,2,3,0:T(8,128)} %copy.291), channel_id=1, source_target_pairs={{0,32},{32,64},{64,96},{1,33},{33,65},{65,97},{2,34},{34,66},{66,9... | collective-permute-start | bytes 50696 | tf_op jit(solution)/shard_map/ppermute | solution.py:27
  24.1 99.9 %collective-permute-start.3 = (f32[22,24,8,1]{1,2,3,0:T(8,128)}, f32[22,24,8,1]{1,2,3,0:T(8,128)}, u32[]{:S(2)}, u32[]{:S(2)}) collective-permute-start(f32[22,24,8,1]{1,2,3,0:T(8,128)} %copy.293), channel_id=1, source_target_pairs={{32,0},{64,32},{96,64},{33,1},{65,33},{97,65},{34,2},{66,34},{98,6... | collective-permute-start | bytes 50696 | tf_op jit(solution)/shard_map/ppermute | solution.py:28
  31.9 15.9 %copy-start.44 = (s32[32]{0:T(128)S(1)}, s32[32]{0:T(128)}, u32[]{:S(2)}) copy-start(s32[32]{0:T(128)} %param.39) | copy-start | bytes 388
  31.9 15.9 %copy-start.50 = (s32[32]{0:T(128)S(1)}, s32[32]{0:T(128)}, u32[]{:S(2)}) copy-start(s32[32]{0:T(128)} %param.40) | copy-start | bytes 388
  31.9 16.0 %copy-start.43 = (f32[32]{0:T(128)S(1)}, f32[32]{0:T(128)}, u32[]{:S(2)}) copy-start(f32[32]{0:T(128)} %param.41) | copy-start | bytes 388
  50.7 14.8 %copy-start.20 = (f32[24,32]{0,1:T(8,128)}, f32[24,32]{0,1:T(8,128)S(1)}, u32[]{:S(2)}) copy-start(f32[24,32]{0,1:T(8,128)S(1)} %get-tuple-element.38) | copy-start | bytes 9220
  50.7 14.8 %copy-start.22 = (f32[24,32]{0,1:T(8,128)}, f32[24,32]{0,1:T(8,128)S(1)}, u32[]{:S(2)}) copy-start(f32[24,32]{0,1:T(8,128)S(1)} %get-tuple-element.39) | copy-start | bytes 9220
  60.7 6.7 %collective-permute-start.4 = (f32[1,11,32]{1,2,0:T(8,128)}, f32[1,11,32]{1,2,0:T(8,128)}, u32[]{:S(2)}, u32[]{:S(2)}) collective-permute-start(f32[1,11,32]{1,2,0:T(8,128)} %bitcast.274), channel_id=1, source_target_pairs={{0,1},{1,0},{2,3},{3,2},{4,5},{5,4},{6,7},{7,6},{8,9},{9,8},{10,11... | collective-permute-start | bytes 4232 | tf_op jit(solution)/shard_map/ppermute | solution.py:45
  68.2 4.7 %collective-permute-start.5 = (f32[2,11,32]{2,0,1:T(2,128)S(1)}, f32[2,11,32]{2,0,1:T(2,128)S(1)}, u32[]{:S(2)}, u32[]{:S(2)}) collective-permute-start(f32[2,11,32]{2,0,1:T(2,128)S(1)} %pad_maximum_fusion.20), channel_id=1, source_target_pairs={{0,32},{32,0},{64,96},{96,64},{1,33},{33,1},{65,97},{97,65},{2,34}... | collective-permute-start | bytes 8456 | tf_op jit(solution)/shard_map/ppermute | solution.py:45
  72.9 15.4 %slice-start.1 = ((f32[24,8,128]{2,1,0:T(8,128)}), f32[23,8,128]{2,1,0:T(8,128)S(1)}, s32[]{:S(2)}) async-start(f32[24,8,128]{2,1,0:T(8,128)} %param.31), calls=%async_computation.1 | async-start | bytes 188416 | tf_op jit(solution)/shard_map/slice | solution.py:126
  72.9 15.4 %copy-start.33 = (f32[2,11,32]{2,0,1:T(2,128)}, f32[2,11,32]{2,0,1:T(2,128)S(1)}, u32[]{:S(2)}) copy-start(f32[2,11,32]{2,0,1:T(2,128)S(1)} %collective-permute-done.5) | copy-start | bytes 8452
  72.9 5.4 %collective-permute-start.6 = (f32[4,11,32]{2,0,1:T(4,128)S(1)}, f32[4,11,32]{2,0,1:T(4,128)S(1)}, u32[]{:S(2)}, u32[]{:S(2)}) collective-permute-start(f32[4,11,32]{2,0,1:T(4,128)S(1)} %pad_maximum_fusion.19), channel_id=1, source_target_pairs={{0,64},{32,96},{64,0},{96,32},{1,65},{33,97},{65,1},{97,33},{2,66}... | collective-permute-start | bytes 16904 | tf_op jit(solution)/shard_map/ppermute | solution.py:45
  76.4 21.8 %copy-start.15 = (f32[23,8,128]{2,0,1:T(8,128)}, f32[23,8,128]{2,0,1:T(8,128)S(1)}, u32[]{:S(2)}) copy-start(f32[23,8,128]{2,0,1:T(8,128)S(1)} %get-tuple-element.24) | copy-start | bytes 282628
  78.3 22.9 %copy-start.30 = (f32[4,11,32]{2,0,1:T(4,128)}, f32[4,11,32]{2,0,1:T(4,128)S(1)}, u32[]{:S(2)}) copy-start(f32[4,11,32]{2,0,1:T(4,128)S(1)} %collective-permute-done.6) | copy-start | bytes 16900
  78.4 4.3 %collective-permute-start.7 = (f32[8,11,32]{2,0,1:T(8,128)S(1)}, f32[8,11,32]{2,0,1:T(8,128)S(1)}, u32[]{:S(2)}, u32[]{:S(2)}) collective-permute-start(f32[8,11,32]{2,0,1:T(8,128)S(1)} %pad_maximum_fusion.17), channel_id=1, source_target_pairs={{0,2},{2,0},{4,6},{6,4},{1,3},{3,1},{5,7},{7,5},{8,10},{10,8},{12,... | collective-permute-start | bytes 33800 | tf_op jit(solution)/shard_map/ppermute | solution.py:45
  82.6 15.6 %copy-start.24 = (f32[8,11,32]{2,0,1:T(8,128)}, f32[8,11,32]{2,0,1:T(8,128)S(1)}, u32[]{:S(2)}) copy-start(f32[8,11,32]{2,0,1:T(8,128)S(1)} %collective-permute-done.7) | copy-start | bytes 33796
  83.9 6.5 %collective-permute-start.8 = (f32[16,11,32]{2,0,1:T(8,128)}, f32[16,11,32]{2,0,1:T(8,128)}, u32[]{:S(2)}, u32[]{:S(2)}) collective-permute-start(f32[16,11,32]{2,0,1:T(8,128)} %concatenate.98), channel_id=1, source_target_pairs={{0,4},{2,6},{4,0},{6,2},{1,5},{3,7},{5,1},{7,3},{8,12},{10,14},{12... | collective-permute-start | bytes 67592 | tf_op jit(solution)/shard_map/ppermute | solution.py:45
  88.3 12.9 %copy-start.34 = (f32[2,11,32]{2,0,1:T(2,128)S(1)}, f32[2,11,32]{2,0,1:T(2,128)}, u32[]{:S(2)}) copy-start(f32[2,11,32]{2,0,1:T(2,128)} %copy-done.33) | copy-start | bytes 8452
  93.9 11.6 %collective-permute-start.9 = (f32[32,11,32]{2,0,1:T(8,128)}, f32[32,11,32]{2,0,1:T(8,128)}, u32[]{:S(2)}, u32[]{:S(2)}) collective-permute-start(f32[32,11,32]{2,0,1:T(8,128)} %concatenate.99), channel_id=1, source_target_pairs={{0,8},{8,0},{16,24},{24,16},{1,9},{9,1},{17,25},{25,17},{2,10},{10... | collective-permute-start | bytes 135176 | tf_op jit(solution)/shard_map/ppermute | solution.py:45
  99.1 16.9 %copy-start.4 = (f32[2048]{0:T(1024)S(1)}, f32[2048]{0:T(1024)}, u32[]{:S(2)}) copy-start(f32[2048]{0:T(1024)} %param.43) | copy-start | bytes 24580
  109.3 21.4 %collective-permute-start.10 = (f32[64,11,32]{0,2,1:T(8,128)}, f32[64,11,32]{0,2,1:T(8,128)}, u32[]{:S(2)}, u32[]{:S(2)}) collective-permute-start(f32[64,11,32]{0,2,1:T(8,128)} %concatenate.100), channel_id=1, source_target_pairs={{0,16},{8,24},{16,0},{24,8},{1,17},{9,25},{17,1},{25,9},{2,18},{10... | collective-permute-start | bytes 270344 | tf_op jit(solution)/shard_map/ppermute | solution.py:45
  (41 other events, 139.1 us)

commit v2 on v1

v2 whole, which is shorter than its diff:
```python
import jax
import jax.numpy as jnp
from jax import lax
from jax.experimental import pallas as pl
from jax.experimental.pallas import tpu as pltpu
from jax.sharding import Mesh
from jax.sharding import PartitionSpec as P

GY_WA = ("gy_0", "gy_1", "wa")
GX_GY_WA = ("gx", "gy_0", "gy_1", "wa")


water_visc = 0.5
oil_visc = 2.0
water_head = 0.3
oil_head = 0.2


def gather_everywhere(block):
    held = block[None]
    for axis in ("wa", "gx", "gy_1", "gy_0"):
        size = lax.axis_size(axis)
        step = 1
        while step < size:
            other = lax.ppermute(held, axis, [(i, i ^ step) for i in range(size)])
            held = jnp.concatenate([held, other], axis=0)
            step *= 2
    return held


def shift_along(block, axis, down):
    size = lax.axis_size(axis)
    pairs = [(i, i + 1) for i in range(size - 1)]
    if not down:
        pairs = [(b, a) for a, b in pairs]
    return lax.ppermute(block, axis, pairs)


def mobility(sat):
    return jnp.stack([sat * sat / water_visc, (1.0 - sat) * (1.0 - sat) / oil_visc])


def mobility_slope(sat):
    return jnp.stack([2.0 * sat / water_visc, -2.0 * (1.0 - sat) / oil_visc])


def well_factors(sums, goal):
    return jnp.concatenate([((sums[1] - goal) / sums[0])[None], sums[2:] / sums[0][None]], axis=0)


def face_terms(trans, up, a, b, heads, ndir):
    pa, sa, vpa, vsa, wwa, woa = a
    pb, sb, vpb, vsb, wwb, wob = b
    su = jnp.where(up, sa, sb)
    drop = pa - pb
    pot_w = drop + heads[0]
    pot_o = drop + heads[1]
    tl_w = trans * (su * su / water_visc)
    tl_o = trans * ((1.0 - su) * (1.0 - su) / oil_visc)
    f_w = tl_w * pot_w
    f_o = tl_o * pot_o
    td_w = trans * (2.0 * su / water_visc) * pot_w
    td_o = trans * (-2.0 * (1.0 - su) / oil_visc) * pot_o
    jv_w, jv_o, jt_p, jt_s = [], [], [], []
    for d in range(ndir):
        vsu = jnp.where(up, vsa[d], vsb[d])
        dvp = vpa[d] - vpb[d]
        jv_w.append(td_w * vsu + tl_w * dvp)
        jv_o.append(td_o * vsu + tl_o * dvp)
        dww = wwa[d] - wwb[d]
        dwo = woa[d] - wob[d]
        jt_p.append(dww * tl_w + dwo * tl_o)
        jt_s.append(dww * td_w + dwo * td_o)
    zero = jnp.zeros_like(su)
    as_a = [f_w, f_o] + jv_w + jv_o + jt_p + [jnp.where(up, g, zero) for g in jt_s]
    as_b = [-f_w, -f_o] + [-x for x in jv_w] + [-x for x in jv_o] + [-x for x in jt_p]
    as_b = as_b + [jnp.where(up, zero, g) for g in jt_s]
    return as_a, as_b


def stencil_kernel(
    edge_ref,
    p_ref,
    s_ref,
    so_ref,
    pore_ref,
    tx_ref,
    ty_ref,
    tz_ref,
    ux_ref,
    uy_ref,
    uz_ref,
    d_ref,
    w_ref,
    hxl_ref,
    hxr_ref,
    hyd_ref,
    hyu_ref,
    r_out,
    jv_out,
    jt_out,
):
    ndir = d_ref.shape[0]
    layers, rows, cols = p_ref.shape
    lane = lax.broadcasted_iota(jnp.int32, (rows, cols), 1)
    sub = lax.broadcasted_iota(jnp.int32, (rows, cols), 0)
    first_lane = lane == 0
    last_lane = lane == cols - 1
    first_sub = sub == 0
    last_sub = sub == rows - 1
    cut_x = jnp.logical_and(last_lane, edge_ref[0] == 1)
    cut_y = jnp.logical_and(last_sub, edge_ref[1] == 1)
    nf = 2 + 4 * ndir

    def cells(k):
        out = [p_ref[k], s_ref[k]]
        for half in range(2):
            out += [d_ref[d, half, k] for d in range(ndir)]
        for half in range(2):
            out += [w_ref[d, half, k] for d in range(ndir)]
        return out

    def group(flat):
        return (
            flat[0],
            flat[1],
            flat[2 : 2 + ndir],
            flat[2 + ndir : 2 + 2 * ndir],
            flat[2 + 2 * ndir : 2 + 3 * ndir],
            flat[2 + 3 * ndir : 2 + 4 * ndir],
        )

    def col(ref, k, f):
        return jnp.broadcast_to(ref[k, :, pl.ds(f, 1)], (rows, cols))

    def row(ref, k, f):
        return jnp.broadcast_to(ref[k, pl.ds(f, 1), :], (rows, cols))

    def store(k, vals, add_prev):
        for i in range(nf):
            if i < 2:
                ref, idx = r_out, (i, k)
            elif i < 2 + 2 * ndir:
                j = i - 2
                ref, idx = jv_out, (j % ndir, j // ndir, k)
            else:
                j = i - 2 - 2 * ndir
                ref, idx = jt_out, (j % ndir, j // ndir, k)
            if add_prev:
                ref[idx] = ref[idx] + vals[i]
            else:
                ref[idx] = vals[i]

    def body(k, carry):
        here = cells(k)
        kn = jnp.minimum(k + 1, layers - 1)
        above = cells(kn)
        left = [jnp.where(first_lane, col(hxl_ref, k, f), pltpu.roll(x, 1, 1)) for f, x in enumerate(here)]
        right = [jnp.where(last_lane, col(hxr_ref, k, f), pltpu.roll(x, cols - 1, 1)) for f, x in enumerate(here)]
        down = [jnp.where(first_sub, row(hyd_ref, k, f), pltpu.roll(x, 1, 0)) for f, x in enumerate(here)]
        up_ = [jnp.where(last_sub, row(hyu_ref, k, f), pltpu.roll(x, rows - 1, 0)) for f, x in enumerate(here)]

        tx = tx_ref[k]
        ux = ux_ref[k].astype(jnp.float32)
        ty = ty_ref[k]
        uy = uy_ref[k].astype(jnp.float32)
        tx_f = jnp.where(cut_x, 0.0, tx)
        ty_f = jnp.where(cut_y, 0.0, ty)
        tx_b = jnp.where(first_lane, col(hxl_ref, k, nf), pltpu.roll(tx, 1, 1))
        ux_b = jnp.where(first_lane, col(hxl_ref, k, nf + 1), pltpu.roll(ux, 1, 1))
        ty_b = jnp.where(first_sub, row(hyd_ref, k, nf), pltpu.roll(ty, 1, 0))
        uy_b = jnp.where(first_sub, row(hyd_ref, k, nf + 1), pltpu.roll(uy, 1, 0))
        tz = jnp.where(k < layers - 1, tz_ref[k], 0.0)
        uz = uz_ref[k] == 1

        g_here = group(here)
        acc, _ = face_terms(tx_f, ux > 0.5, g_here, group(right), (0.0, 0.0), ndir)
        _, xb = face_terms(tx_b, ux_b > 0.5, group(left), g_here, (0.0, 0.0), ndir)
        yf, _ = face_terms(ty_f, uy > 0.5, g_here, group(up_), (0.0, 0.0), ndir)
        _, yb = face_terms(ty_b, uy_b > 0.5, group(down), g_here, (0.0, 0.0), ndir)
        zf, zb = face_terms(tz, uz, g_here, group(above), (water_head, oil_head), ndir)
        acc = [a + b + c + e for a, b, c, e in zip(acc, xb, yf, yb)]
        acc = [a + z for a, z in zip(acc, zf)]

        change = here[1] - so_ref[k]
        pore = pore_ref[k]
        acc[0] = acc[0] + pore * change
        acc[1] = acc[1] - pore * change
        for d in range(ndir):
            vs = here[2 + ndir + d]
            acc[2 + d] = acc[2 + d] + pore * vs
            acc[2 + ndir + d] = acc[2 + ndir + d] - pore * vs
            jt_s = 2 + 3 * ndir + d
            acc[jt_s] = acc[jt_s] + pore * (here[2 + 2 * ndir + d] - here[2 + 3 * ndir + d])
        acc = [a + c for a, c in zip(acc, carry)]
        store(k, acc, False)
        return tuple(zb)

    zero = jnp.zeros((rows, cols), jnp.float32)
    lax.fori_loop(0, layers, body, tuple([zero] * nf))


def body(
    pressure,
    saturation,
    sat_old,
    pore,
    trans_x,
    trans_y,
    trans_z,
    upwind_x,
    upwind_y,
    upwind_z,
    directions,
    adjoint_weights,
    perf_well,
    perf_col,
    perf_top,
    perf_span,
    perf_index,
    bhp,
    target,
):
    layers, rows, cols = pressure.shape
    spatial = (layers, rows, cols)
    ndir = directions.shape[0]
    last_x = lax.axis_index("gx") == lax.axis_size("gx") - 1
    last_y = lax.axis_index(GY_WA) == lax.axis_size(GY_WA) - 1
    edge = jnp.stack([last_x, last_y]).astype(jnp.int32)

    lane_hit = (jnp.arange(cols)[:, None] == (perf_col % cols)[None, :]).astype(jnp.float32)
    row_hit = (jnp.arange(rows)[:, None] == (perf_col // cols)[None, :]).astype(jnp.float32)

    def at_perfs(field):
        by_lane = jnp.dot(field, lane_hit, precision=lax.Precision.HIGHEST)
        return jnp.sum(by_lane * row_hit, axis=-2)

    p_cells = at_perfs(pressure)
    s_cells = at_perfs(saturation)
    dir_cells = at_perfs(directions)
    wts_cells = at_perfs(adjoint_weights)
    depth = jnp.arange(layers)[:, None]
    open_layer = jnp.logical_and(
        depth >= perf_top[None, :], depth < (perf_top + perf_span)[None, :]
    )
    weight = jnp.where(open_layer, perf_index[None, :], 0.0)
    row_bhp = jnp.take(bhp, perf_well)
    drive = p_cells - row_bhp
    mob = mobility(s_cells)
    slope = mobility_slope(s_cells)
    mob_total = mob[0] + mob[1]
    slope_total = slope[0] + slope[1]
    rates = weight * mob * drive
    rate_tangent = weight * (mob * dir_cells[:, 0:1] + slope * drive * dir_cells[:, 1:2])
    grad_p = weight * (mob[0] * wts_cells[:, 0] + mob[1] * wts_cells[:, 1])
    grad_s = weight * drive * (slope[0] * wts_cells[:, 0] + slope[1] * wts_cells[:, 1])
    row_sums = jnp.concatenate(
        [
            jnp.sum(weight * mob_total, axis=0)[None],
            jnp.sum(rates[0] + rates[1], axis=0)[None],
            jnp.sum(rate_tangent[:, 0] + rate_tangent[:, 1], axis=1),
            jnp.sum(grad_p, axis=1),
        ],
        axis=0,
    )
    packed = jnp.concatenate([row_sums, perf_well.astype(jnp.float32)[None]], axis=0)
    everyone = gather_everywhere(packed)

    cell_fields = [pressure, saturation] + [directions[d, h] for h in range(2) for d in range(ndir)]
    cell_fields += [adjoint_weights[d, h] for h in range(2) for d in range(ndir)]
    x_low = jnp.stack(
        [f[:, :, cols - 1] for f in cell_fields]
        + [trans_x[:, :, cols - 1], upwind_x[:, :, cols - 1].astype(jnp.float32)],
        axis=-1,
    )
    x_high = jnp.stack([f[:, :, 0] for f in cell_fields], axis=-1)
    y_low = jnp.stack(
        [f[:, rows - 1, :] for f in cell_fields]
        + [trans_y[:, rows - 1, :], upwind_y[:, rows - 1, :].astype(jnp.float32)],
        axis=1,
    )
    y_high = jnp.stack([f[:, 0, :] for f in cell_fields], axis=1)
    hxl = shift_along(x_low, "gx", True)
    hxr = shift_along(x_high, "gx", False)
    hyd = shift_along(y_low, GY_WA, True)
    hyu = shift_along(y_high, GY_WA, False)

    nf = 2 + 4 * ndir
    vmem = pl.BlockSpec(memory_space=pltpu.VMEM)
    flux_r, flux_jv, flux_jt = pl.pallas_call(
        stencil_kernel,
        out_shape=[
            jax.ShapeDtypeStruct((2,) + spatial, jnp.float32),
            jax.ShapeDtypeStruct((ndir, 2) + spatial, jnp.float32),
            jax.ShapeDtypeStruct((ndir, 2) + spatial, jnp.float32),
        ],
        in_specs=[pl.BlockSpec(memory_space=pltpu.SMEM)] + [vmem] * 16,
        out_specs=[vmem] * 3,
        cost_estimate=pl.CostEstimate(
            flops=layers * rows * cols * 1200,
            transcendentals=0,
            bytes_accessed=(10 + 4 * 4 * ndir + 2 + 2 * 2 * ndir) * layers * rows * cols * 4,
        ),
    )(
        edge,
        pressure,
        saturation,
        sat_old,
        pore,
        trans_x,
        trans_y,
        trans_z,
        upwind_x,
        upwind_y,
        upwind_z,
        directions,
        adjoint_weights,
        hxl,
        hxr,
        hyd,
        hyu,
    )

    all_sums = jnp.moveaxis(everyone[:, :-1], 1, 0).reshape(row_sums.shape[0], -1)
    all_wells = everyone[:, -1].reshape(-1)
    same_well = (perf_well.astype(jnp.float32)[:, None] == all_wells[None, :]).astype(jnp.float32)
    row_totals = jnp.dot(all_sums, same_well.T, precision=lax.Precision.HIGHEST)
    row_target = jnp.take(target, perf_well)
    row_factors = well_factors(row_totals, row_target)
    wells_res = rates - weight * mob * row_factors[0]
    wells_fwd = rate_tangent - (weight * mob)[None] * row_factors[1 : 1 + ndir][:, None, None, :]
    out_f = row_factors[1 + ndir :][:, None, :]
    wells_adj = jnp.stack(
        [grad_p - weight * mob_total * out_f, grad_s - weight * slope_total * drive * out_f], axis=1
    )
    combined = jnp.concatenate([wells_res[None], wells_fwd, wells_adj], axis=0)
    by_row = combined[..., None, :] * row_hit
    spread = jnp.dot(by_row, lane_hit.T, precision=lax.Precision.HIGHEST)
    reduced_residual = flux_r + spread[0]
    forward_products = flux_jv + spread[1 : 1 + ndir]
    adjoint_products = flux_jt + spread[1 + ndir :]
    return (reduced_residual, forward_products, adjoint_products)


def solution(mesh):
    split = Mesh(
        mesh.devices.reshape(mesh.shape["gx"], 4, 4, mesh.shape["wa"]), ("gx", "gy_0", "gy_1", "wa")
    )
    return jax.shard_map(
        body,
        mesh=split,
        in_specs=(
            P(None, GY_WA, "gx"),
            P(None, GY_WA, "gx"),
            P(None, GY_WA, "gx"),
            P(None, GY_WA, "gx"),
            P(None, GY_WA, "gx"),
            P(None, GY_WA, "gx"),
            P(None, GY_WA, "gx"),
            P(None, GY_WA, "gx"),
            P(None, GY_WA, "gx"),
            P(None, GY_WA, "gx"),
            P(None, None, None, GY_WA, "gx"),
            P(None, None, None, GY_WA, "gx"),
            P(GX_GY_WA),
            P(GX_GY_WA),
            P(GX_GY_WA),
            P(GX_GY_WA),
            P(GX_GY_WA),
            P(),
            P(),
        ),
        out_specs=(
            P(None, None, GY_WA, "gx"),
            P(None, None, None, GY_WA, "gx"),
            P(None, None, None, GY_WA, "gx"),
        ),
        check_vma=False,
    )
```

time: 164 us -> 90.9 us (0.55)
  the two profiles are of different devices: /device:TPU:0 before, /device:TPU:63 now
where the time goes in v2:
time: 90.9 us; the launch traced here: 90.3 us
  waiting for transfers between devices  22.2 us (24%)
  starting transfers between devices  21.6 us (24%)
  local copies, waits for them, and re-layouts  19.8 us (22%)
  other arithmetic  11.6 us (13%)
  Pallas kernels  7.71 us (8%)
  matrix products  6.03 us (7%)
  between operations  1.37 us (2%)
    ppermute x7, waiting for transfers between devices, gather_everywhere(): other = lax.ppermute(held, axis, [(i, i ^ step) for i in range(size)])  22.2 us
    ppermute x4, starting transfers between devices, shift_along(): return lax.ppermute(block, axis, pairs)  15.6 us
    pallas_call x1, Pallas kernels, body(): pl.pallas_call(stencil_kernel, out_shape=[jax.ShapeDtypeStruct((2,) + spa...  7.71 us
    slice x9, local copies, waits for them, and re-layouts, body(): x_high = jnp.stack([f[:, :, 0] for f in cell_fields], axis=-1)  6.16 us
    ppermute x7, starting transfers between devices, gather_everywhere(): other = lax.ppermute(held, axis, [(i, i ^ step) for i in range(size)])  6 us
    dot_general x4, matrix products, at_perfs(): by_lane = jnp.dot(field, lane_hit, precision=lax.Precision.HIGHEST)  4.56 us
    add x1, other arithmetic, body(): adjoint_products = flux_jt + spread[1 + ndir:]  2.77 us
    another operation x1, local copies, waits for them, and re-layouts, body(): x_high = jnp.stack([f[:, :, 0] for f in cell_fields], axis=-1)  2.59 us
  transfers between devices with their start and end apart: 11, of which 5 were waited for; matrix products, arithmetic and copies ran while one was open for 24% of the time, Pallas kernels for 0%

profile of v2, /device:TPU:63, one launch (start us, length us, event | category | flops | bytes accessed | tf_op | source)
XLA Modules:
  0.0 90.3 jit_solution(4923003220241537911)
XLA Ops:
  1.4 1.2 %fusion.88 = (f32[32]{0:T(128)}, f32[1,32]{1,0:T(1,128)S(1)}, s32[32]{0:T(128)S(1)}) fusion(s32[32]{0:T(128)} %param.33), kind=kLoop, calls=%fused_computation.167 | loop fusion | flops 128 | bytes 512 | tf_op jit(solution)/shard_map/convert_element_type | solution.py:266
  4.1 1.1 %fusion.9 = f32[24,32]{1,0:T(8,128)S(1)} fusion(f32[24,8,128]{2,1,0:T(8,128)} %p_ref.1, f32[8,32]{1,0:T(8,128)S(1)} %fusion.41, s32[32]{0:T(128)S(1)} %get-tuple-element.142), kind=kOutput, calls=%fused_computation.15 | convolution fusion | flops 9452800 | bytes 102528 | tf_op jit(solution)/shard_map/dot_general | solution.py:235
  5.2 1.1 %fusion.8 = f32[24,32]{1,0:T(8,128)S(1)} fusion(f32[24,8,128]{2,1,0:T(8,128)} %s_ref.1, f32[8,32]{1,0:T(8,128)S(1)} %fusion.41, s32[32]{0:T(128)S(1)} %get-tuple-element.142), kind=kOutput, calls=%fused_computation.14 | convolution fusion | flops 9452800 | bytes 102528 | tf_op jit(solution)/shard_map/dot_general | solution.py:235
  6.4 1.7 %fusion.5 = f32[4,2,24,32]{3,2,1,0:T(8,128)S(1)} fusion(f32[4,2,24,8,128]{4,3,2,1,0:T(8,128)} %w_ref.1, f32[8,32]{1,0:T(8,128)S(1)} %fusion.41, s32[32]{0:T(128)S(1)} %get-tuple-element.142), kind=kOutput, calls=%fused_computation.9 | convolution fusion | flops 75593728 | bytes 812160 | tf_op jit(solution)/shard_map/dot_general | solution.py:235
  18.0 2.6 %stack.48 = f32[24,8,18]{2,1,0:T(8,128)} concatenate(f32[24,8,1]{2,1,0:T(8,128)S(1)} %get-tuple-element.177, f32[24,8,1]{2,1,0:T(8,128)S(1)} %get-tuple-element.106, f32[24,8,1]{2,1,0:T(8,128)} %get-tuple-element.159, f32[24,8,1]{2,1,0:T(8,128)} %get-tuple-element.102, f32[24,8,1]{2,1,0:T(8,128)} %get-tuple-element.157, f32[24,8,1]{2,1,0:T(8,128)} %get-tuple-element.98, ...), dimensions={2} | concatenate | bytes 27648 | tf_op jit(solution)/shard_map/stack | solution.py:276
  20.5 3.1 %collective-permute-start.1 = (f32[24,8,18]{2,1,0:T(8,128)}, f32[24,8,18]{2,1,0:T(8,128)}, u32[]{:S(2)}, u32[]{:S(2)}) collective-permute-start(f32[24,8,18]{2,1,0:T(8,128)} %stack.48), channel_id=1, source_target_pairs={{32,0},{64,32},{96,64},{33,1},{65,33},{97,65},{34,2},{66,34},{98,6... | collective-permute-start | bytes 41480 | tf_op jit(solution)/shard_map/ppermute | solution.py:36
  23.6 1.0 %slice.367 = f32[24,8,1]{2,1,0:T(8,128)S(1)} slice(f32[24,8,128]{2,1,0:T(8,128)} %tx_ref.1), slice={[0:24], [0:8], [127:128]} | slice | bytes 1536 | tf_op jit(solution)/shard_map/slice | solution.py:273
  24.6 1.0 %slice_convert_fusion = f32[24,8,1]{2,1,0:T(8,128)S(1)} fusion(s32[24,8,128]{2,1,0:T(8,128)} %ux_ref.1), kind=kLoop, calls=%fused_computation.34 | loop fusion | flops 192 | bytes 1536 | tf_op jit(solution)/shard_map/convert_element_type | solution.py:273
  25.6 2.3 %stack.47 = f32[24,8,20]{2,1,0:T(8,128)} concatenate(f32[24,8,1]{2,1,0:T(8,128)S(1)} %get-tuple-element.176, f32[24,8,1]{2,1,0:T(8,128)S(1)} %get-tuple-element.107, f32[24,8,1]{2,1,0:T(8,128)S(1)} %get-tuple-element.158, f32[24,8,1]{2,1,0:T(8,128)S(1)} %get-tuple-element.103, f32[24,8,1]{2,1,0:T(8,128)S(1)} %get-tuple-element.156, f32[24,8,1]{2,1,0:T(8,128)S(1)} %get-tuple-element.99, ...), dimensions={2} | concatenate | bytes 30720 | tf_op jit(solution)/shard_map/stack | solution.py:271
  27.9 1.4 %collective-permute-start = (f32[24,8,20]{2,1,0:T(8,128)}, f32[24,8,20]{2,1,0:T(8,128)}, u32[]{:S(2)}, u32[]{:S(2)}) collective-permute-start(f32[24,8,20]{2,1,0:T(8,128)} %stack.47), channel_id=1, source_target_pairs={{0,32},{32,64},{64,96},{1,33},{33,65},{65,97},{2,34},{34,66},{66,9... | collective-permute-start | bytes 46088 | tf_op jit(solution)/shard_map/ppermute | solution.py:36
  29.7 2.2 %collective-permute-start.5 = (f32[2,11,32]{2,1,0:T(8,128)S(1)}, f32[2,11,32]{2,1,0:T(8,128)S(1)}, u32[]{:S(2)}, u32[]{:S(2)}) collective-permute-start(f32[2,11,32]{2,1,0:T(8,128)S(1)} %pad_maximum_fusion.3), channel_id=1, source_target_pairs={{0,32},{32,0},{64,96},{96,64},{1,33},{33,1},{65,97},{97,65},{2,34}... | collective-permute-start | bytes 8456 | tf_op jit(solution)/shard_map/ppermute | solution.py:25
  31.9 2.8 %collective-permute-done.5 = f32[2,11,32]{2,1,0:T(8,128)S(1)} collective-permute-done((f32[2,11,32]{2,1,0:T(8,128)S(1)}, f32[2,11,32]{2,1,0:T(8,128)S(1)}, u32[]{:S(2)}, u32[]{:S(2)}) %collective-permute-start.5) | collective-permute-done | bytes 2848 | tf_op jit(solution)/shard_map/ppermute | solution.py:25
  35.0 3.9 %collective-permute-done.6 = f32[4,11,32]{2,1,0:T(8,128)S(1)} collective-permute-done((f32[4,11,32]{2,1,0:T(8,128)S(1)}, f32[4,11,32]{2,1,0:T(8,128)S(1)}, u32[]{:S(2)}, u32[]{:S(2)}) %collective-permute-start.6) | collective-permute-done | bytes 5664 | tf_op jit(solution)/shard_map/ppermute | solution.py:25
  39.5 2.6 %collective-permute-done.7 = f32[8,11,32]{2,1,0:T(8,128)S(1)} collective-permute-done((f32[8,11,32]{2,1,0:T(8,128)S(1)}, f32[8,11,32]{2,1,0:T(8,128)S(1)}, u32[]{:S(2)}, u32[]{:S(2)}) %collective-permute-start.7) | collective-permute-done | bytes 11296 | tf_op jit(solution)/shard_map/ppermute | solution.py:25
  42.2 1.0 %collective-permute-start.8 = (f32[16,11,32]{2,1,0:T(8,128)S(1)}, f32[16,11,32]{2,1,0:T(8,128)S(1)}, u32[]{:S(2)}, u32[]{:S(2)}) collective-permute-start(f32[16,11,32]{2,1,0:T(8,128)S(1)} %get-tuple-element.111), channel_id=1, source_target_pairs={{0,4},{2,6},{4,0},{6,2},{1,5},{3,7},{5,1},{7,3},{8,12},{10,14},{12... | collective-permute-start | bytes 67592 | tf_op jit(solution)/shard_map/ppermute | solution.py:25
  43.2 4.3 %collective-permute-done.8 = f32[16,11,32]{2,1,0:T(8,128)S(1)} collective-permute-done((f32[16,11,32]{2,1,0:T(8,128)S(1)}, f32[16,11,32]{2,1,0:T(8,128)S(1)}, u32[]{:S(2)}, u32[]{:S(2)}) %collective-permute-start.8) | collective-permute-done | bytes 22560 | tf_op jit(solution)/shard_map/ppermute | solution.py:25
  49.9 9.2 %collective-permute-start.2 = (f32[24,20,128]{2,1,0:T(8,128)S(1)}, f32[24,20,128]{2,1,0:T(8,128)S(1)}, u32[]{:S(2)}, u32[]{:S(2)}) collective-permute-start(f32[24,20,128]{2,1,0:T(8,128)S(1)} %stack.49), channel_id=1, source_target_pairs={{0,1},{1,2},{2,3},{3,4},{4,5},{5,6},{6,7},{7,8},{8,9},{9,10},{10,1... | collective-permute-start | bytes 737288 | tf_op jit(solution)/shard_map/ppermute | solution.py:36
  59.5 1.9 %collective-permute-start.3 = (f32[24,18,128]{2,1,0:T(8,128)S(1)}, f32[24,18,128]{2,1,0:T(8,128)S(1)}, u32[]{:S(2)}, u32[]{:S(2)}) collective-permute-start(f32[24,18,128]{2,1,0:T(8,128)S(1)} %stack.50), channel_id=1, source_target_pairs={{1,0},{2,1},{3,2},{4,3},{5,4},{6,5},{7,6},{8,7},{9,8},{10,9},{11,1... | collective-permute-start | bytes 663560 | tf_op jit(solution)/shard_map/ppermute | solution.py:36
  63.6 1.1 %collective-permute-start.10 = (f32[64,11,32]{0,2,1:T(8,128)S(1)}, f32[64,11,32]{0,2,1:T(8,128)S(1)}, u32[]{:S(2)}, u32[]{:S(2)}) collective-permute-start(f32[64,11,32]{0,2,1:T(8,128)S(1)} %concatenate.53), channel_id=1, source_target_pairs={{0,16},{8,24},{16,0},{24,8},{1,17},{9,25},{17,1},{25,9},{2,18},{10... | collective-permute-start | bytes 270344 | tf_op jit(solution)/shard_map/ppermute | solution.py:25
  65.2 8.5 %collective-permute-done.10 = f32[64,11,32]{0,2,1:T(8,128)S(1)} collective-permute-done((f32[64,11,32]{0,2,1:T(8,128)S(1)}, f32[64,11,32]{0,2,1:T(8,128)S(1)}, u32[]{:S(2)}, u32[]{:S(2)}) %collective-permute-start.10) | collective-permute-done | bytes 90144 | tf_op jit(solution)/shard_map/ppermute | solution.py:25
  75.7 1.1 %fusion = f32[9,2,24,8,128]{4,3,2,1,0:T(8,128)S(1)} fusion(f32[8,32]{1,0:T(8,128)S(1)} %fusion.41, f32[9,2,24,32]{3,2,1,0:T(8,128)S(1)} %maximum_maximum_fusion, s32[32]{0:T(128)S(1)} %get-tuple-element.142), kind=kOutput, calls=%fused_computation.2 | convolution fusion | flops 169984000 | bytes 1825920 | tf_op jit(solution)/shard_map/dot_general | solution.py:338
  78.2 7.7 %shard_map.202 = (f32[2,24,8,128]{3,2,1,0:T(8,128)}, f32[4,2,24,8,128]{4,3,2,1,0:T(8,128)}, f32[4,2,24,8,128]{4,3,2,1,0:T(8,128)}) custom-call(s32[2]{0:T(128)} %add_convert_fusion.edge_ref, f32[24,8,128]{2,1,0:T(8,128)} %p_ref.1, f32[24,8,128]{2,1,0:T(8,128)} %s_ref.1, f32[24,8,128]{2,1,0:T(8,128)} %so_ref.1, f32[24,8,128]{2,1,0:T(8,128)} %pore_ref.1, ...), custom_call_target="tpu_custom_call" | custom-call | flops 29491200 | bytes 9043968 | tf_op jit(solution)/shard_map/pallas_call | solution.py:290
  85.9 1.6 %fusion.18 = f32[2,24,8,128]{3,2,1,0:T(8,128)} fusion(f32[2,24,8,128]{3,2,1,0:T(8,128)} %get-tuple-element.7, f32[9,2,24,8,128]{4,3,2,1,0:T(8,128)S(1)} %fusion), kind=kLoop, calls=%fused_computation.28 | loop fusion | flops 49152 | bytes 589824 | tf_op jit(solution)/shard_map/add | solution.py:339
  87.5 2.8 %slice_add_fusion = (f32[4,2,24,8,128]{4,3,2,1,0:T(8,128)}, f32[4,2,24,8,128]{4,3,2,1,0:T(8,128)}) fusion(f32[4,2,24,8,128]{4,3,2,1,0:T(8,128)} %get-tuple-element.9, f32[9,2,24,8,128]{4,3,2,1,0:T(8,128)S(1)} %fusion, f32[4,2,24,8,128]{4,3,2,1,0:T(8,128)} %get-tuple-element.8), kind=kLoop, calls=%fused_computation.18 | loop fusion | flops 393216 | bytes 4718592 | tf_op jit(solution)/shard_map/add | solution.py:341
  (137 shorter events, 21.5 us)
Async XLA Ops:
  0.6 2.1 %copy-start = (f32[2048]{0:T(1024)S(1)}, f32[2048]{0:T(1024)}, u32[]{:S(2)}) copy-start(f32[2048]{0:T(1024)} %param.38) | copy-start | bytes 24580
  0.6 7.5 %copy-start.2 = (f32[4,2,24,8,128]{4,3,2,1,0:T(8,128)S(1)}, f32[4,2,24,8,128]{4,3,2,1,0:T(8,128)}, u32[]{:S(2)}) copy-start(f32[4,2,24,8,128]{4,3,2,1,0:T(8,128)} %d_ref.1) | copy-start | bytes 2359300
  0.7 8.1 %copy-start.22 = (s32[32]{0:T(128)S(1)}, s32[32]{0:T(128)}, u32[]{:S(2)}) copy-start(s32[32]{0:T(128)} %param.35) | copy-start | bytes 388
  0.7 8.1 %copy-start.25 = (s32[32]{0:T(128)S(1)}, s32[32]{0:T(128)}, u32[]{:S(2)}) copy-start(s32[32]{0:T(128)} %param.36) | copy-start | bytes 388
  0.7 8.1 %copy-start.21 = (f32[32]{0:T(128)S(1)}, f32[32]{0:T(128)}, u32[]{:S(2)}) copy-start(f32[32]{0:T(128)} %param.37) | copy-start | bytes 388
  2.7 2.5 %copy-start.20 = (s32[1024]{0:T(1024)}, s32[1024]{0:T(1024)S(1)}, u32[]{:S(2)}) copy-start(s32[1024]{0:T(1024)S(1)} %pad_clamp_fusion) | copy-start | bytes 12292
  2.7 8.9 %copy-start.4 = (f32[24,8,128]{2,1,0:T(8,128)S(1)}, f32[24,8,128]{2,1,0:T(8,128)}, u32[]{:S(2)}) copy-start(f32[24,8,128]{2,1,0:T(8,128)} %p_ref.1) | copy-start | bytes 294916
  2.7 8.9 %copy-start.5 = (f32[24,8,128]{2,1,0:T(8,128)S(1)}, f32[24,8,128]{2,1,0:T(8,128)}, u32[]{:S(2)}) copy-start(f32[24,8,128]{2,1,0:T(8,128)} %s_ref.1) | copy-start | bytes 294916
  8.7 3.1 %copy-start.3 = (f32[4,2,24,8,128]{4,3,2,1,0:T(8,128)S(1)}, f32[4,2,24,8,128]{4,3,2,1,0:T(8,128)}, u32[]{:S(2)}) copy-start(f32[4,2,24,8,128]{4,3,2,1,0:T(8,128)} %w_ref.1) | copy-start | bytes 2359300
  10.9 18.8 %collective-permute-start.4 = (f32[1,11,32]{2,1,0:T(8,128)S(1)}, f32[1,11,32]{2,1,0:T(8,128)S(1)}, u32[]{:S(2)}, u32[]{:S(2)}) collective-permute-start(f32[1,11,32]{2,1,0:T(8,128)S(1)} %bitcast.123), channel_id=1, source_target_pairs={{0,1},{1,0},{2,3},{3,2},{4,5},{5,4},{6,7},{7,6},{8,9},{9,8},{10,11... | collective-permute-start | bytes 4232 | tf_op jit(solution)/shard_map/ppermute | solution.py:25
  20.5 56.2 %collective-permute-start.1 = (f32[24,8,18]{2,1,0:T(8,128)}, f32[24,8,18]{2,1,0:T(8,128)}, u32[]{:S(2)}, u32[]{:S(2)}) collective-permute-start(f32[24,8,18]{2,1,0:T(8,128)} %stack.48), channel_id=1, source_target_pairs={{32,0},{64,32},{96,64},{33,1},{65,33},{97,65},{34,2},{66,34},{98,6... | collective-permute-start | bytes 41480 | tf_op jit(solution)/shard_map/ppermute | solution.py:36
  27.9 33.6 %copy-start.1 = (f32[2048]{0:T(1024)S(1)}, f32[2048]{0:T(1024)}, u32[]{:S(2)}) copy-start(f32[2048]{0:T(1024)} %param.39) | copy-start | bytes 24580
  27.9 48.8 %collective-permute-start = (f32[24,8,20]{2,1,0:T(8,128)}, f32[24,8,20]{2,1,0:T(8,128)}, u32[]{:S(2)}, u32[]{:S(2)}) collective-permute-start(f32[24,8,20]{2,1,0:T(8,128)} %stack.47), channel_id=1, source_target_pairs={{0,32},{32,64},{64,96},{1,33},{33,65},{65,97},{2,34},{34,66},{66,9... | collective-permute-start | bytes 46088 | tf_op jit(solution)/shard_map/ppermute | solution.py:36
  29.7 4.9 %collective-permute-start.5 = (f32[2,11,32]{2,1,0:T(8,128)S(1)}, f32[2,11,32]{2,1,0:T(8,128)S(1)}, u32[]{:S(2)}, u32[]{:S(2)}) collective-permute-start(f32[2,11,32]{2,1,0:T(8,128)S(1)} %pad_maximum_fusion.3), channel_id=1, source_target_pairs={{0,32},{32,0},{64,96},{96,64},{1,33},{33,1},{65,97},{97,65},{2,34}... | collective-permute-start | bytes 8456 | tf_op jit(solution)/shard_map/ppermute | solution.py:25
  34.7 4.3 %collective-permute-start.6 = (f32[4,11,32]{2,1,0:T(8,128)S(1)}, f32[4,11,32]{2,1,0:T(8,128)S(1)}, u32[]{:S(2)}, u32[]{:S(2)}) collective-permute-start(f32[4,11,32]{2,1,0:T(8,128)S(1)} %pad_maximum_fusion.1), channel_id=1, source_target_pairs={{0,64},{32,96},{64,0},{96,32},{1,65},{33,97},{65,1},{97,33},{2,66}... | collective-permute-start | bytes 16904 | tf_op jit(solution)/shard_map/ppermute | solution.py:25
  39.0 3.2 %collective-permute-start.7 = (f32[8,11,32]{2,1,0:T(8,128)S(1)}, f32[8,11,32]{2,1,0:T(8,128)S(1)}, u32[]{:S(2)}, u32[]{:S(2)}) collective-permute-start(f32[8,11,32]{2,1,0:T(8,128)S(1)} %pad_maximum_fusion), channel_id=1, source_target_pairs={{0,2},{2,0},{4,6},{6,4},{1,3},{3,1},{5,7},{7,5},{8,10},{10,8},{12,... | collective-permute-start | bytes 33800 | tf_op jit(solution)/shard_map/ppermute | solution.py:25
  42.2 5.4 %collective-permute-start.8 = (f32[16,11,32]{2,1,0:T(8,128)S(1)}, f32[16,11,32]{2,1,0:T(8,128)S(1)}, u32[]{:S(2)}, u32[]{:S(2)}) collective-permute-start(f32[16,11,32]{2,1,0:T(8,128)S(1)} %get-tuple-element.111), channel_id=1, source_target_pairs={{0,4},{2,6},{4,0},{6,2},{1,5},{3,7},{5,1},{7,3},{8,12},{10,14},{12... | collective-permute-start | bytes 67592 | tf_op jit(solution)/shard_map/ppermute | solution.py:25
  47.6 15.5 %collective-permute-start.9 = (f32[32,11,32]{2,1,0:T(8,128)S(1)}, f32[32,11,32]{2,1,0:T(8,128)S(1)}, u32[]{:S(2)}, u32[]{:S(2)}) collective-permute-start(f32[32,11,32]{2,1,0:T(8,128)S(1)} %constant_dynamic-update-slice_fusion.5), channel_id=1, source_target_pairs={{0,8},{8,0},{16,24},{24,16},{1,9},{9,1},{17,25},{25,17},{2,10},{10... | collective-permute-start | bytes 135176 | tf_op jit(solution)/shard_map/ppermute | solution.py:25
  49.9 26.9 %collective-permute-start.2 = (f32[24,20,128]{2,1,0:T(8,128)S(1)}, f32[24,20,128]{2,1,0:T(8,128)S(1)}, u32[]{:S(2)}, u32[]{:S(2)}) collective-permute-start(f32[24,20,128]{2,1,0:T(8,128)S(1)} %stack.49), channel_id=1, source_target_pairs={{0,1},{1,2},{2,3},{3,4},{4,5},{5,6},{6,7},{7,8},{8,9},{9,10},{10,1... | collective-permute-start | bytes 737288 | tf_op jit(solution)/shard_map/ppermute | solution.py:36
  59.5 17.3 %collective-permute-start.3 = (f32[24,18,128]{2,1,0:T(8,128)S(1)}, f32[24,18,128]{2,1,0:T(8,128)S(1)}, u32[]{:S(2)}, u32[]{:S(2)}) collective-permute-start(f32[24,18,128]{2,1,0:T(8,128)S(1)} %stack.50), channel_id=1, source_target_pairs={{1,0},{2,1},{3,2},{4,3},{5,4},{6,5},{7,6},{8,7},{9,8},{10,9},{11,1... | collective-permute-start | bytes 663560 | tf_op jit(solution)/shard_map/ppermute | solution.py:36
  63.6 10.1 %collective-permute-start.10 = (f32[64,11,32]{0,2,1:T(8,128)S(1)}, f32[64,11,32]{0,2,1:T(8,128)S(1)}, u32[]{:S(2)}, u32[]{:S(2)}) collective-permute-start(f32[64,11,32]{0,2,1:T(8,128)S(1)} %concatenate.53), channel_id=1, source_target_pairs={{0,16},{8,24},{16,0},{24,8},{1,17},{9,25},{17,1},{25,9},{2,18},{10... | collective-permute-start | bytes 270344 | tf_op jit(solution)/shard_map/ppermute | solution.py:25
  65.2 9.7 %copy-start.23 = (f32[32]{0:T(128)S(1)}, f32[32]{0:T(128)}, u32[]{:S(2)}) copy-start(f32[32]{0:T(128)} %get-tuple-element.139) | copy-start | bytes 388
  65.2 10.2 %copy-start.24 = (s32[32]{0:T(128)S(1)}, s32[32]{0:T(128)}, u32[]{:S(2)}) copy-start(s32[32]{0:T(128)} %param.33) | copy-start | bytes 388
  65.2 10.2 %copy-start.12 = (f32[2,24,32]{2,1,0:T(8,128)S(1)}, f32[2,24,32]{2,1,0:T(8,128)}, u32[]{:S(2)}) copy-start(f32[2,24,32]{2,1,0:T(8,128)} %get-tuple-element.11) | copy-start | bytes 18436
  (13 other events, 17.7 us)

commit v3 on v2

--- a/solution.py
+++ b/solution.py
@@ -78,6 +78,49 @@
     return as_a, as_b
 
 
+def pack_kernel(p_ref, s_ref, d_ref, w_ref, tx_ref, ux_ref, ty_ref, uy_ref, xl_ref, xr_ref, yd_ref, yu_ref):
+    ndir = d_ref.shape[0]
+    layers, rows, cols = p_ref.shape
+    lane = lax.broadcasted_iota(jnp.int32, (rows, cols), 1)
+    sub = lax.broadcasted_iota(jnp.int32, (rows, cols), 0)
+    nf = 2 + 4 * ndir
+
+    def rolled(x, shift, axis):
+        return x if shift == 0 else pltpu.roll(x, shift, axis)
+
+    def rows_into(ref, k, tiles, source_row):
+        count = len(tiles)
+        for start in range(0, count, rows):
+            acc = jnp.zeros((rows, cols), jnp.float32)
+            for f in range(start, min(start + rows, count)):
+                r = f - start
+                acc = jnp.where(sub == r, rolled(tiles[f], (r - source_row) % rows, 0), acc)
+            n = min(rows, count - start)
+            ref[k, pl.ds(start, n), :] = acc[:n]
+
+    def body(k, carry):
+        cells = [p_ref[k], s_ref[k]]
+        for half in range(2):
+            cells += [d_ref[d, half, k] for d in range(ndir)]
+        for half in range(2):
+            cells += [w_ref[d, half, k] for d in range(ndir)]
+        low_x = cells + [tx_ref[k], ux_ref[k].astype(jnp.float32)]
+        low_y = cells + [ty_ref[k], uy_ref[k].astype(jnp.float32)]
+        xl = jnp.zeros((rows, cols), jnp.float32)
+        for f, t in enumerate(low_x):
+            xl = jnp.where(lane == f, rolled(t, (f - (cols - 1)) % cols, 1), xl)
+        xr = jnp.zeros((rows, cols), jnp.float32)
+        for f, t in enumerate(cells):
+            xr = jnp.where(lane == f, rolled(t, f % cols, 1), xr)
+        xl_ref[k] = xl[:, : nf + 2]
+        xr_ref[k] = xr[:, :nf]
+        rows_into(yd_ref, k, low_y, rows - 1)
+        rows_into(yu_ref, k, cells, 0)
+        return carry
+
+    lax.fori_loop(0, layers, body, 0)
+
+
 def stencil_kernel(
     edge_ref,
     p_ref,
@@ -96,6 +139,7 @@
     hxr_ref,
     hyd_ref,
     hyu_ref,
+    spread_ref,
     r_out,
     jv_out,
     jt_out,
@@ -136,20 +180,17 @@
     def row(ref, k, f):
         return jnp.broadcast_to(ref[k, pl.ds(f, 1), :], (rows, cols))
 
-    def store(k, vals, add_prev):
+    def store(k, vals):
         for i in range(nf):
             if i < 2:
-                ref, idx = r_out, (i, k)
+                ref, idx, extra = r_out, (i, k), (0, i, k)
             elif i < 2 + 2 * ndir:
                 j = i - 2
-                ref, idx = jv_out, (j % ndir, j // ndir, k)
+                ref, idx, extra = jv_out, (j % ndir, j // ndir, k), (1 + j % ndir, j // ndir, k)
             else:
                 j = i - 2 - 2 * ndir
-                ref, idx = jt_out, (j % ndir, j // ndir, k)
-            if add_prev:
-                ref[idx] = ref[idx] + vals[i]
-            else:
-                ref[idx] = vals[i]
+                ref, idx, extra = jt_out, (j % ndir, j // ndir, k), (1 + ndir + j % ndir, j // ndir, k)
+            ref[idx] = vals[i] + spread_ref[extra]
 
     def body(k, carry):
         here = cells(k)
@@ -193,7 +234,7 @@
             jt_s = 2 + 3 * ndir + d
             acc[jt_s] = acc[jt_s] + pore * (here[2 + 2 * ndir + d] - here[2 + 3 * ndir + d])
         acc = [a + c for a, c in zip(acc, carry)]
-        store(k, acc, False)
+        store(k, acc)
         return tuple(zb)
 
     zero = jnp.zeros((rows, cols), jnp.float32)
@@ -266,35 +307,53 @@
     packed = jnp.concatenate([row_sums, perf_well.astype(jnp.float32)[None]], axis=0)
     everyone = gather_everywhere(packed)
 
-    cell_fields = [pressure, saturation] + [directions[d, h] for h in range(2) for d in range(ndir)]
-    cell_fields += [adjoint_weights[d, h] for h in range(2) for d in range(ndir)]
-    x_low = jnp.stack(
-        [f[:, :, cols - 1] for f in cell_fields]
-        + [trans_x[:, :, cols - 1], upwind_x[:, :, cols - 1].astype(jnp.float32)],
-        axis=-1,
-    )
-    x_high = jnp.stack([f[:, :, 0] for f in cell_fields], axis=-1)
-    y_low = jnp.stack(
-        [f[:, rows - 1, :] for f in cell_fields]
-        + [trans_y[:, rows - 1, :], upwind_y[:, rows - 1, :].astype(jnp.float32)],
-        axis=1,
-    )
-    y_high = jnp.stack([f[:, 0, :] for f in cell_fields], axis=1)
+    nf = 2 + 4 * ndir
+    vmem = pl.BlockSpec(memory_space=pltpu.VMEM)
+    x_low, x_high, y_low, y_high = pl.pallas_call(
+        pack_kernel,
+        out_shape=[
+            jax.ShapeDtypeStruct((layers, rows, nf + 2), jnp.float32),
+            jax.ShapeDtypeStruct((layers, rows, nf), jnp.float32),
+            jax.ShapeDtypeStruct((layers, nf + 2, cols), jnp.float32),
+            jax.ShapeDtypeStruct((layers, nf, cols), jnp.float32),
+        ],
+        in_specs=[vmem] * 8,
+        out_specs=[vmem] * 4,
+        cost_estimate=pl.CostEstimate(
+            flops=layers * rows * cols * 160,
+            transcendentals=0,
+            bytes_accessed=(6 + 4 * ndir) * layers * rows * cols * 4,
+        ),
+    )(pressure, saturation, directions, adjoint_weights, trans_x, upwind_x, trans_y, upwind_y)
     hxl = shift_along(x_low, "gx", True)
     hxr = shift_along(x_high, "gx", False)
     hyd = shift_along(y_low, GY_WA, True)
     hyu = shift_along(y_high, GY_WA, False)
 
-    nf = 2 + 4 * ndir
-    vmem = pl.BlockSpec(memory_space=pltpu.VMEM)
-    flux_r, flux_jv, flux_jt = pl.pallas_call(
+    all_sums = jnp.moveaxis(everyone[:, :-1], 1, 0).reshape(row_sums.shape[0], -1)
+    all_wells = everyone[:, -1].reshape(-1)
+    same_well = (perf_well.astype(jnp.float32)[:, None] == all_wells[None, :]).astype(jnp.float32)
+    row_totals = jnp.dot(all_sums, same_well.T, precision=lax.Precision.HIGHEST)
+    row_target = jnp.take(target, perf_well)
+    row_factors = well_factors(row_totals, row_target)
+    wells_res = rates - weight * mob * row_factors[0]
+    wells_fwd = rate_tangent - (weight * mob)[None] * row_factors[1 : 1 + ndir][:, None, None, :]
+    out_f = row_factors[1 + ndir :][:, None, :]
+    wells_adj = jnp.stack(
+        [grad_p - weight * mob_total * out_f, grad_s - weight * slope_total * drive * out_f], axis=1
+    )
+    combined = jnp.concatenate([wells_res[None], wells_fwd, wells_adj], axis=0)
+    by_row = combined[..., None, :] * row_hit
+    spread = jnp.dot(by_row, lane_hit.T, precision=lax.Precision.HIGHEST)
+
+    reduced_residual, forward_products, adjoint_products = pl.pallas_call(
         stencil_kernel,
         out_shape=[
             jax.ShapeDtypeStruct((2,) + spatial, jnp.float32),
             jax.ShapeDtypeStruct((ndir, 2) + spatial, jnp.float32),
             jax.ShapeDtypeStruct((ndir, 2) + spatial, jnp.float32),
         ],
-        in_specs=[pl.BlockSpec(memory_space=pltpu.SMEM)] + [vmem] * 16,
+        in_specs=[pl.BlockSpec(memory_space=pltpu.SMEM)] + [vmem] * 17,
         out_specs=[vmem] * 3,
         cost_estimate=pl.CostEstimate(
             flops=layers * rows * cols * 1200,
@@ -319,26 +378,8 @@
         hxr,
         hyd,
         hyu,
-    )
-
-    all_sums = jnp.moveaxis(everyone[:, :-1], 1, 0).reshape(row_sums.shape[0], -1)
-    all_wells = everyone[:, -1].reshape(-1)
-    same_well = (perf_well.astype(jnp.float32)[:, None] == all_wells[None, :]).astype(jnp.float32)
-    row_totals = jnp.dot(all_sums, same_well.T, precision=lax.Precision.HIGHEST)
-    row_target = jnp.take(target, perf_well)
-    row_factors = well_factors(row_totals, row_target)
-    wells_res = rates - weight * mob * row_factors[0]
-    wells_fwd = rate_tangent - (weight * mob)[None] * row_factors[1 : 1 + ndir][:, None, None, :]
-    out_f = row_factors[1 + ndir :][:, None, :]
-    wells_adj = jnp.stack(
-        [grad_p - weight * mob_total * out_f, grad_s - weight * slope_total * drive * out_f], axis=1
-    )
-    combined = jnp.concatenate([wells_res[None], wells_fwd, wells_adj], axis=0)
-    by_row = combined[..., None, :] * row_hit
-    spread = jnp.dot(by_row, lane_hit.T, precision=lax.Precision.HIGHEST)
-    reduced_residual = flux_r + spread[0]
-    forward_products = flux_jv + spread[1 : 1 + ndir]
-    adjoint_products = flux_jt + spread[1 + ndir :]
+        spread,
+    )
     return (reduced_residual, forward_products, adjoint_products)
 
 

time: 90.9 us -> 74.9 us (0.82)
  the two profiles are of different devices: /device:TPU:63 before, /device:TPU:59 now
where the time goes in v3:
time: 74.9 us; the launch traced here: 74.5 us
  starting transfers between devices  22.8 us (30%)
  waiting for transfers between devices  21.5 us (29%)
  Pallas kernels  13.3 us (18%)
  matrix products  7.23 us (10%)
  local copies, waits for them, and re-layouts  5.59 us (7%)
  other arithmetic  3.02 us (4%)
  between operations  1.01 us (1%)
    ppermute x7, waiting for transfers between devices, gather_everywhere(): other = lax.ppermute(held, axis, [(i, i ^ step) for i in range(size)])  21.5 us
    ppermute x4, starting transfers between devices, shift_along(): return lax.ppermute(block, axis, pairs)  17.4 us
    pallas_call x1, Pallas kernels, body(): pl.pallas_call(stencil_kernel, out_shape=[jax.ShapeDtypeStruct((2,) + spa...  8.36 us
    ppermute x7, starting transfers between devices, gather_everywhere(): other = lax.ppermute(held, axis, [(i, i ^ step) for i in range(size)])  5.46 us
    pallas_call x1, Pallas kernels, body(): pl.pallas_call(pack_kernel, out_shape=[jax.ShapeDtypeStruct((layers, rows...  4.93 us
    dot_general x4, matrix products, at_perfs(): by_lane = jnp.dot(field, lane_hit, precision=lax.Precision.HIGHEST)  4.57 us
    dot_general x1, matrix products, body(): spread = jnp.dot(by_row, lane_hit.T, precision=lax.Precision.HIGHEST)  2.25 us
    unnamed x27, local copies, waits for them, and re-layouts  1.56 us
  transfers between devices with their start and end apart: 11, of which 6 were waited for; matrix products, arithmetic and copies ran while one was open for 9% of the time, Pallas kernels for 7%

profile of v3, /device:TPU:59, one launch (start us, length us, event | category | flops | bytes accessed | tf_op | source)
XLA Modules:
  0.0 74.5 jit_solution(16875531465985845865)
XLA Ops:
  0.7 0.7 and_select_fusion.1
  1.4 0.7 fusion.51
  3.5 1.1 %fusion.9 = f32[24,32]{1,0:T(8,128)S(1)} fusion(f32[24,8,128]{2,1,0:T(8,128)} %p_ref.3, f32[8,32]{1,0:T(8,128)S(1)} %fusion.40, s32[32]{0:T(128)S(1)} %get-tuple-element.54), kind=kOutput, calls=%fused_computation.15 | convolution fusion | flops 9452800 | bytes 102528 | tf_op jit(solution)/shard_map/dot_general | solution.py:276
  4.7 1.1 %fusion.8 = f32[24,32]{1,0:T(8,128)S(1)} fusion(f32[24,8,128]{2,1,0:T(8,128)} %s_ref.3, f32[8,32]{1,0:T(8,128)S(1)} %fusion.40, s32[32]{0:T(128)S(1)} %get-tuple-element.54), kind=kOutput, calls=%fused_computation.14 | convolution fusion | flops 9452800 | bytes 102528 | tf_op jit(solution)/shard_map/dot_general | solution.py:276
  5.8 1.7 %fusion.5 = f32[4,2,24,32]{3,2,1,0:T(8,128)S(1)} fusion(f32[4,2,24,8,128]{4,3,2,1,0:T(8,128)} %w_ref.3, f32[8,32]{1,0:T(8,128)S(1)} %fusion.40, s32[32]{0:T(128)S(1)} %get-tuple-element.54), kind=kOutput, calls=%fused_computation.9 | convolution fusion | flops 75593728 | bytes 812160 | tf_op jit(solution)/shard_map/dot_general | solution.py:276
  8.5 0.8 %collective-permute-start.4 = (f32[1,11,32]{2,1,0:T(8,128)S(1)}, f32[1,11,32]{2,1,0:T(8,128)S(1)}, u32[]{:S(2)}, u32[]{:S(2)}) collective-permute-start(f32[1,11,32]{2,1,0:T(8,128)S(1)} %bitcast.87), channel_id=1, source_target_pairs={{0,1},{1,0},{2,3},{3,2},{4,5},{5,4},{6,7},{7,6},{8,9},{9,8},{10,11... | collective-permute-start | bytes 4232 | tf_op jit(solution)/shard_map/ppermute | solution.py:25
  9.3 0.8 %collective-permute-done.4 = f32[1,11,32]{2,1,0:T(8,128)S(1)} collective-permute-done((f32[1,11,32]{2,1,0:T(8,128)S(1)}, f32[1,11,32]{2,1,0:T(8,128)S(1)}, u32[]{:S(2)}, u32[]{:S(2)}) %collective-permute-start.4) | collective-permute-done | bytes 1440 | tf_op jit(solution)/shard_map/ppermute | solution.py:25
  10.3 2.3 %collective-permute-done.5 = f32[2,11,32]{2,1,0:T(8,128)S(1)} collective-permute-done((f32[2,11,32]{2,1,0:T(8,128)S(1)}, f32[2,11,32]{2,1,0:T(8,128)S(1)}, u32[]{:S(2)}, u32[]{:S(2)}) %collective-permute-start.5) | collective-permute-done | bytes 2848 | tf_op jit(solution)/shard_map/ppermute | solution.py:25
  12.7 1.8 %collective-permute-start.6 = (f32[4,11,32]{2,1,0:T(8,128)S(1)}, f32[4,11,32]{2,1,0:T(8,128)S(1)}, u32[]{:S(2)}, u32[]{:S(2)}) collective-permute-start(f32[4,11,32]{2,1,0:T(8,128)S(1)} %pad_maximum_fusion.1), channel_id=1, source_target_pairs={{0,64},{32,96},{64,0},{96,32},{1,65},{33,97},{65,1},{97,33},{2,66}... | collective-permute-start | bytes 16904 | tf_op jit(solution)/shard_map/ppermute | solution.py:25
  14.5 2.4 %collective-permute-done.6 = f32[4,11,32]{2,1,0:T(8,128)S(1)} collective-permute-done((f32[4,11,32]{2,1,0:T(8,128)S(1)}, f32[4,11,32]{2,1,0:T(8,128)S(1)}, u32[]{:S(2)}, u32[]{:S(2)}) %collective-permute-start.6) | collective-permute-done | bytes 5664 | tf_op jit(solution)/shard_map/ppermute | solution.py:25
  17.5 2.6 %collective-permute-done.7 = f32[8,11,32]{2,1,0:T(8,128)S(1)} collective-permute-done((f32[8,11,32]{2,1,0:T(8,128)S(1)}, f32[8,11,32]{2,1,0:T(8,128)S(1)}, u32[]{:S(2)}, u32[]{:S(2)}) %collective-permute-start.7) | collective-permute-done | bytes 11296 | tf_op jit(solution)/shard_map/ppermute | solution.py:25
  20.2 1.0 %collective-permute-start.8 = (f32[16,11,32]{2,1,0:T(8,128)S(1)}, f32[16,11,32]{2,1,0:T(8,128)S(1)}, u32[]{:S(2)}, u32[]{:S(2)}) collective-permute-start(f32[16,11,32]{2,1,0:T(8,128)S(1)} %get-tuple-element.23), channel_id=1, source_target_pairs={{0,4},{2,6},{4,0},{6,2},{1,5},{3,7},{5,1},{7,3},{8,12},{10,14},{12... | collective-permute-start | bytes 67592 | tf_op jit(solution)/shard_map/ppermute | solution.py:25
  21.2 4.4 %collective-permute-done.8 = f32[16,11,32]{2,1,0:T(8,128)S(1)} collective-permute-done((f32[16,11,32]{2,1,0:T(8,128)S(1)}, f32[16,11,32]{2,1,0:T(8,128)S(1)}, u32[]{:S(2)}, u32[]{:S(2)}) %collective-permute-start.8) | collective-permute-done | bytes 22560 | tf_op jit(solution)/shard_map/ppermute | solution.py:25
  25.7 4.9 %shard_map.202 = (f32[24,8,20]{2,1,0:T(8,128)}, f32[24,8,18]{2,1,0:T(8,128)}, f32[24,20,128]{2,1,0:T(8,128)}, f32[24,18,128]{2,1,0:T(8,128)}) custom-call(f32[24,8,128]{2,1,0:T(8,128)} %p_ref.3, f32[24,8,128]{2,1,0:T(8,128)} %s_ref.3, f32[4,2,24,8,128]{4,3,2,1,0:T(8,128)} %d_ref.3, f32[4,2,24,8,128]{4,3,2,1,0:T(8,128)} %w_ref.3, f32[24,8,128]{2,1,0:T(8,128)} %tx_ref.3, ...), custom_call_target="tpu_custom_call" | custom-call | flops 3932160 | bytes 2162688 | tf_op jit(solution)/shard_map/pallas_call | solution.py:312
  30.6 3.1 %collective-permute-start = (f32[24,8,20]{2,1,0:T(8,128)}, f32[24,8,20]{2,1,0:T(8,128)S(1)}, u32[]{:S(2)}, u32[]{:S(2)}) collective-permute-start(f32[24,8,20]{2,1,0:T(8,128)} %get-tuple-element.8), channel_id=1, source_target_pairs={{0,32},{32,64},{64,96},{1,33},{33,65},{65,97},{2,34},{34,66},{66,9... | collective-permute-start | bytes 46088 | tf_op jit(solution)/shard_map/ppermute | solution.py:36
  33.7 2.2 %collective-permute-start.1 = (f32[24,8,18]{2,1,0:T(8,128)}, f32[24,8,18]{2,1,0:T(8,128)S(1)}, u32[]{:S(2)}, u32[]{:S(2)}) collective-permute-start(f32[24,8,18]{2,1,0:T(8,128)} %get-tuple-element.9), channel_id=1, source_target_pairs={{32,0},{64,32},{96,64},{33,1},{65,33},{97,65},{34,2},{66,34},{98,6... | collective-permute-start | bytes 41480 | tf_op jit(solution)/shard_map/ppermute | solution.py:36
  35.9 10.2 %collective-permute-start.2 = (f32[24,20,128]{2,1,0:T(8,128)}, f32[24,20,128]{2,1,0:T(8,128)S(1)}, u32[]{:S(2)}, u32[]{:S(2)}) collective-permute-start(f32[24,20,128]{2,1,0:T(8,128)} %get-tuple-element.10), channel_id=1, source_target_pairs={{0,1},{1,2},{2,3},{3,4},{4,5},{5,6},{6,7},{7,8},{8,9},{9,10},{10,1... | collective-permute-start | bytes 737288 | tf_op jit(solution)/shard_map/ppermute | solution.py:36
  46.1 1.9 %collective-permute-start.3 = (f32[24,18,128]{2,1,0:T(8,128)}, f32[24,18,128]{2,1,0:T(8,128)S(1)}, u32[]{:S(2)}, u32[]{:S(2)}) collective-permute-start(f32[24,18,128]{2,1,0:T(8,128)} %get-tuple-element.11), channel_id=1, source_target_pairs={{1,0},{2,1},{3,2},{4,3},{5,4},{6,5},{7,6},{8,7},{9,8},{10,9},{11,1... | collective-permute-start | bytes 663560 | tf_op jit(solution)/shard_map/ppermute | solution.py:36
  48.2 0.7 gather_fusion.1
  50.1 0.9 %collective-permute-start.10 = (f32[64,11,32]{0,2,1:T(8,128)S(1)}, f32[64,11,32]{0,2,1:T(8,128)S(1)}, u32[]{:S(2)}, u32[]{:S(2)}) collective-permute-start(f32[64,11,32]{0,2,1:T(8,128)S(1)} %concatenate.53), channel_id=1, source_target_pairs={{0,16},{8,24},{16,0},{24,8},{1,17},{9,25},{17,1},{25,9},{2,18},{10... | collective-permute-start | bytes 270344 | tf_op jit(solution)/shard_map/ppermute | solution.py:25
  51.7 8.9 %collective-permute-done.10 = f32[64,11,32]{0,2,1:T(8,128)S(1)} collective-permute-done((f32[64,11,32]{0,2,1:T(8,128)S(1)}, f32[64,11,32]{0,2,1:T(8,128)S(1)}, u32[]{:S(2)}, u32[]{:S(2)}) %collective-permute-start.10) | collective-permute-done | bytes 90144 | tf_op jit(solution)/shard_map/ppermute | solution.py:25
  62.3 2.3 %fusion.spread_ref = f32[9,2,24,8,128]{4,3,2,1,0:T(8,128)} fusion(f32[8,32]{1,0:T(8,128)S(1)} %fusion.40, f32[9,2,24,32]{3,2,1,0:T(8,128)S(1)} %maximum_maximum_fusion, s32[32]{0:T(128)S(1)} %get-tuple-element.54), kind=kOutput, calls=%fused_computation.2 | convolution fusion | flops 169984000 | bytes 1825920 | tf_op jit(solution)/shard_map/dot_general | solution.py:347
  65.4 0.7 copy-done.3
  66.1 8.4 %shard_map.203 = (f32[2,24,8,128]{3,2,1,0:T(8,128)}, f32[4,2,24,8,128]{4,3,2,1,0:T(8,128)}, f32[4,2,24,8,128]{4,3,2,1,0:T(8,128)}) custom-call(s32[2]{0:T(128)} %add_convert_fusion.edge_ref, f32[24,8,128]{2,1,0:T(8,128)} %p_ref.3, f32[24,8,128]{2,1,0:T(8,128)} %s_ref.3, f32[24,8,128]{2,1,0:T(8,128)} %so_ref.1, f32[24,8,128]{2,1,0:T(8,128)} %pore_ref.1, ...), custom_call_target="tpu_custom_call" | custom-call | flops 29491200 | bytes 9043968 | tf_op jit(solution)/shard_map/pallas_call | solution.py:349
  (78 shorter events, 7.6 us)
Async XLA Ops:
  0.6 1.5 %copy-start = (f32[2048]{0:T(1024)S(1)}, f32[2048]{0:T(1024)}, u32[]{:S(2)}) copy-start(f32[2048]{0:T(1024)} %param.38) | copy-start | bytes 24580
  0.6 6.9 %copy-start.2 = (f32[4,2,24,8,128]{4,3,2,1,0:T(8,128)S(1)}, f32[4,2,24,8,128]{4,3,2,1,0:T(8,128)}, u32[]{:S(2)}) copy-start(f32[4,2,24,8,128]{4,3,2,1,0:T(8,128)} %d_ref.3) | copy-start | bytes 2359300
  0.7 7.5 %copy-start.8 = (s32[32]{0:T(128)S(1)}, s32[32]{0:T(128)}, u32[]{:S(2)}) copy-start(s32[32]{0:T(128)} %param.35) | copy-start | bytes 388
  0.7 7.5 %copy-start.10 = (s32[32]{0:T(128)S(1)}, s32[32]{0:T(128)}, u32[]{:S(2)}) copy-start(s32[32]{0:T(128)} %param.36) | copy-start | bytes 388
  0.7 7.5 %copy-start.7 = (f32[32]{0:T(128)S(1)}, f32[32]{0:T(128)}, u32[]{:S(2)}) copy-start(f32[32]{0:T(128)} %param.37) | copy-start | bytes 388
  8.3 39.9 %copy-start.1 = (f32[2048]{0:T(1024)S(1)}, f32[2048]{0:T(1024)}, u32[]{:S(2)}) copy-start(f32[2048]{0:T(1024)} %param.39) | copy-start | bytes 24580
  8.5 1.6 %collective-permute-start.4 = (f32[1,11,32]{2,1,0:T(8,128)S(1)}, f32[1,11,32]{2,1,0:T(8,128)S(1)}, u32[]{:S(2)}, u32[]{:S(2)}) collective-permute-start(f32[1,11,32]{2,1,0:T(8,128)S(1)} %bitcast.87), channel_id=1, source_target_pairs={{0,1},{1,0},{2,3},{3,2},{4,5},{5,4},{6,7},{7,6},{8,9},{9,8},{10,11... | collective-permute-start | bytes 4232 | tf_op jit(solution)/shard_map/ppermute | solution.py:25
  10.1 2.6 %collective-permute-start.5 = (f32[2,11,32]{2,1,0:T(8,128)S(1)}, f32[2,11,32]{2,1,0:T(8,128)S(1)}, u32[]{:S(2)}, u32[]{:S(2)}) collective-permute-start(f32[2,11,32]{2,1,0:T(8,128)S(1)} %pad_maximum_fusion.3), channel_id=1, source_target_pairs={{0,32},{32,0},{64,96},{96,64},{1,33},{33,1},{65,97},{97,65},{2,34}... | collective-permute-start | bytes 8456 | tf_op jit(solution)/shard_map/ppermute | solution.py:25
  12.7 4.3 %collective-permute-start.6 = (f32[4,11,32]{2,1,0:T(8,128)S(1)}, f32[4,11,32]{2,1,0:T(8,128)S(1)}, u32[]{:S(2)}, u32[]{:S(2)}) collective-permute-start(f32[4,11,32]{2,1,0:T(8,128)S(1)} %pad_maximum_fusion.1), channel_id=1, source_target_pairs={{0,64},{32,96},{64,0},{96,32},{1,65},{33,97},{65,1},{97,33},{2,66}... | collective-permute-start | bytes 16904 | tf_op jit(solution)/shard_map/ppermute | solution.py:25
  17.0 3.2 %collective-permute-start.7 = (f32[8,11,32]{2,1,0:T(8,128)S(1)}, f32[8,11,32]{2,1,0:T(8,128)S(1)}, u32[]{:S(2)}, u32[]{:S(2)}) collective-permute-start(f32[8,11,32]{2,1,0:T(8,128)S(1)} %pad_maximum_fusion), channel_id=1, source_target_pairs={{0,2},{2,0},{4,6},{6,4},{1,3},{3,1},{5,7},{7,5},{8,10},{10,8},{12,... | collective-permute-start | bytes 33800 | tf_op jit(solution)/shard_map/ppermute | solution.py:25
  20.2 5.4 %collective-permute-start.8 = (f32[16,11,32]{2,1,0:T(8,128)S(1)}, f32[16,11,32]{2,1,0:T(8,128)S(1)}, u32[]{:S(2)}, u32[]{:S(2)}) collective-permute-start(f32[16,11,32]{2,1,0:T(8,128)S(1)} %get-tuple-element.23), channel_id=1, source_target_pairs={{0,4},{2,6},{4,0},{6,2},{1,5},{3,7},{5,1},{7,3},{8,12},{10,14},{12... | collective-permute-start | bytes 67592 | tf_op jit(solution)/shard_map/ppermute | solution.py:25
  25.6 24.0 %collective-permute-start.9 = (f32[32,11,32]{2,1,0:T(8,128)S(1)}, f32[32,11,32]{2,1,0:T(8,128)S(1)}, u32[]{:S(2)}, u32[]{:S(2)}) collective-permute-start(f32[32,11,32]{2,1,0:T(8,128)S(1)} %constant_dynamic-update-slice_fusion.5), channel_id=1, source_target_pairs={{0,8},{8,0},{16,24},{24,16},{1,9},{9,1},{17,25},{25,17},{2,10},{10... | collective-permute-start | bytes 135176 | tf_op jit(solution)/shard_map/ppermute | solution.py:25
  30.6 34.0 %collective-permute-start = (f32[24,8,20]{2,1,0:T(8,128)}, f32[24,8,20]{2,1,0:T(8,128)S(1)}, u32[]{:S(2)}, u32[]{:S(2)}) collective-permute-start(f32[24,8,20]{2,1,0:T(8,128)} %get-tuple-element.8), channel_id=1, source_target_pairs={{0,32},{32,64},{64,96},{1,33},{33,65},{65,97},{2,34},{34,66},{66,9... | collective-permute-start | bytes 46088 | tf_op jit(solution)/shard_map/ppermute | solution.py:36
  33.7 30.9 %collective-permute-start.1 = (f32[24,8,18]{2,1,0:T(8,128)}, f32[24,8,18]{2,1,0:T(8,128)S(1)}, u32[]{:S(2)}, u32[]{:S(2)}) collective-permute-start(f32[24,8,18]{2,1,0:T(8,128)} %get-tuple-element.9), channel_id=1, source_target_pairs={{32,0},{64,32},{96,64},{33,1},{65,33},{97,65},{34,2},{66,34},{98,6... | collective-permute-start | bytes 41480 | tf_op jit(solution)/shard_map/ppermute | solution.py:36
  35.9 28.7 %collective-permute-start.2 = (f32[24,20,128]{2,1,0:T(8,128)}, f32[24,20,128]{2,1,0:T(8,128)S(1)}, u32[]{:S(2)}, u32[]{:S(2)}) collective-permute-start(f32[24,20,128]{2,1,0:T(8,128)} %get-tuple-element.10), channel_id=1, source_target_pairs={{0,1},{1,2},{2,3},{3,4},{4,5},{5,6},{6,7},{7,8},{8,9},{9,10},{10,1... | collective-permute-start | bytes 737288 | tf_op jit(solution)/shard_map/ppermute | solution.py:36
  46.1 18.5 %collective-permute-start.3 = (f32[24,18,128]{2,1,0:T(8,128)}, f32[24,18,128]{2,1,0:T(8,128)S(1)}, u32[]{:S(2)}, u32[]{:S(2)}) collective-permute-start(f32[24,18,128]{2,1,0:T(8,128)} %get-tuple-element.11), channel_id=1, source_target_pairs={{1,0},{2,1},{3,2},{4,3},{5,4},{6,5},{7,6},{8,7},{9,8},{10,9},{11,1... | collective-permute-start | bytes 663560 | tf_op jit(solution)/shard_map/ppermute | solution.py:36
  50.1 10.4 %collective-permute-start.10 = (f32[64,11,32]{0,2,1:T(8,128)S(1)}, f32[64,11,32]{0,2,1:T(8,128)S(1)}, u32[]{:S(2)}, u32[]{:S(2)}) collective-permute-start(f32[64,11,32]{0,2,1:T(8,128)S(1)} %concatenate.53), channel_id=1, source_target_pairs={{0,16},{8,24},{16,0},{24,8},{1,17},{9,25},{17,1},{25,9},{2,18},{10... | collective-permute-start | bytes 270344 | tf_op jit(solution)/shard_map/ppermute | solution.py:25
  51.7 10.5 %copy-start.9 = (s32[32]{0:T(128)S(1)}, s32[32]{0:T(128)}, u32[]{:S(2)}) copy-start(s32[32]{0:T(128)} %param.33) | copy-start | bytes 388
  64.6 0.6 copy-start.6
  64.6 0.7 copy-start.5
  64.6 0.8 %copy-start.4 = (f32[24,18,128]{2,1,0:T(8,128)}, f32[24,18,128]{2,1,0:T(8,128)S(1)}, u32[]{:S(2)}) copy-start(f32[24,18,128]{2,1,0:T(8,128)S(1)} %collective-permute-done.3.hyu_ref) | copy-start | bytes 663556
  65.4 0.7 copy-start.3

commit v4 on v3

--- a/solution.py
+++ b/solution.py
@@ -269,6 +269,32 @@
     last_y = lax.axis_index(GY_WA) == lax.axis_size(GY_WA) - 1
     edge = jnp.stack([last_x, last_y]).astype(jnp.int32)
 
+    nf = 2 + 4 * ndir
+    vmem = pl.BlockSpec(memory_space=pltpu.VMEM)
+    x_low, x_high, y_low, y_high = pl.pallas_call(
+        pack_kernel,
+        out_shape=[
+            jax.ShapeDtypeStruct((layers, rows, nf + 2), jnp.float32),
+            jax.ShapeDtypeStruct((layers, rows, nf), jnp.float32),
+            jax.ShapeDtypeStruct((layers, nf + 2, cols), jnp.float32),
+            jax.ShapeDtypeStruct((layers, nf, cols), jnp.float32),
+        ],
+        in_specs=[vmem] * 8,
+        out_specs=[vmem] * 4,
+        cost_estimate=pl.CostEstimate(
+            flops=layers * rows * cols * 160,
+            transcendentals=0,
+            bytes_accessed=(6 + 4 * ndir) * layers * rows * cols * 4,
+        ),
+    )(pressure, saturation, directions, adjoint_weights, trans_x, upwind_x, trans_y, upwind_y)
+    x_low, x_high, y_low, y_high, pressure, saturation, directions, adjoint_weights = lax.optimization_barrier(
+        (x_low, x_high, y_low, y_high, pressure, saturation, directions, adjoint_weights)
+    )
+    hxl = shift_along(x_low, "gx", True)
+    hxr = shift_along(x_high, "gx", False)
+    hyd = shift_along(y_low, GY_WA, True)
+    hyu = shift_along(y_high, GY_WA, False)
+
     lane_hit = (jnp.arange(cols)[:, None] == (perf_col % cols)[None, :]).astype(jnp.float32)
     row_hit = (jnp.arange(rows)[:, None] == (perf_col // cols)[None, :]).astype(jnp.float32)
 
@@ -305,30 +331,9 @@
         axis=0,
     )
     packed = jnp.concatenate([row_sums, perf_well.astype(jnp.float32)[None]], axis=0)
+    packed, hxl, hxr, hyd, hyu = lax.optimization_barrier((packed, hxl, hxr, hyd, hyu))
     everyone = gather_everywhere(packed)
 
-    nf = 2 + 4 * ndir
-    vmem = pl.BlockSpec(memory_space=pltpu.VMEM)
-    x_low, x_high, y_low, y_high = pl.pallas_call(
-        pack_kernel,
-        out_shape=[
-            jax.ShapeDtypeStruct((layers, rows, nf + 2), jnp.float32),
-            jax.ShapeDtypeStruct((layers, rows, nf), jnp.float32),
-            jax.ShapeDtypeStruct((layers, nf + 2, cols), jnp.float32),
-            jax.ShapeDtypeStruct((layers, nf, cols), jnp.float32),
-        ],
-        in_specs=[vmem] * 8,
-        out_specs=[vmem] * 4,
-        cost_estimate=pl.CostEstimate(
-            flops=layers * rows * cols * 160,
-            transcendentals=0,
-            bytes_accessed=(6 + 4 * ndir) * layers * rows * cols * 4,
-        ),
-    )(pressure, saturation, directions, adjoint_weights, trans_x, upwind_x, trans_y, upwind_y)
-    hxl = shift_along(x_low, "gx", True)
-    hxr = shift_along(x_high, "gx", False)
-    hyd = shift_along(y_low, GY_WA, True)
-    hyu = shift_along(y_high, GY_WA, False)
 
     all_sums = jnp.moveaxis(everyone[:, :-1], 1, 0).reshape(row_sums.shape[0], -1)
     all_wells = everyone[:, -1].reshape(-1)

time: 74.9 us -> 75.6 us (level)
  the two profiles are of different devices: /device:TPU:59 before, /device:TPU:26 now
where the time goes in v4:
time: 75.6 us; the launch traced here: 75.5 us
  waiting for transfers between devices  27.2 us (36%)
  starting transfers between devices  24.2 us (32%)
  Pallas kernels  13.4 us (18%)
  matrix products  4.57 us (6%)
  local copies, waits for them, and re-layouts  4.12 us (5%)
  between operations  1.12 us (1%)
  other arithmetic  0.91 us (1%)
    ppermute x7, waiting for transfers between devices, gather_everywhere(): other = lax.ppermute(held, axis, [(i, i ^ step) for i in range(size)])  25.8 us
    ppermute x7, starting transfers between devices, gather_everywhere(): other = lax.ppermute(held, axis, [(i, i ^ step) for i in range(size)])  12.6 us
    ppermute x4, starting transfers between devices, shift_along(): return lax.ppermute(block, axis, pairs)  11.5 us
    pallas_call x1, Pallas kernels, body(): pl.pallas_call(stencil_kernel, out_shape=[jax.ShapeDtypeStruct((2,) + spa...  8.36 us
    pallas_call x1, Pallas kernels, body(): pl.pallas_call(pack_kernel, out_shape=[jax.ShapeDtypeStruct((layers, rows...  5.04 us
    dot_general x1, matrix products, body(): spread = jnp.dot(by_row, lane_hit.T, precision=lax.Precision.HIGHEST)  2.27 us
    dot_general x4, matrix products, at_perfs(): by_lane = jnp.dot(field, lane_hit, precision=lax.Precision.HIGHEST)  1.89 us
  transfers between devices with their start and end apart: 11, of which 8 were waited for; matrix products, arithmetic and copies ran while one was open for 7% of the time, Pallas kernels for 0%

profile of v4, /device:TPU:26, one launch (start us, length us, event | category | flops | bytes accessed | tf_op | source)
XLA Modules:
  0.0 75.5 jit_solution(4299812311372926500)
XLA Ops:
  0.7 5.0 %shard_map.202 = (f32[24,8,20]{2,1,0:T(8,128)}, f32[24,8,18]{2,1,0:T(8,128)}, f32[24,20,128]{2,1,0:T(8,128)}, f32[24,18,128]{2,1,0:T(8,128)}) custom-call(f32[24,8,128]{2,1,0:T(8,128)} %p_ref.2, f32[24,8,128]{2,1,0:T(8,128)} %s_ref.2, f32[4,2,24,8,128]{4,3,2,1,0:T(8,128)} %d_ref.2, f32[4,2,24,8,128]{4,3,2,1,0:T(8,128)} %w_ref.2, f32[24,8,128]{2,1,0:T(8,128)} %tx_ref.3, ...), custom_call_target="tpu_custom_call" | custom-call | flops 3932160 | bytes 2162688 | tf_op jit(solution)/shard_map/pallas_call | solution.py:274
  5.8 3.5 %collective-permute-start = (f32[24,8,20]{2,1,0:T(8,128)}, f32[24,8,20]{2,1,0:T(8,128)S(1)}, u32[]{:S(2)}, u32[]{:S(2)}) collective-permute-start(f32[24,8,20]{2,1,0:T(8,128)} %get-tuple-element.29), channel_id=1, source_target_pairs={{0,32},{32,64},{64,96},{1,33},{33,65},{65,97},{2,34},{34,66},{66,9... | collective-permute-start | bytes 46088 | tf_op jit(solution)/shard_map/ppermute | solution.py:36
  9.3 2.4 %collective-permute-start.1 = (f32[24,8,18]{2,1,0:T(8,128)}, f32[24,8,18]{2,1,0:T(8,128)S(1)}, u32[]{:S(2)}, u32[]{:S(2)}) collective-permute-start(f32[24,8,18]{2,1,0:T(8,128)} %get-tuple-element.30), channel_id=1, source_target_pairs={{32,0},{64,32},{96,64},{33,1},{65,33},{97,65},{34,2},{66,34},{98,6... | collective-permute-start | bytes 41480 | tf_op jit(solution)/shard_map/ppermute | solution.py:36
  11.8 1.9 %collective-permute-start.2 = (f32[24,20,128]{2,1,0:T(8,128)}, f32[24,20,128]{2,1,0:T(8,128)S(1)}, u32[]{:S(2)}, u32[]{:S(2)}) collective-permute-start(f32[24,20,128]{2,1,0:T(8,128)} %get-tuple-element.31), channel_id=1, source_target_pairs={{0,1},{1,2},{2,3},{3,4},{4,5},{5,6},{6,7},{7,8},{8,9},{9,10},{10,1... | collective-permute-start | bytes 737288 | tf_op jit(solution)/shard_map/ppermute | solution.py:36
  13.7 3.6 %collective-permute-start.3 = (f32[24,18,128]{2,1,0:T(8,128)}, f32[24,18,128]{2,1,0:T(8,128)S(1)}, u32[]{:S(2)}, u32[]{:S(2)}) collective-permute-start(f32[24,18,128]{2,1,0:T(8,128)} %get-tuple-element.32), channel_id=1, source_target_pairs={{1,0},{2,1},{3,2},{4,3},{5,4},{6,5},{7,6},{8,7},{9,8},{10,9},{11,1... | collective-permute-start | bytes 663560 | tf_op jit(solution)/shard_map/ppermute | solution.py:36
  17.4 0.7 gather_fusion
  18.7 0.7 fusion.3
  19.4 0.7 fusion.2
  20.5 1.4 %collective-permute-done.3.hyu_ref = f32[24,18,128]{2,1,0:T(8,128)S(1)} collective-permute-done((f32[24,18,128]{2,1,0:T(8,128)}, f32[24,18,128]{2,1,0:T(8,128)S(1)}, u32[]{:S(2)}, u32[]{:S(2)}) %collective-permute-start.3) | collective-permute-done | bytes 221216 | tf_op jit(solution)/shard_map/ppermute | solution.py:36
  21.9 3.9 %collective-permute-start.4 = (f32[1,11,32]{2,1,0:T(8,128)S(1)}, f32[1,11,32]{2,1,0:T(8,128)S(1)}, u32[]{:S(2)}, u32[]{:S(2)}) collective-permute-start(f32[1,11,32]{2,1,0:T(8,128)S(1)} %bitcast.67), channel_id=1, source_target_pairs={{0,1},{1,0},{2,3},{3,2},{4,5},{5,4},{6,7},{7,6},{8,9},{9,8},{10,11... | collective-permute-start | bytes 4232 | tf_op jit(solution)/shard_map/ppermute | solution.py:25
  25.8 0.8 %collective-permute-done.4 = f32[1,11,32]{2,1,0:T(8,128)S(1)} collective-permute-done((f32[1,11,32]{2,1,0:T(8,128)S(1)}, f32[1,11,32]{2,1,0:T(8,128)S(1)}, u32[]{:S(2)}, u32[]{:S(2)}) %collective-permute-start.4) | collective-permute-done | bytes 1440 | tf_op jit(solution)/shard_map/ppermute | solution.py:25
  26.7 3.7 %collective-permute-done.5 = f32[2,11,32]{2,1,0:T(8,128)S(1)} collective-permute-done((f32[2,11,32]{2,1,0:T(8,128)S(1)}, f32[2,11,32]{2,1,0:T(8,128)S(1)}, u32[]{:S(2)}, u32[]{:S(2)}) %collective-permute-start.5) | collective-permute-done | bytes 2848 | tf_op jit(solution)/shard_map/ppermute | solution.py:25
  30.4 2.1 %collective-permute-start.6 = (f32[4,11,32]{2,1,0:T(8,128)S(1)}, f32[4,11,32]{2,1,0:T(8,128)S(1)}, u32[]{:S(2)}, u32[]{:S(2)}) collective-permute-start(f32[4,11,32]{2,1,0:T(8,128)S(1)} %pad_maximum_fusion.1), channel_id=1, source_target_pairs={{0,64},{32,96},{64,0},{96,32},{1,65},{33,97},{65,1},{97,33},{2,66}... | collective-permute-start | bytes 16904 | tf_op jit(solution)/shard_map/ppermute | solution.py:25
  32.5 3.3 %collective-permute-done.6 = f32[4,11,32]{2,1,0:T(8,128)S(1)} collective-permute-done((f32[4,11,32]{2,1,0:T(8,128)S(1)}, f32[4,11,32]{2,1,0:T(8,128)S(1)}, u32[]{:S(2)}, u32[]{:S(2)}) %collective-permute-start.6) | collective-permute-done | bytes 5664 | tf_op jit(solution)/shard_map/ppermute | solution.py:25
  35.9 4.5 %collective-permute-done.7 = f32[8,11,32]{2,1,0:T(8,128)S(1)} collective-permute-done((f32[8,11,32]{2,1,0:T(8,128)S(1)}, f32[8,11,32]{2,1,0:T(8,128)S(1)}, u32[]{:S(2)}, u32[]{:S(2)}) %collective-permute-start.7) | collective-permute-done | bytes 11296 | tf_op jit(solution)/shard_map/ppermute | solution.py:25
  40.5 6.5 %collective-permute-done.8 = f32[16,11,32]{2,1,0:T(8,128)S(1)} collective-permute-done((f32[16,11,32]{2,1,0:T(8,128)S(1)}, f32[16,11,32]{2,1,0:T(8,128)S(1)}, u32[]{:S(2)}, u32[]{:S(2)}) %collective-permute-start.8) | collective-permute-done | bytes 22560 | tf_op jit(solution)/shard_map/ppermute | solution.py:25
  47.0 2.0 %collective-permute-start.9 = (f32[32,11,32]{2,1,0:T(8,128)S(1)}, f32[32,11,32]{2,1,0:T(8,128)S(1)}, u32[]{:S(2)}, u32[]{:S(2)}) collective-permute-start(f32[32,11,32]{2,1,0:T(8,128)S(1)} %constant_dynamic-update-slice_fusion.5), channel_id=1, source_target_pairs={{0,8},{8,0},{16,24},{24,16},{1,9},{9,1},{17,25},{25,17},{2,10},{10... | collective-permute-start | bytes 135176 | tf_op jit(solution)/shard_map/ppermute | solution.py:25
  49.0 0.7 gather_fusion.1
  50.5 4.1 %collective-permute-done.9 = f32[32,11,32]{2,1,0:T(8,128)S(1)} collective-permute-done((f32[32,11,32]{2,1,0:T(8,128)S(1)}, f32[32,11,32]{2,1,0:T(8,128)S(1)}, u32[]{:S(2)}, u32[]{:S(2)}) %collective-permute-start.9) | collective-permute-done | bytes 45088 | tf_op jit(solution)/shard_map/ppermute | solution.py:25
  55.2 4.4 %collective-permute-start.10 = (f32[64,11,32]{0,2,1:T(8,128)S(1)}, f32[64,11,32]{0,2,1:T(8,128)S(1)}, u32[]{:S(2)}, u32[]{:S(2)}) collective-permute-start(f32[64,11,32]{0,2,1:T(8,128)S(1)} %concatenate.53), channel_id=1, source_target_pairs={{0,16},{8,24},{16,0},{24,8},{1,17},{9,25},{17,1},{25,9},{2,18},{10... | collective-permute-start | bytes 270344 | tf_op jit(solution)/shard_map/ppermute | solution.py:25
  59.6 0.6 add_convert_fusion.edge_ref
  60.2 2.9 %collective-permute-done.10 = f32[64,11,32]{0,2,1:T(8,128)S(1)} collective-permute-done((f32[64,11,32]{0,2,1:T(8,128)S(1)}, f32[64,11,32]{0,2,1:T(8,128)S(1)}, u32[]{:S(2)}, u32[]{:S(2)}) %collective-permute-start.10) | collective-permute-done | bytes 90144 | tf_op jit(solution)/shard_map/ppermute | solution.py:25
  64.8 2.3 %fusion.spread_ref = f32[9,2,24,8,128]{4,3,2,1,0:T(8,128)} fusion(f32[8,32]{1,0:T(8,128)S(1)} %fusion.32, f32[9,2,24,32]{3,2,1,0:T(8,128)S(1)} %maximum_maximum_fusion, s32[32]{0:T(128)S(1)} %get-tuple-element.80), kind=kOutput, calls=%fused_computation.2 | convolution fusion | flops 169984000 | bytes 1825920 | tf_op jit(solution)/shard_map/dot_general | solution.py:352
  67.1 8.4 %shard_map.203 = (f32[2,24,8,128]{3,2,1,0:T(8,128)}, f32[4,2,24,8,128]{4,3,2,1,0:T(8,128)}, f32[4,2,24,8,128]{4,3,2,1,0:T(8,128)}) custom-call(s32[2]{0:T(128)} %add_convert_fusion.edge_ref, f32[24,8,128]{2,1,0:T(8,128)} %p_ref.2, f32[24,8,128]{2,1,0:T(8,128)} %s_ref.2, f32[24,8,128]{2,1,0:T(8,128)} %so_ref.1, f32[24,8,128]{2,1,0:T(8,128)} %pore_ref.1, ...), custom_call_target="tpu_custom_call" | custom-call | flops 29491200 | bytes 9043968 | tf_op jit(solution)/shard_map/pallas_call | solution.py:354
  (86 shorter events, 4.2 us)
Async XLA Ops:
  0.6 16.8 %copy-start = (f32[2048]{0:T(1024)S(1)}, f32[2048]{0:T(1024)}, u32[]{:S(2)}) copy-start(f32[2048]{0:T(1024)} %param.38) | copy-start | bytes 24580
  0.6 18.1 %copy-start.3 = (f32[4,2,24,8,128]{4,3,2,1,0:T(8,128)S(1)}, f32[4,2,24,8,128]{4,3,2,1,0:T(8,128)}, u32[]{:S(2)}) copy-start(f32[4,2,24,8,128]{4,3,2,1,0:T(8,128)} %w_ref.2) | copy-start | bytes 2359300
  0.7 18.8 %copy-start.2 = (f32[4,2,24,8,128]{4,3,2,1,0:T(8,128)S(1)}, f32[4,2,24,8,128]{4,3,2,1,0:T(8,128)}, u32[]{:S(2)}) copy-start(f32[4,2,24,8,128]{4,3,2,1,0:T(8,128)} %d_ref.2) | copy-start | bytes 2359300
  0.7 17.8 %copy-start.5 = (f32[24,8,128]{2,1,0:T(8,128)S(1)}, f32[24,8,128]{2,1,0:T(8,128)}, u32[]{:S(2)}) copy-start(f32[24,8,128]{2,1,0:T(8,128)} %s_ref.2) | copy-start | bytes 294916
  0.7 17.5 %copy-start.4 = (f32[24,8,128]{2,1,0:T(8,128)S(1)}, f32[24,8,128]{2,1,0:T(8,128)}, u32[]{:S(2)}) copy-start(f32[24,8,128]{2,1,0:T(8,128)} %p_ref.2) | copy-start | bytes 294916
  0.7 16.7 %copy-start.13 = (s32[32]{0:T(128)S(1)}, s32[32]{0:T(128)}, u32[]{:S(2)}) copy-start(s32[32]{0:T(128)} %param.34) | copy-start | bytes 388
  0.7 16.7 %copy-start.12 = (s32[32]{0:T(128)S(1)}, s32[32]{0:T(128)}, u32[]{:S(2)}) copy-start(s32[32]{0:T(128)} %param.33) | copy-start | bytes 388
  5.8 14.4 %copy-start.10 = (f32[32]{0:T(128)S(1)}, f32[32]{0:T(128)}, u32[]{:S(2)}) copy-start(f32[32]{0:T(128)} %param.37) | copy-start | bytes 388
  5.8 14.7 %collective-permute-start = (f32[24,8,20]{2,1,0:T(8,128)}, f32[24,8,20]{2,1,0:T(8,128)S(1)}, u32[]{:S(2)}, u32[]{:S(2)}) collective-permute-start(f32[24,8,20]{2,1,0:T(8,128)} %get-tuple-element.29), channel_id=1, source_target_pairs={{0,32},{32,64},{64,96},{1,33},{33,65},{65,97},{2,34},{34,66},{66,9... | collective-permute-start | bytes 46088 | tf_op jit(solution)/shard_map/ppermute | solution.py:36
  9.3 11.1 %collective-permute-start.1 = (f32[24,8,18]{2,1,0:T(8,128)}, f32[24,8,18]{2,1,0:T(8,128)S(1)}, u32[]{:S(2)}, u32[]{:S(2)}) collective-permute-start(f32[24,8,18]{2,1,0:T(8,128)} %get-tuple-element.30), channel_id=1, source_target_pairs={{32,0},{64,32},{96,64},{33,1},{65,33},{97,65},{34,2},{66,34},{98,6... | collective-permute-start | bytes 41480 | tf_op jit(solution)/shard_map/ppermute | solution.py:36
  11.8 10.1 %collective-permute-start.2 = (f32[24,20,128]{2,1,0:T(8,128)}, f32[24,20,128]{2,1,0:T(8,128)S(1)}, u32[]{:S(2)}, u32[]{:S(2)}) collective-permute-start(f32[24,20,128]{2,1,0:T(8,128)} %get-tuple-element.31), channel_id=1, source_target_pairs={{0,1},{1,2},{2,3},{3,4},{4,5},{5,6},{6,7},{7,8},{8,9},{9,10},{10,1... | collective-permute-start | bytes 737288 | tf_op jit(solution)/shard_map/ppermute | solution.py:36
  13.7 8.2 %collective-permute-start.3 = (f32[24,18,128]{2,1,0:T(8,128)}, f32[24,18,128]{2,1,0:T(8,128)S(1)}, u32[]{:S(2)}, u32[]{:S(2)}) collective-permute-start(f32[24,18,128]{2,1,0:T(8,128)} %get-tuple-element.32), channel_id=1, source_target_pairs={{1,0},{2,1},{3,2},{4,3},{5,4},{6,5},{7,6},{8,7},{9,8},{10,9},{11,1... | collective-permute-start | bytes 663560 | tf_op jit(solution)/shard_map/ppermute | solution.py:36
  18.7 30.3 %copy-start.1 = (f32[2048]{0:T(1024)S(1)}, f32[2048]{0:T(1024)}, u32[]{:S(2)}) copy-start(f32[2048]{0:T(1024)} %param.39) | copy-start | bytes 24580
  20.5 34.7 %copy-start.9 = (f32[24,8,18]{2,1,0:T(8,128)}, f32[24,8,18]{2,1,0:T(8,128)S(1)}, u32[]{:S(2)}) copy-start(f32[24,8,18]{2,1,0:T(8,128)S(1)} %collective-permute-done.1.hxr_ref) | copy-start | bytes 41476
  20.5 34.7 %copy-start.8 = (f32[24,8,20]{2,1,0:T(8,128)}, f32[24,8,20]{2,1,0:T(8,128)S(1)}, u32[]{:S(2)}) copy-start(f32[24,8,20]{2,1,0:T(8,128)S(1)} %collective-permute-done.hxl_ref) | copy-start | bytes 46084
  21.9 33.3 %copy-start.7 = (f32[24,18,128]{2,1,0:T(8,128)}, f32[24,18,128]{2,1,0:T(8,128)S(1)}, u32[]{:S(2)}) copy-start(f32[24,18,128]{2,1,0:T(8,128)S(1)} %collective-permute-done.3.hyu_ref) | copy-start | bytes 663556
  21.9 33.3 %copy-start.6 = (f32[24,20,128]{2,1,0:T(8,128)}, f32[24,20,128]{2,1,0:T(8,128)S(1)}, u32[]{:S(2)}) copy-start(f32[24,20,128]{2,1,0:T(8,128)S(1)} %collective-permute-done.2.hyd_ref) | copy-start | bytes 737284
  21.9 4.8 %collective-permute-start.4 = (f32[1,11,32]{2,1,0:T(8,128)S(1)}, f32[1,11,32]{2,1,0:T(8,128)S(1)}, u32[]{:S(2)}, u32[]{:S(2)}) collective-permute-start(f32[1,11,32]{2,1,0:T(8,128)S(1)} %bitcast.67), channel_id=1, source_target_pairs={{0,1},{1,0},{2,3},{3,2},{4,5},{5,4},{6,7},{7,6},{8,9},{9,8},{10,11... | collective-permute-start | bytes 4232 | tf_op jit(solution)/shard_map/ppermute | solution.py:25
  26.7 3.7 %collective-permute-start.5 = (f32[2,11,32]{2,1,0:T(8,128)S(1)}, f32[2,11,32]{2,1,0:T(8,128)S(1)}, u32[]{:S(2)}, u32[]{:S(2)}) collective-permute-start(f32[2,11,32]{2,1,0:T(8,128)S(1)} %pad_maximum_fusion.3), channel_id=1, source_target_pairs={{0,32},{32,0},{64,96},{96,64},{1,33},{33,1},{65,97},{97,65},{2,34}... | collective-permute-start | bytes 8456 | tf_op jit(solution)/shard_map/ppermute | solution.py:25
  30.4 5.4 %collective-permute-start.6 = (f32[4,11,32]{2,1,0:T(8,128)S(1)}, f32[4,11,32]{2,1,0:T(8,128)S(1)}, u32[]{:S(2)}, u32[]{:S(2)}) collective-permute-start(f32[4,11,32]{2,1,0:T(8,128)S(1)} %pad_maximum_fusion.1), channel_id=1, source_target_pairs={{0,64},{32,96},{64,0},{96,32},{1,65},{33,97},{65,1},{97,33},{2,66}... | collective-permute-start | bytes 16904 | tf_op jit(solution)/shard_map/ppermute | solution.py:25
  35.8 4.6 %collective-permute-start.7 = (f32[8,11,32]{2,1,0:T(8,128)S(1)}, f32[8,11,32]{2,1,0:T(8,128)S(1)}, u32[]{:S(2)}, u32[]{:S(2)}) collective-permute-start(f32[8,11,32]{2,1,0:T(8,128)S(1)} %pad_maximum_fusion), channel_id=1, source_target_pairs={{0,2},{2,0},{4,6},{6,4},{1,3},{3,1},{5,7},{7,5},{8,10},{10,8},{12,... | collective-permute-start | bytes 33800 | tf_op jit(solution)/shard_map/ppermute | solution.py:25
  40.4 6.6 %collective-permute-start.8 = (f32[16,11,32]{2,1,0:T(8,128)S(1)}, f32[16,11,32]{2,1,0:T(8,128)S(1)}, u32[]{:S(2)}, u32[]{:S(2)}) collective-permute-start(f32[16,11,32]{2,1,0:T(8,128)S(1)} %get-tuple-element.49), channel_id=1, source_target_pairs={{0,4},{2,6},{4,0},{6,2},{1,5},{3,7},{5,1},{7,3},{8,12},{10,14},{12... | collective-permute-start | bytes 67592 | tf_op jit(solution)/shard_map/ppermute | solution.py:25
  47.0 7.6 %collective-permute-start.9 = (f32[32,11,32]{2,1,0:T(8,128)S(1)}, f32[32,11,32]{2,1,0:T(8,128)S(1)}, u32[]{:S(2)}, u32[]{:S(2)}) collective-permute-start(f32[32,11,32]{2,1,0:T(8,128)S(1)} %constant_dynamic-update-slice_fusion.5), channel_id=1, source_target_pairs={{0,8},{8,0},{16,24},{24,16},{1,9},{9,1},{17,25},{25,17},{2,10},{10... | collective-permute-start | bytes 135176 | tf_op jit(solution)/shard_map/ppermute | solution.py:25
  55.2 7.9 %collective-permute-start.10 = (f32[64,11,32]{0,2,1:T(8,128)S(1)}, f32[64,11,32]{0,2,1:T(8,128)S(1)}, u32[]{:S(2)}, u32[]{:S(2)}) collective-permute-start(f32[64,11,32]{0,2,1:T(8,128)S(1)} %concatenate.53), channel_id=1, source_target_pairs={{0,16},{8,24},{16,0},{24,8},{1,17},{9,25},{17,1},{25,9},{2,18},{10... | collective-permute-start | bytes 270344 | tf_op jit(solution)/shard_map/ppermute | solution.py:25
  (2 other events, 28.7 us)

commit v5 on v4

--- a/solution.py
+++ b/solution.py
@@ -17,15 +17,8 @@
 
 
 def gather_everywhere(block):
-    held = block[None]
-    for axis in ("wa", "gx", "gy_1", "gy_0"):
-        size = lax.axis_size(axis)
-        step = 1
-        while step < size:
-            other = lax.ppermute(held, axis, [(i, i ^ step) for i in range(size)])
-            held = jnp.concatenate([held, other], axis=0)
-            step *= 2
-    return held
+    peers = lax.axis_size(GX_GY_WA)
+    return lax.all_to_all(jnp.broadcast_to(block[None], (peers,) + block.shape), GX_GY_WA, 0, 0)
 
 
 def shift_along(block, axis, down):
@@ -331,7 +324,6 @@
         axis=0,
     )
     packed = jnp.concatenate([row_sums, perf_well.astype(jnp.float32)[None]], axis=0)
-    packed, hxl, hxr, hyd, hyu = lax.optimization_barrier((packed, hxl, hxr, hyd, hyu))
     everyone = gather_everywhere(packed)
 
 

time: 75.6 us -> 53.1 us (0.70)
  the two profiles are of different devices: /device:TPU:26 before, /device:TPU:27 now
where the time goes in v5:
time: 53.1 us; the launch traced here: 52.2 us
  starting transfers between devices  21.7 us (41%)
  Pallas kernels  13.3 us (25%)
  local copies, waits for them, and re-layouts  5.91 us (11%)
  matrix products  4.57 us (9%)
  other arithmetic  4.24 us (8%)
  waiting for transfers between devices  1.43 us (3%)
  between operations  1 us (2%)
    ppermute x4, starting transfers between devices, shift_along(): return lax.ppermute(block, axis, pairs)  11.2 us
    all_to_all x1, starting transfers between devices, gather_everywhere(): lax.all_to_all(jnp.broadcast_to(block[None], (peers,) + block.shape), GX_...  10.5 us
    pallas_call x1, Pallas kernels, body(): pl.pallas_call(stencil_kernel, out_shape=[jax.ShapeDtypeStruct((2,) + spa...  8.36 us
    pallas_call x1, Pallas kernels, body(): pl.pallas_call(pack_kernel, out_shape=[jax.ShapeDtypeStruct((layers, rows...  4.95 us
    unnamed x32, local copies, waits for them, and re-layouts  2.91 us
    dot_general x1, matrix products, body(): spread = jnp.dot(by_row, lane_hit.T, precision=lax.Precision.HIGHEST)  2.27 us
    dot_general x4, matrix products, at_perfs(): by_lane = jnp.dot(field, lane_hit, precision=lax.Precision.HIGHEST)  1.9 us
    ppermute x4, waiting for transfers between devices, shift_along(): return lax.ppermute(block, axis, pairs)  1.42 us
  transfers between devices with their start and end apart: 5, of which 1 were waited for; matrix products, arithmetic and copies ran while one was open for 13% of the time, Pallas kernels for 0%

profile of v5, /device:TPU:27, one launch (start us, length us, event | category | flops | bytes accessed | tf_op | source)
XLA Modules:
  0.0 52.2 jit_solution(8331342535161016141)
XLA Ops:
  0.7 0.8 %and_select_fusion.1 = (s32[32]{0:T(128)S(1)}, s32[32]{0:T(128)S(1)}) fusion(s32[32]{0:T(128)} %param.34), kind=kLoop, calls=%fused_computation.70 | loop fusion | flops 608 | bytes 384 | tf_op jit(solution)/shard_map/jit(remainder)/select_n | solution.py:291
  1.5 0.7 %fusion.43 = (f32[32]{0:T(128)S(1)}, f32[1,32]{1,0:T(1,128)S(1)}, s32[32]{0:T(128)S(1)}) fusion(s32[32]{0:T(128)} %param.33), kind=kLoop, calls=%fused_computation.88 | loop fusion | flops 128 | bytes 512 | tf_op jit(solution)/shard_map/convert_element_type | solution.py:326
  2.2 0.7 %gather_fusion = f32[32]{0:T(128)S(1)} fusion(f32[2048]{0:T(1024)S(1)} %copy-done, s32[1024]{0:T(1024)S(1)} %pad_clamp_fusion), kind=kCustom, calls=%fused_computation.clone | custom fusion | bytes 384 | tf_op jit(solution)/shard_map/jit(_take)/gather | solution.py:307
  2.9 0.7 %broadcast_select_fusion = f32[32]{0:T(128)S(1)} fusion(f32[32]{0:T(128)S(1)} %gather_fusion, s32[32]{0:T(128)} %param.33), kind=kLoop, calls=%fused_computation.78 | loop fusion | flops 224 | bytes 384 | tf_op jit(solution)/shard_map/jit(_take)/select_n | solution.py:307
  3.7 5.0 %shard_map.202 = (f32[24,8,20]{2,1,0:T(8,128)}, f32[24,8,18]{2,1,0:T(8,128)}, f32[24,20,128]{2,1,0:T(8,128)}, f32[24,18,128]{2,1,0:T(8,128)}) custom-call(f32[24,8,128]{2,1,0:T(8,128)} %p_ref.2, f32[24,8,128]{2,1,0:T(8,128)} %s_ref.2, f32[4,2,24,8,128]{4,3,2,1,0:T(8,128)} %d_ref.2, f32[4,2,24,8,128]{4,3,2,1,0:T(8,128)} %w_ref.2, f32[24,8,128]{2,1,0:T(8,128)} %tx_ref.3, ...), custom_call_target="tpu_custom_call" | custom-call | flops 3932160 | bytes 2162688 | tf_op jit(solution)/shard_map/pallas_call | solution.py:267
  9.2 0.7 %fusion.3 = f32[4,2,24,32]{3,2,1,0:T(8,128)S(1)} fusion(f32[4,2,24,8,128]{4,3,2,1,0:T(8,128)S(1)} %copy-done.3, f32[8,32]{1,0:T(8,128)S(1)} %fusion.32, s32[32]{0:T(128)S(1)} %get-tuple-element.60), kind=kOutput, calls=%fused_computation.7 | convolution fusion | flops 75593728 | bytes 812160 | tf_op jit(solution)/shard_map/dot_general | solution.py:295
  9.9 0.7 %fusion.2 = f32[4,2,24,32]{3,2,1,0:T(8,128)S(1)} fusion(f32[4,2,24,8,128]{4,3,2,1,0:T(8,128)S(1)} %copy-done.2, f32[8,32]{1,0:T(8,128)S(1)} %fusion.32, s32[32]{0:T(128)S(1)} %get-tuple-element.60), kind=kOutput, calls=%fused_computation.6 | convolution fusion | flops 75593728 | bytes 812160 | tf_op jit(solution)/shard_map/dot_general | solution.py:295
  11.0 1.1 %reshape.528 = f32[128,1,352]{2,1,0:T(1,128)} reshape(f32[128,11,32]{2,1,0:T(8,128)S(1)} %broadcast_in_dim.31) | data formatting | bytes 360448
  12.1 10.5 %all-to-all-start = ((f32[128,1,352]{2,1,0:T(1,128)}), f32[128,1,352]{2,1,0:T(1,128)S(1)}, u32[]{:S(2)}, u32[]{:S(2)}) async-start(f32[128,1,352]{2,1,0:T(1,128)} %reshape.528), calls=%async_computation | async-start | bytes 393216 | tf_op jit(solution)/shard_map/all_to_all | solution.py:21
  22.7 3.1 %collective-permute-start = (f32[24,8,20]{2,1,0:T(8,128)S(1)}, f32[24,8,20]{2,1,0:T(8,128)S(1)}, u32[]{:S(2)}, u32[]{:S(2)}) collective-permute-start(f32[24,8,20]{2,1,0:T(8,128)S(1)} %copy-done.13), channel_id=1, source_target_pairs={{0,32},{32,64},{64,96},{1,33},{33,65},{65,97},{2,34},{34,66},{66,9... | collective-permute-start | bytes 46088 | tf_op jit(solution)/shard_map/ppermute | solution.py:29
  25.8 2.2 %collective-permute-start.1 = (f32[24,8,18]{2,1,0:T(8,128)}, f32[24,8,18]{2,1,0:T(8,128)S(1)}, u32[]{:S(2)}, u32[]{:S(2)}) collective-permute-start(f32[24,8,18]{2,1,0:T(8,128)} %get-tuple-element.25), channel_id=1, source_target_pairs={{32,0},{64,32},{96,64},{33,1},{65,33},{97,65},{34,2},{66,34},{98,6... | collective-permute-start | bytes 41480 | tf_op jit(solution)/shard_map/ppermute | solution.py:29
  28.0 4.0 %collective-permute-start.2 = (f32[24,20,128]{2,1,0:T(8,128)}, f32[24,20,128]{2,1,0:T(8,128)S(1)}, u32[]{:S(2)}, u32[]{:S(2)}) collective-permute-start(f32[24,20,128]{2,1,0:T(8,128)} %get-tuple-element.26), channel_id=1, source_target_pairs={{0,1},{1,2},{2,3},{3,4},{4,5},{5,6},{6,7},{7,8},{8,9},{9,10},{10,1... | collective-permute-start | bytes 737288 | tf_op jit(solution)/shard_map/ppermute | solution.py:29
  32.0 1.9 %collective-permute-start.3 = (f32[24,18,128]{2,1,0:T(8,128)}, f32[24,18,128]{2,1,0:T(8,128)S(1)}, u32[]{:S(2)}, u32[]{:S(2)}) collective-permute-start(f32[24,18,128]{2,1,0:T(8,128)} %get-tuple-element.27), channel_id=1, source_target_pairs={{1,0},{2,1},{3,2},{4,3},{5,4},{6,5},{7,6},{8,7},{9,8},{10,9},{11,1... | collective-permute-start | bytes 663560 | tf_op jit(solution)/shard_map/ppermute | solution.py:29
  33.9 0.7 %gather_fusion.1 = f32[32]{0:T(128)S(1)} fusion(f32[2048]{0:T(1024)S(1)} %copy-done.1, s32[1024]{0:T(1024)S(1)} %pad_clamp_fusion), kind=kCustom, calls=%fused_computation.1.clone | custom fusion | bytes 384 | tf_op jit(solution)/shard_map/jit(_take)/gather | solution.py:334
  34.6 0.6 %add_convert_fusion.edge_ref = s32[2]{0:T(128)} fusion(pred[1]{0:T(512)(128)(4,1)} %bitcast.1, pred[1]{0:T(512)(128)(4,1)} %bitcast), kind=kLoop, calls=%fused_computation.67 | loop fusion | flops 4 | bytes 10 | tf_op jit(solution)/shard_map/convert_element_type | solution.py:263
  35.2 0.5 broadcast.527
  35.7 1.1 %reduce.6 = f32[128,352]{1,0:T(8,128)S(1)} reduce(f32[128,1,352]{2,1,0:T(1,128)S(1)} %all-to-all-done, f32[]{:T(128)} %broadcast.527), dimensions={1}, to_apply=%all_to_all.3.reduce_sub_computation | reduce | bytes 360452 | tf_op jit(solution)/shard_map/all_to_all | solution.py:21
  37.7 0.3 reshape.496
  38.1 0.4 fusion.8
  38.6 2.3 %fusion.spread_ref = f32[9,2,24,8,128]{4,3,2,1,0:T(8,128)} fusion(f32[8,32]{1,0:T(8,128)S(1)} %fusion.32, f32[9,2,24,32]{3,2,1,0:T(8,128)S(1)} %maximum_maximum_fusion, s32[32]{0:T(128)S(1)} %get-tuple-element.60), kind=kOutput, calls=%fused_computation.2 | convolution fusion | flops 169984000 | bytes 1825920 | tf_op jit(solution)/shard_map/dot_general | solution.py:344
  40.9 1.4 %collective-permute-done.3.hyu_ref = f32[24,18,128]{2,1,0:T(8,128)S(1)} collective-permute-done((f32[24,18,128]{2,1,0:T(8,128)}, f32[24,18,128]{2,1,0:T(8,128)S(1)}, u32[]{:S(2)}, u32[]{:S(2)}) %collective-permute-start.3) | collective-permute-done | bytes 221216 | tf_op jit(solution)/shard_map/ppermute | solution.py:29
  42.4 0.7 %copy-done.7 = f32[24,18,128]{2,1,0:T(8,128)} copy-done((f32[24,18,128]{2,1,0:T(8,128)}, f32[24,18,128]{2,1,0:T(8,128)S(1)}, u32[]{:S(2)}) %copy-start.7) | copy-done | bytes 221208
  43.1 0.7 %copy-done.6 = f32[24,20,128]{2,1,0:T(8,128)} copy-done((f32[24,20,128]{2,1,0:T(8,128)}, f32[24,20,128]{2,1,0:T(8,128)S(1)}, u32[]{:S(2)}) %copy-start.6) | copy-done | bytes 245784
  43.8 8.4 %shard_map.203 = (f32[2,24,8,128]{3,2,1,0:T(8,128)}, f32[4,2,24,8,128]{4,3,2,1,0:T(8,128)}, f32[4,2,24,8,128]{4,3,2,1,0:T(8,128)}) custom-call(s32[2]{0:T(128)} %add_convert_fusion.edge_ref, f32[24,8,128]{2,1,0:T(8,128)} %p_ref.2, f32[24,8,128]{2,1,0:T(8,128)} %s_ref.2, f32[24,8,128]{2,1,0:T(8,128)} %so_ref.1, f32[24,8,128]{2,1,0:T(8,128)} %pore_ref.1, ...), custom_call_target="tpu_custom_call" | custom-call | flops 29491200 | bytes 9043968 | tf_op jit(solution)/shard_map/pallas_call | solution.py:346
  (60 shorter events, 1.9 us)
Async XLA Ops:
  0.6 1.6 %copy-start = (f32[2048]{0:T(1024)S(1)}, f32[2048]{0:T(1024)}, u32[]{:S(2)}) copy-start(f32[2048]{0:T(1024)} %param.38) | copy-start | bytes 24580
  0.6 8.5 %copy-start.3 = (f32[4,2,24,8,128]{4,3,2,1,0:T(8,128)S(1)}, f32[4,2,24,8,128]{4,3,2,1,0:T(8,128)}, u32[]{:S(2)}) copy-start(f32[4,2,24,8,128]{4,3,2,1,0:T(8,128)} %w_ref.2) | copy-start | bytes 2359300
  0.7 8.2 %copy-start.5 = (f32[24,8,128]{2,1,0:T(8,128)S(1)}, f32[24,8,128]{2,1,0:T(8,128)}, u32[]{:S(2)}) copy-start(f32[24,8,128]{2,1,0:T(8,128)} %s_ref.2) | copy-start | bytes 294916
  0.7 7.9 %copy-start.4 = (f32[24,8,128]{2,1,0:T(8,128)S(1)}, f32[24,8,128]{2,1,0:T(8,128)}, u32[]{:S(2)}) copy-start(f32[24,8,128]{2,1,0:T(8,128)} %p_ref.2) | copy-start | bytes 294916
  2.9 7.0 %copy-start.2 = (f32[4,2,24,8,128]{4,3,2,1,0:T(8,128)S(1)}, f32[4,2,24,8,128]{4,3,2,1,0:T(8,128)}, u32[]{:S(2)}) copy-start(f32[4,2,24,8,128]{4,3,2,1,0:T(8,128)} %d_ref.2) | copy-start | bytes 2359300
  3.6 6.9 %copy-start.11 = (s32[32]{0:T(128)S(1)}, s32[32]{0:T(128)}, u32[]{:S(2)}) copy-start(s32[32]{0:T(128)} %param.35) | copy-start | bytes 388
  3.6 7.0 %copy-start.14 = (s32[32]{0:T(128)S(1)}, s32[32]{0:T(128)}, u32[]{:S(2)}) copy-start(s32[32]{0:T(128)} %param.36) | copy-start | bytes 388
  3.6 7.0 %copy-start.10 = (f32[32]{0:T(128)S(1)}, f32[32]{0:T(128)}, u32[]{:S(2)}) copy-start(f32[32]{0:T(128)} %param.37) | copy-start | bytes 388
  10.6 12.0 %copy-start.13 = (f32[24,8,20]{2,1,0:T(8,128)S(1)}, f32[24,8,20]{2,1,0:T(8,128)}, u32[]{:S(2)}) copy-start(f32[24,8,20]{2,1,0:T(8,128)} %get-tuple-element.24) | copy-start | bytes 46084
  10.7 23.2 %copy-start.1 = (f32[2048]{0:T(1024)S(1)}, f32[2048]{0:T(1024)}, u32[]{:S(2)}) copy-start(f32[2048]{0:T(1024)} %param.39) | copy-start | bytes 24580
  12.1 23.1 %all-to-all-start = ((f32[128,1,352]{2,1,0:T(1,128)}), f32[128,1,352]{2,1,0:T(1,128)S(1)}, u32[]{:S(2)}, u32[]{:S(2)}) async-start(f32[128,1,352]{2,1,0:T(1,128)} %reshape.528), calls=%async_computation | async-start | bytes 393216 | tf_op jit(solution)/shard_map/all_to_all | solution.py:21
  22.7 18.2 %collective-permute-start = (f32[24,8,20]{2,1,0:T(8,128)S(1)}, f32[24,8,20]{2,1,0:T(8,128)S(1)}, u32[]{:S(2)}, u32[]{:S(2)}) collective-permute-start(f32[24,8,20]{2,1,0:T(8,128)S(1)} %copy-done.13), channel_id=1, source_target_pairs={{0,32},{32,64},{64,96},{1,33},{33,65},{65,97},{2,34},{34,66},{66,9... | collective-permute-start | bytes 46088 | tf_op jit(solution)/shard_map/ppermute | solution.py:29
  25.8 15.1 %collective-permute-start.1 = (f32[24,8,18]{2,1,0:T(8,128)}, f32[24,8,18]{2,1,0:T(8,128)S(1)}, u32[]{:S(2)}, u32[]{:S(2)}) collective-permute-start(f32[24,8,18]{2,1,0:T(8,128)} %get-tuple-element.25), channel_id=1, source_target_pairs={{32,0},{64,32},{96,64},{33,1},{65,33},{97,65},{34,2},{66,34},{98,6... | collective-permute-start | bytes 41480 | tf_op jit(solution)/shard_map/ppermute | solution.py:29
  28.0 14.4 %collective-permute-start.2 = (f32[24,20,128]{2,1,0:T(8,128)}, f32[24,20,128]{2,1,0:T(8,128)S(1)}, u32[]{:S(2)}, u32[]{:S(2)}) collective-permute-start(f32[24,20,128]{2,1,0:T(8,128)} %get-tuple-element.26), channel_id=1, source_target_pairs={{0,1},{1,2},{2,3},{3,4},{4,5},{5,6},{6,7},{7,8},{8,9},{9,10},{10,1... | collective-permute-start | bytes 737288 | tf_op jit(solution)/shard_map/ppermute | solution.py:29
  32.0 10.4 %collective-permute-start.3 = (f32[24,18,128]{2,1,0:T(8,128)}, f32[24,18,128]{2,1,0:T(8,128)S(1)}, u32[]{:S(2)}, u32[]{:S(2)}) collective-permute-start(f32[24,18,128]{2,1,0:T(8,128)} %get-tuple-element.27), channel_id=1, source_target_pairs={{1,0},{2,1},{3,2},{4,3},{5,4},{6,5},{7,6},{8,7},{9,8},{10,9},{11,1... | collective-permute-start | bytes 663560 | tf_op jit(solution)/shard_map/ppermute | solution.py:29
  37.4 1.0 %copy-start.12 = (s32[32]{0:T(128)S(1)}, s32[32]{0:T(128)}, u32[]{:S(2)}) copy-start(s32[32]{0:T(128)} %param.33) | copy-start | bytes 388
  40.9 1.4 %copy-start.9 = (f32[24,8,18]{2,1,0:T(8,128)}, f32[24,8,18]{2,1,0:T(8,128)S(1)}, u32[]{:S(2)}) copy-start(f32[24,8,18]{2,1,0:T(8,128)S(1)} %collective-permute-done.1.hxr_ref) | copy-start | bytes 41476
  40.9 1.4 %copy-start.8 = (f32[24,8,20]{2,1,0:T(8,128)}, f32[24,8,20]{2,1,0:T(8,128)S(1)}, u32[]{:S(2)}) copy-start(f32[24,8,20]{2,1,0:T(8,128)S(1)} %collective-permute-done.hxl_ref) | copy-start | bytes 46084
  42.3 0.8 %copy-start.7 = (f32[24,18,128]{2,1,0:T(8,128)}, f32[24,18,128]{2,1,0:T(8,128)S(1)}, u32[]{:S(2)}) copy-start(f32[24,18,128]{2,1,0:T(8,128)S(1)} %collective-permute-done.3.hyu_ref) | copy-start | bytes 663556
  43.1 0.7 %copy-start.6 = (f32[24,20,128]{2,1,0:T(8,128)}, f32[24,20,128]{2,1,0:T(8,128)S(1)}, u32[]{:S(2)}) copy-start(f32[24,20,128]{2,1,0:T(8,128)S(1)} %collective-permute-done.2.hyd_ref) | copy-start | bytes 737284

commit v6 on v5

--- a/solution.py
+++ b/solution.py
@@ -128,6 +128,10 @@
     uz_ref,
     d_ref,
     w_ref,
+    pn_ref,
+    sn_ref,
+    dn_ref,
+    wn_ref,
     hxl_ref,
     hxr_ref,
     hyd_ref,
@@ -136,9 +140,12 @@
     r_out,
     jv_out,
     jt_out,
+    carry_ref,
 ):
     ndir = d_ref.shape[0]
-    layers, rows, cols = p_ref.shape
+    span, rows, cols = p_ref.shape
+    block = pl.program_id(0)
+    layers = span * pl.num_programs(0)
     lane = lax.broadcasted_iota(jnp.int32, (rows, cols), 1)
     sub = lax.broadcasted_iota(jnp.int32, (rows, cols), 0)
     first_lane = lane == 0
@@ -149,12 +156,12 @@
     cut_y = jnp.logical_and(last_sub, edge_ref[1] == 1)
     nf = 2 + 4 * ndir
 
-    def cells(k):
-        out = [p_ref[k], s_ref[k]]
+    def cells_of(pr, sr, dr, wr, k):
+        out = [pr[k], sr[k]]
         for half in range(2):
-            out += [d_ref[d, half, k] for d in range(ndir)]
+            out += [dr[d, half, k] for d in range(ndir)]
         for half in range(2):
-            out += [w_ref[d, half, k] for d in range(ndir)]
+            out += [wr[d, half, k] for d in range(ndir)]
         return out
 
     def group(flat):
@@ -185,10 +192,8 @@
                 ref, idx, extra = jt_out, (j % ndir, j // ndir, k), (1 + ndir + j % ndir, j // ndir, k)
             ref[idx] = vals[i] + spread_ref[extra]
 
-    def body(k, carry):
-        here = cells(k)
-        kn = jnp.minimum(k + 1, layers - 1)
-        above = cells(kn)
+    def layer(k, carry, above):
+        here = cells_of(p_ref, s_ref, d_ref, w_ref, k)
         left = [jnp.where(first_lane, col(hxl_ref, k, f), pltpu.roll(x, 1, 1)) for f, x in enumerate(here)]
         right = [jnp.where(last_lane, col(hxr_ref, k, f), pltpu.roll(x, cols - 1, 1)) for f, x in enumerate(here)]
         down = [jnp.where(first_sub, row(hyd_ref, k, f), pltpu.roll(x, 1, 0)) for f, x in enumerate(here)]
@@ -204,7 +209,7 @@
         ux_b = jnp.where(first_lane, col(hxl_ref, k, nf + 1), pltpu.roll(ux, 1, 1))
         ty_b = jnp.where(first_sub, row(hyd_ref, k, nf), pltpu.roll(ty, 1, 0))
         uy_b = jnp.where(first_sub, row(hyd_ref, k, nf + 1), pltpu.roll(uy, 1, 0))
-        tz = jnp.where(k < layers - 1, tz_ref[k], 0.0)
+        tz = jnp.where(block * span + k < layers - 1, tz_ref[k], 0.0)
         uz = uz_ref[k] == 1
 
         g_here = group(here)
@@ -230,8 +235,18 @@
         store(k, acc)
         return tuple(zb)
 
-    zero = jnp.zeros((rows, cols), jnp.float32)
-    lax.fori_loop(0, layers, body, tuple([zero] * nf))
+    @pl.when(block == 0)
+    def _():
+        carry_ref[...] = jnp.zeros_like(carry_ref)
+
+    def inner(k, carry):
+        return layer(k, carry, cells_of(p_ref, s_ref, d_ref, w_ref, k + 1))
+
+    carry = tuple(carry_ref[i] for i in range(nf))
+    carry = lax.fori_loop(0, span - 1, inner, carry)
+    carry = layer(span - 1, carry, cells_of(pn_ref, sn_ref, dn_ref, wn_ref, 0))
+    for i in range(nf):
+        carry_ref[i] = carry[i]
 
 
 def body(
@@ -343,15 +358,44 @@
     by_row = combined[..., None, :] * row_hit
     spread = jnp.dot(by_row, lane_hit.T, precision=lax.Precision.HIGHEST)
 
+    span = 6 if layers % 6 == 0 else layers
+    blocks = layers // span
+
+    def layer_block(*lead):
+        return pl.BlockSpec(tuple(lead) + (span, rows, cols), lambda b: (0,) * len(lead) + (b, 0, 0))
+
+    def next_layer(*lead):
+        return pl.BlockSpec(
+            tuple(lead) + (1, rows, cols),
+            lambda b: (0,) * len(lead) + (jnp.minimum((b + 1) * span, layers - 1), 0, 0),
+        )
+
+    def halo_block(mid, last):
+        return pl.BlockSpec((span, mid, last), lambda b: (b, 0, 0))
+
     reduced_residual, forward_products, adjoint_products = pl.pallas_call(
         stencil_kernel,
+        grid=(blocks,),
         out_shape=[
             jax.ShapeDtypeStruct((2,) + spatial, jnp.float32),
             jax.ShapeDtypeStruct((ndir, 2) + spatial, jnp.float32),
             jax.ShapeDtypeStruct((ndir, 2) + spatial, jnp.float32),
         ],
-        in_specs=[pl.BlockSpec(memory_space=pltpu.SMEM)] + [vmem] * 17,
-        out_specs=[vmem] * 3,
+        in_specs=[pl.BlockSpec(memory_space=pltpu.SMEM)]
+        + [layer_block()] * 10
+        + [layer_block(ndir, 2)] * 2
+        + [next_layer()] * 2
+        + [next_layer(ndir, 2)] * 2
+        + [
+            halo_block(rows, nf + 2),
+            halo_block(rows, nf),
+            halo_block(nf + 2, cols),
+            halo_block(nf, cols),
+            layer_block(1 + 2 * ndir, 2),
+        ],
+        out_specs=[layer_block(2), layer_block(ndir, 2), layer_block(ndir, 2)],
+        scratch_shapes=[pltpu.VMEM((nf, rows, cols), jnp.float32)],
+        compiler_params=pltpu.CompilerParams(dimension_semantics=("arbitrary",)),
         cost_estimate=pl.CostEstimate(
             flops=layers * rows * cols * 1200,
             transcendentals=0,
@@ -371,6 +415,10 @@
         upwind_z,
         directions,
         adjoint_weights,
+        pressure,
+        saturation,
+        directions,
+        adjoint_weights,
         hxl,
         hxr,
         hyd,

time: 53.1 us -> 52.3 us (0.985)
  Pallas kernels: 13.3 us -> 12.4 us
    pallas_call x1, Pallas kernels: 8.36 us -> 7.46 us  [body(): pl.pallas_call(stencil_kernel, grid=(blocks,), out_shape=[jax.ShapeDtypeS...]
where the time goes in v6:
time: 52.3 us; the launch traced here: 51.3 us
  starting transfers between devices  21.7 us (41%)
  Pallas kernels  12.4 us (24%)
  local copies, waits for them, and re-layouts  5.91 us (11%)
  matrix products  4.57 us (9%)
  other arithmetic  4.24 us (8%)
  waiting for transfers between devices  1.43 us (3%)
  between operations  1 us (2%)
    ppermute x4, starting transfers between devices, shift_along(): return lax.ppermute(block, axis, pairs)  11.2 us
    all_to_all x1, starting transfers between devices, gather_everywhere(): lax.all_to_all(jnp.broadcast_to(block[None], (peers,) + block.shape), GX_...  10.5 us
    pallas_call x1, Pallas kernels, body(): pl.pallas_call(stencil_kernel, grid=(blocks,), out_shape=[jax.ShapeDtypeS...  7.46 us
    pallas_call x1, Pallas kernels, body(): pl.pallas_call(pack_kernel, out_shape=[jax.ShapeDtypeStruct((layers, rows...  4.95 us
    unnamed x32, local copies, waits for them, and re-layouts  2.91 us
    dot_general x1, matrix products, body(): spread = jnp.dot(by_row, lane_hit.T, precision=lax.Precision.HIGHEST)  2.27 us
    dot_general x4, matrix products, at_perfs(): by_lane = jnp.dot(field, lane_hit, precision=lax.Precision.HIGHEST)  1.9 us
    ppermute x4, waiting for transfers between devices, shift_along(): return lax.ppermute(block, axis, pairs)  1.42 us
  transfers between devices with their start and end apart: 5, of which 1 were waited for; matrix products, arithmetic and copies ran while one was open for 13% of the time, Pallas kernels for 0%

profile of v6, /device:TPU:27, one launch (start us, length us, event | category | flops | bytes accessed | tf_op | source)
XLA Modules:
  0.0 51.3 jit_solution(13753996077874267544)
XLA Ops:
  0.7 0.8 %and_select_fusion.1 = (s32[32]{0:T(128)S(1)}, s32[32]{0:T(128)S(1)}) fusion(s32[32]{0:T(128)} %param.34), kind=kLoop, calls=%fused_computation.70 | loop fusion | flops 608 | bytes 384 | tf_op jit(solution)/shard_map/jit(remainder)/select_n | solution.py:306
  1.5 0.7 %fusion.43 = (f32[32]{0:T(128)S(1)}, f32[1,32]{1,0:T(1,128)S(1)}, s32[32]{0:T(128)S(1)}) fusion(s32[32]{0:T(128)} %param.33), kind=kLoop, calls=%fused_computation.88 | loop fusion | flops 128 | bytes 512 | tf_op jit(solution)/shard_map/convert_element_type | solution.py:341
  2.2 0.7 %gather_fusion = f32[32]{0:T(128)S(1)} fusion(f32[2048]{0:T(1024)S(1)} %copy-done, s32[1024]{0:T(1024)S(1)} %pad_clamp_fusion), kind=kCustom, calls=%fused_computation.clone | custom fusion | bytes 384 | tf_op jit(solution)/shard_map/jit(_take)/gather | solution.py:322
  2.9 0.7 %broadcast_select_fusion = f32[32]{0:T(128)S(1)} fusion(f32[32]{0:T(128)S(1)} %gather_fusion, s32[32]{0:T(128)} %param.33), kind=kLoop, calls=%fused_computation.78 | loop fusion | flops 224 | bytes 384 | tf_op jit(solution)/shard_map/jit(_take)/select_n | solution.py:322
  3.7 5.0 %shard_map.202 = (f32[24,8,20]{2,1,0:T(8,128)}, f32[24,8,18]{2,1,0:T(8,128)}, f32[24,20,128]{2,1,0:T(8,128)}, f32[24,18,128]{2,1,0:T(8,128)}) custom-call(f32[24,8,128]{2,1,0:T(8,128)} %pn_ref, f32[24,8,128]{2,1,0:T(8,128)} %sn_ref, f32[4,2,24,8,128]{4,3,2,1,0:T(8,128)} %dn_ref, f32[4,2,24,8,128]{4,3,2,1,0:T(8,128)} %wn_ref, f32[24,8,128]{2,1,0:T(8,128)} %tx_ref.3, ...), custom_call_target="tpu_custom_call" | custom-call | flops 3932160 | bytes 2162688 | tf_op jit(solution)/shard_map/pallas_call | solution.py:282
  9.2 0.7 %fusion.3 = f32[4,2,24,32]{3,2,1,0:T(8,128)S(1)} fusion(f32[4,2,24,8,128]{4,3,2,1,0:T(8,128)S(1)} %copy-done.3, f32[8,32]{1,0:T(8,128)S(1)} %fusion.32, s32[32]{0:T(128)S(1)} %get-tuple-element.60), kind=kOutput, calls=%fused_computation.7 | convolution fusion | flops 75593728 | bytes 812160 | tf_op jit(solution)/shard_map/dot_general | solution.py:310
  9.9 0.7 %fusion.2 = f32[4,2,24,32]{3,2,1,0:T(8,128)S(1)} fusion(f32[4,2,24,8,128]{4,3,2,1,0:T(8,128)S(1)} %copy-done.2, f32[8,32]{1,0:T(8,128)S(1)} %fusion.32, s32[32]{0:T(128)S(1)} %get-tuple-element.60), kind=kOutput, calls=%fused_computation.6 | convolution fusion | flops 75593728 | bytes 812160 | tf_op jit(solution)/shard_map/dot_general | solution.py:310
  11.0 1.1 %reshape.528 = f32[128,1,352]{2,1,0:T(1,128)} reshape(f32[128,11,32]{2,1,0:T(8,128)S(1)} %broadcast_in_dim.31) | data formatting | bytes 360448
  12.1 10.5 %all-to-all-start = ((f32[128,1,352]{2,1,0:T(1,128)}), f32[128,1,352]{2,1,0:T(1,128)S(1)}, u32[]{:S(2)}, u32[]{:S(2)}) async-start(f32[128,1,352]{2,1,0:T(1,128)} %reshape.528), calls=%async_computation | async-start | bytes 393216 | tf_op jit(solution)/shard_map/all_to_all | solution.py:21
  22.7 3.1 %collective-permute-start = (f32[24,8,20]{2,1,0:T(8,128)S(1)}, f32[24,8,20]{2,1,0:T(8,128)S(1)}, u32[]{:S(2)}, u32[]{:S(2)}) collective-permute-start(f32[24,8,20]{2,1,0:T(8,128)S(1)} %copy-done.13), channel_id=1, source_target_pairs={{0,32},{32,64},{64,96},{1,33},{33,65},{65,97},{2,34},{34,66},{66,9... | collective-permute-start | bytes 46088 | tf_op jit(solution)/shard_map/ppermute | solution.py:29
  25.8 2.2 %collective-permute-start.1 = (f32[24,8,18]{2,1,0:T(8,128)}, f32[24,8,18]{2,1,0:T(8,128)S(1)}, u32[]{:S(2)}, u32[]{:S(2)}) collective-permute-start(f32[24,8,18]{2,1,0:T(8,128)} %get-tuple-element.25), channel_id=1, source_target_pairs={{32,0},{64,32},{96,64},{33,1},{65,33},{97,65},{34,2},{66,34},{98,6... | collective-permute-start | bytes 41480 | tf_op jit(solution)/shard_map/ppermute | solution.py:29
  28.0 4.0 %collective-permute-start.2 = (f32[24,20,128]{2,1,0:T(8,128)}, f32[24,20,128]{2,1,0:T(8,128)S(1)}, u32[]{:S(2)}, u32[]{:S(2)}) collective-permute-start(f32[24,20,128]{2,1,0:T(8,128)} %get-tuple-element.26), channel_id=1, source_target_pairs={{0,1},{1,2},{2,3},{3,4},{4,5},{5,6},{6,7},{7,8},{8,9},{9,10},{10,1... | collective-permute-start | bytes 737288 | tf_op jit(solution)/shard_map/ppermute | solution.py:29
  32.0 1.9 %collective-permute-start.3 = (f32[24,18,128]{2,1,0:T(8,128)}, f32[24,18,128]{2,1,0:T(8,128)S(1)}, u32[]{:S(2)}, u32[]{:S(2)}) collective-permute-start(f32[24,18,128]{2,1,0:T(8,128)} %get-tuple-element.27), channel_id=1, source_target_pairs={{1,0},{2,1},{3,2},{4,3},{5,4},{6,5},{7,6},{8,7},{9,8},{10,9},{11,1... | collective-permute-start | bytes 663560 | tf_op jit(solution)/shard_map/ppermute | solution.py:29
  33.9 0.7 %gather_fusion.1 = f32[32]{0:T(128)S(1)} fusion(f32[2048]{0:T(1024)S(1)} %copy-done.1, s32[1024]{0:T(1024)S(1)} %pad_clamp_fusion), kind=kCustom, calls=%fused_computation.1.clone | custom fusion | bytes 384 | tf_op jit(solution)/shard_map/jit(_take)/gather | solution.py:349
  34.6 0.6 %add_convert_fusion.edge_ref = s32[2]{0:T(128)} fusion(pred[1]{0:T(512)(128)(4,1)} %bitcast.1, pred[1]{0:T(512)(128)(4,1)} %bitcast), kind=kLoop, calls=%fused_computation.67 | loop fusion | flops 4 | bytes 10 | tf_op jit(solution)/shard_map/convert_element_type | solution.py:278
  35.2 0.5 broadcast.527
  35.7 1.1 %reduce.6 = f32[128,352]{1,0:T(8,128)S(1)} reduce(f32[128,1,352]{2,1,0:T(1,128)S(1)} %all-to-all-done, f32[]{:T(128)} %broadcast.527), dimensions={1}, to_apply=%all_to_all.3.reduce_sub_computation | reduce | bytes 360452 | tf_op jit(solution)/shard_map/all_to_all | solution.py:21
  37.7 0.3 reshape.496
  38.1 0.4 fusion.8
  38.6 2.3 %fusion.spread_ref = f32[9,2,24,8,128]{4,3,2,1,0:T(8,128)} fusion(f32[8,32]{1,0:T(8,128)S(1)} %fusion.32, f32[9,2,24,32]{3,2,1,0:T(8,128)S(1)} %maximum_maximum_fusion, s32[32]{0:T(128)S(1)} %get-tuple-element.60), kind=kOutput, calls=%fused_computation.2 | convolution fusion | flops 169984000 | bytes 1825920 | tf_op jit(solution)/shard_map/dot_general | solution.py:359
  40.9 1.4 %collective-permute-done.3.hyu_ref = f32[24,18,128]{2,1,0:T(8,128)S(1)} collective-permute-done((f32[24,18,128]{2,1,0:T(8,128)}, f32[24,18,128]{2,1,0:T(8,128)S(1)}, u32[]{:S(2)}, u32[]{:S(2)}) %collective-permute-start.3) | collective-permute-done | bytes 221216 | tf_op jit(solution)/shard_map/ppermute | solution.py:29
  42.4 0.7 %copy-done.7 = f32[24,18,128]{2,1,0:T(8,128)} copy-done((f32[24,18,128]{2,1,0:T(8,128)}, f32[24,18,128]{2,1,0:T(8,128)S(1)}, u32[]{:S(2)}) %copy-start.7) | copy-done | bytes 221208
  43.1 0.7 %copy-done.6 = f32[24,20,128]{2,1,0:T(8,128)} copy-done((f32[24,20,128]{2,1,0:T(8,128)}, f32[24,20,128]{2,1,0:T(8,128)S(1)}, u32[]{:S(2)}) %copy-start.6) | copy-done | bytes 245784
  43.8 7.5 %shard_map.203 = (f32[2,24,8,128]{3,2,1,0:T(8,128)}, f32[4,2,24,8,128]{4,3,2,1,0:T(8,128)}, f32[4,2,24,8,128]{4,3,2,1,0:T(8,128)}) custom-call(s32[2]{0:T(128)} %add_convert_fusion.edge_ref, f32[24,8,128]{2,1,0:T(8,128)} %pn_ref, f32[24,8,128]{2,1,0:T(8,128)} %sn_ref, f32[24,8,128]{2,1,0:T(8,128)} %so_ref.1, f32[24,8,128]{2,1,0:T(8,128)} %pore_ref.1, ...), custom_call_target="tpu_custom_call" | custom-call | flops 29491200 | bytes 9043968 | tf_op jit(solution)/shard_map/pallas_call | solution.py:376
  (60 shorter events, 1.9 us)
Async XLA Ops:
  0.6 1.6 %copy-start = (f32[2048]{0:T(1024)S(1)}, f32[2048]{0:T(1024)}, u32[]{:S(2)}) copy-start(f32[2048]{0:T(1024)} %param.38) | copy-start | bytes 24580
  0.6 8.5 %copy-start.3 = (f32[4,2,24,8,128]{4,3,2,1,0:T(8,128)S(1)}, f32[4,2,24,8,128]{4,3,2,1,0:T(8,128)}, u32[]{:S(2)}) copy-start(f32[4,2,24,8,128]{4,3,2,1,0:T(8,128)} %wn_ref) | copy-start | bytes 2359300
  0.7 8.2 %copy-start.5 = (f32[24,8,128]{2,1,0:T(8,128)S(1)}, f32[24,8,128]{2,1,0:T(8,128)}, u32[]{:S(2)}) copy-start(f32[24,8,128]{2,1,0:T(8,128)} %sn_ref) | copy-start | bytes 294916
  0.7 7.9 %copy-start.4 = (f32[24,8,128]{2,1,0:T(8,128)S(1)}, f32[24,8,128]{2,1,0:T(8,128)}, u32[]{:S(2)}) copy-start(f32[24,8,128]{2,1,0:T(8,128)} %pn_ref) | copy-start | bytes 294916
  2.9 7.0 %copy-start.2 = (f32[4,2,24,8,128]{4,3,2,1,0:T(8,128)S(1)}, f32[4,2,24,8,128]{4,3,2,1,0:T(8,128)}, u32[]{:S(2)}) copy-start(f32[4,2,24,8,128]{4,3,2,1,0:T(8,128)} %dn_ref) | copy-start | bytes 2359300
  3.6 6.9 %copy-start.11 = (s32[32]{0:T(128)S(1)}, s32[32]{0:T(128)}, u32[]{:S(2)}) copy-start(s32[32]{0:T(128)} %param.35) | copy-start | bytes 388
  3.6 7.0 %copy-start.14 = (s32[32]{0:T(128)S(1)}, s32[32]{0:T(128)}, u32[]{:S(2)}) copy-start(s32[32]{0:T(128)} %param.36) | copy-start | bytes 388
  3.6 7.0 %copy-start.10 = (f32[32]{0:T(128)S(1)}, f32[32]{0:T(128)}, u32[]{:S(2)}) copy-start(f32[32]{0:T(128)} %param.37) | copy-start | bytes 388
  10.6 12.0 %copy-start.13 = (f32[24,8,20]{2,1,0:T(8,128)S(1)}, f32[24,8,20]{2,1,0:T(8,128)}, u32[]{:S(2)}) copy-start(f32[24,8,20]{2,1,0:T(8,128)} %get-tuple-element.24) | copy-start | bytes 46084
  10.7 23.2 %copy-start.1 = (f32[2048]{0:T(1024)S(1)}, f32[2048]{0:T(1024)}, u32[]{:S(2)}) copy-start(f32[2048]{0:T(1024)} %param.39) | copy-start | bytes 24580
  12.1 23.1 %all-to-all-start = ((f32[128,1,352]{2,1,0:T(1,128)}), f32[128,1,352]{2,1,0:T(1,128)S(1)}, u32[]{:S(2)}, u32[]{:S(2)}) async-start(f32[128,1,352]{2,1,0:T(1,128)} %reshape.528), calls=%async_computation | async-start | bytes 393216 | tf_op jit(solution)/shard_map/all_to_all | solution.py:21
  22.7 18.2 %collective-permute-start = (f32[24,8,20]{2,1,0:T(8,128)S(1)}, f32[24,8,20]{2,1,0:T(8,128)S(1)}, u32[]{:S(2)}, u32[]{:S(2)}) collective-permute-start(f32[24,8,20]{2,1,0:T(8,128)S(1)} %copy-done.13), channel_id=1, source_target_pairs={{0,32},{32,64},{64,96},{1,33},{33,65},{65,97},{2,34},{34,66},{66,9... | collective-permute-start | bytes 46088 | tf_op jit(solution)/shard_map/ppermute | solution.py:29
  25.8 15.1 %collective-permute-start.1 = (f32[24,8,18]{2,1,0:T(8,128)}, f32[24,8,18]{2,1,0:T(8,128)S(1)}, u32[]{:S(2)}, u32[]{:S(2)}) collective-permute-start(f32[24,8,18]{2,1,0:T(8,128)} %get-tuple-element.25), channel_id=1, source_target_pairs={{32,0},{64,32},{96,64},{33,1},{65,33},{97,65},{34,2},{66,34},{98,6... | collective-permute-start | bytes 41480 | tf_op jit(solution)/shard_map/ppermute | solution.py:29
  28.0 14.4 %collective-permute-start.2 = (f32[24,20,128]{2,1,0:T(8,128)}, f32[24,20,128]{2,1,0:T(8,128)S(1)}, u32[]{:S(2)}, u32[]{:S(2)}) collective-permute-start(f32[24,20,128]{2,1,0:T(8,128)} %get-tuple-element.26), channel_id=1, source_target_pairs={{0,1},{1,2},{2,3},{3,4},{4,5},{5,6},{6,7},{7,8},{8,9},{9,10},{10,1... | collective-permute-start | bytes 737288 | tf_op jit(solution)/shard_map/ppermute | solution.py:29
  32.0 10.4 %collective-permute-start.3 = (f32[24,18,128]{2,1,0:T(8,128)}, f32[24,18,128]{2,1,0:T(8,128)S(1)}, u32[]{:S(2)}, u32[]{:S(2)}) collective-permute-start(f32[24,18,128]{2,1,0:T(8,128)} %get-tuple-element.27), channel_id=1, source_target_pairs={{1,0},{2,1},{3,2},{4,3},{5,4},{6,5},{7,6},{8,7},{9,8},{10,9},{11,1... | collective-permute-start | bytes 663560 | tf_op jit(solution)/shard_map/ppermute | solution.py:29
  37.4 1.0 %copy-start.12 = (s32[32]{0:T(128)S(1)}, s32[32]{0:T(128)}, u32[]{:S(2)}) copy-start(s32[32]{0:T(128)} %param.33) | copy-start | bytes 388
  40.9 1.4 %copy-start.9 = (f32[24,8,18]{2,1,0:T(8,128)}, f32[24,8,18]{2,1,0:T(8,128)S(1)}, u32[]{:S(2)}) copy-start(f32[24,8,18]{2,1,0:T(8,128)S(1)} %collective-permute-done.1.hxr_ref) | copy-start | bytes 41476
  40.9 1.4 %copy-start.8 = (f32[24,8,20]{2,1,0:T(8,128)}, f32[24,8,20]{2,1,0:T(8,128)S(1)}, u32[]{:S(2)}) copy-start(f32[24,8,20]{2,1,0:T(8,128)S(1)} %collective-permute-done.hxl_ref) | copy-start | bytes 46084
  42.3 0.8 %copy-start.7 = (f32[24,18,128]{2,1,0:T(8,128)}, f32[24,18,128]{2,1,0:T(8,128)S(1)}, u32[]{:S(2)}) copy-start(f32[24,18,128]{2,1,0:T(8,128)S(1)} %collective-permute-done.3.hyu_ref) | copy-start | bytes 663556
  43.1 0.7 %copy-start.6 = (f32[24,20,128]{2,1,0:T(8,128)}, f32[24,20,128]{2,1,0:T(8,128)S(1)}, u32[]{:S(2)}) copy-start(f32[24,20,128]{2,1,0:T(8,128)S(1)} %collective-permute-done.2.hyd_ref) | copy-start | bytes 737284

commit v7 on v6

--- a/solution.py
+++ b/solution.py
@@ -18,7 +18,8 @@
 
 def gather_everywhere(block):
     peers = lax.axis_size(GX_GY_WA)
-    return lax.all_to_all(jnp.broadcast_to(block[None], (peers,) + block.shape), GX_GY_WA, 0, 0)
+    flat = jnp.broadcast_to(block.reshape(1, -1), (peers, block.size))
+    return lax.all_to_all(flat, GX_GY_WA, 0, 0, tiled=True).reshape((peers,) + block.shape)
 
 
 def shift_along(block, axis, down):

time: 52.3 us -> 51.2 us (0.979); the launches traced: 51.3 us -> 50.8 us
  waiting for transfers between devices: 1.43 us -> 3.07 us
  local copies, waits for them, and re-layouts: 5.91 us -> 4.77 us
  other arithmetic: 4.24 us -> 3.16 us
    ppermute x4, waiting for transfers between devices: 1.42 us -> 3.07 us  [shift_along(): return lax.ppermute(block, axis, pairs)]
    unnamed x32 -> x36, local copies, waits for them, and re-layouts: 2.91 us -> 1.49 us
    all_to_all x1 -> x0, other arithmetic: 1.12 us -> none  [gather_everywhere(): lax.all_to_all(jnp.broadcast_to(block[None], (peers,) + block.shape), GX_...]
    broadcast_in_dim x1 -> x2, local copies, waits for them, and re-layouts: 0.07 us -> 0.86 us  [gather_everywhere(): flat = jnp.broadcast_to(block.reshape(1, -1), (peers, block.size))]
  transfers between devices with their start and end apart: 5 -> 5, of which waited for: 1 -> 1; matrix products, arithmetic and copies ran while one was open for 13% -> 10% of each run, Pallas kernels for 0% -> 0%
where the time goes in v7:
time: 51.2 us; the launch traced here: 50.8 us
  starting transfers between devices  21.7 us (42%)
  Pallas kernels  12.4 us (24%)
  local copies, waits for them, and re-layouts  4.77 us (9%)
  matrix products  4.55 us (9%)
  other arithmetic  3.16 us (6%)
  waiting for transfers between devices  3.07 us (6%)
  between operations  1.05 us (2%)
    ppermute x4, starting transfers between devices, shift_along(): return lax.ppermute(block, axis, pairs)  11.2 us
    all_to_all x1, starting transfers between devices, gather_everywhere(): lax.all_to_all(flat, GX_GY_WA, 0, 0, tiled=True)  10.5 us
    pallas_call x1, Pallas kernels, body(): pl.pallas_call(stencil_kernel, grid=(blocks,), out_shape=[jax.ShapeDtypeS...  7.46 us
    pallas_call x1, Pallas kernels, body(): pl.pallas_call(pack_kernel, out_shape=[jax.ShapeDtypeStruct((layers, rows...  4.95 us
    ppermute x4, waiting for transfers between devices, shift_along(): return lax.ppermute(block, axis, pairs)  3.07 us
    dot_general x1, matrix products, body(): spread = jnp.dot(by_row, lane_hit.T, precision=lax.Precision.HIGHEST)  2.26 us
    dot_general x4, matrix products, at_perfs(): by_lane = jnp.dot(field, lane_hit, precision=lax.Precision.HIGHEST)  1.88 us
    unnamed x36, local copies, waits for them, and re-layouts  1.49 us
  transfers between devices with their start and end apart: 5, of which 1 were waited for; matrix products, arithmetic and copies ran while one was open for 10% of the time, Pallas kernels for 0%

profile of v7, /device:TPU:27, one launch (start us, length us, event | category | flops | bytes accessed | tf_op | source)
XLA Modules:
  0.0 50.8 jit_solution(13863749822891792317)
XLA Ops:
  0.7 0.8 %and_select_fusion.1 = (s32[32]{0:T(128)S(1)}, s32[32]{0:T(128)S(1)}) fusion(s32[32]{0:T(128)} %param.34), kind=kLoop, calls=%fused_computation.69 | loop fusion | flops 608 | bytes 384 | tf_op jit(solution)/shard_map/jit(remainder)/select_n | solution.py:307
  1.5 0.7 %fusion.43 = (f32[32]{0:T(128)S(1)}, f32[1,32]{1,0:T(1,128)S(1)}, s32[32]{0:T(128)S(1)}) fusion(s32[32]{0:T(128)} %param.33), kind=kLoop, calls=%fused_computation.87 | loop fusion | flops 128 | bytes 512 | tf_op jit(solution)/shard_map/convert_element_type | solution.py:342
  2.2 0.7 %gather_fusion = f32[32]{0:T(128)S(1)} fusion(f32[2048]{0:T(1024)S(1)} %copy-done, s32[1024]{0:T(1024)S(1)} %pad_clamp_fusion), kind=kCustom, calls=%fused_computation.clone | custom fusion | bytes 384 | tf_op jit(solution)/shard_map/jit(_take)/gather | solution.py:323
  2.9 0.7 %broadcast_select_fusion = f32[32]{0:T(128)S(1)} fusion(f32[32]{0:T(128)S(1)} %gather_fusion, s32[32]{0:T(128)} %param.33), kind=kLoop, calls=%fused_computation.77 | loop fusion | flops 224 | bytes 384 | tf_op jit(solution)/shard_map/jit(_take)/select_n | solution.py:323
  3.7 5.0 %shard_map.202 = (f32[24,8,20]{2,1,0:T(8,128)}, f32[24,8,18]{2,1,0:T(8,128)}, f32[24,20,128]{2,1,0:T(8,128)}, f32[24,18,128]{2,1,0:T(8,128)}) custom-call(f32[24,8,128]{2,1,0:T(8,128)} %pn_ref, f32[24,8,128]{2,1,0:T(8,128)} %sn_ref, f32[4,2,24,8,128]{4,3,2,1,0:T(8,128)} %dn_ref, f32[4,2,24,8,128]{4,3,2,1,0:T(8,128)} %wn_ref, f32[24,8,128]{2,1,0:T(8,128)} %tx_ref.3, ...), custom_call_target="tpu_custom_call" | custom-call | flops 3932160 | bytes 2162688 | tf_op jit(solution)/shard_map/pallas_call | solution.py:283
  8.6 0.3 fusion.5
  8.9 0.3 fusion.4
  9.2 0.7 %fusion.3 = f32[4,2,24,32]{3,2,1,0:T(8,128)S(1)} fusion(f32[4,2,24,8,128]{4,3,2,1,0:T(8,128)S(1)} %copy-done.3, f32[8,32]{1,0:T(8,128)S(1)} %fusion.32, s32[32]{0:T(128)S(1)} %get-tuple-element.60), kind=kOutput, calls=%fused_computation.7 | convolution fusion | flops 75593728 | bytes 812160 | tf_op jit(solution)/shard_map/dot_general | solution.py:311
  9.9 0.7 %fusion.2 = f32[4,2,24,32]{3,2,1,0:T(8,128)S(1)} fusion(f32[4,2,24,8,128]{4,3,2,1,0:T(8,128)S(1)} %copy-done.2, f32[8,32]{1,0:T(8,128)S(1)} %fusion.32, s32[32]{0:T(128)S(1)} %get-tuple-element.60), kind=kOutput, calls=%fused_computation.6 | convolution fusion | flops 75593728 | bytes 812160 | tf_op jit(solution)/shard_map/dot_general | solution.py:311
  11.0 0.8 %broadcast_in_dim.34 = f32[128,1,352]{2,1,0:T(1,128)} broadcast(f32[352]{0:T(512)S(1)} %broadcast_in_dim.33), dimensions={2} | broadcast | bytes 181632 | tf_op jit(solution)/shard_map/broadcast_in_dim | solution.py:21
  11.8 10.5 %all-to-all-start = ((f32[128,1,352]{2,1,0:T(1,128)}), f32[128,1,352]{2,1,0:T(1,128)S(1)}, u32[]{:S(2)}, u32[]{:S(2)}) async-start(f32[128,1,352]{2,1,0:T(1,128)} %broadcast_in_dim.34), calls=%async_computation | async-start | bytes 393216 | tf_op jit(solution)/shard_map/all_to_all | solution.py:22
  22.4 3.1 %collective-permute-start = (f32[24,8,20]{2,1,0:T(8,128)S(1)}, f32[24,8,20]{2,1,0:T(8,128)S(1)}, u32[]{:S(2)}, u32[]{:S(2)}) collective-permute-start(f32[24,8,20]{2,1,0:T(8,128)S(1)} %copy-done.15), channel_id=1, source_target_pairs={{0,32},{32,64},{64,96},{1,33},{33,65},{65,97},{2,34},{34,66},{66,9... | collective-permute-start | bytes 46088 | tf_op jit(solution)/shard_map/ppermute | solution.py:30
  25.5 2.2 %collective-permute-start.1 = (f32[24,8,18]{2,1,0:T(8,128)S(1)}, f32[24,8,18]{2,1,0:T(8,128)S(1)}, u32[]{:S(2)}, u32[]{:S(2)}) collective-permute-start(f32[24,8,18]{2,1,0:T(8,128)S(1)} %copy-done.16), channel_id=1, source_target_pairs={{32,0},{64,32},{96,64},{33,1},{65,33},{97,65},{34,2},{66,34},{98,6... | collective-permute-start | bytes 41480 | tf_op jit(solution)/shard_map/ppermute | solution.py:30
  27.7 4.0 %collective-permute-start.2 = (f32[24,20,128]{2,1,0:T(8,128)S(1)}, f32[24,20,128]{2,1,0:T(8,128)S(1)}, u32[]{:S(2)}, u32[]{:S(2)}) collective-permute-start(f32[24,20,128]{2,1,0:T(8,128)S(1)} %copy-done.13), channel_id=1, source_target_pairs={{0,1},{1,2},{2,3},{3,4},{4,5},{5,6},{6,7},{7,8},{8,9},{9,10},{10,1... | collective-permute-start | bytes 737288 | tf_op jit(solution)/shard_map/ppermute | solution.py:30
  31.7 1.9 %collective-permute-start.3 = (f32[24,18,128]{2,1,0:T(8,128)S(1)}, f32[24,18,128]{2,1,0:T(8,128)S(1)}, u32[]{:S(2)}, u32[]{:S(2)}) collective-permute-start(f32[24,18,128]{2,1,0:T(8,128)S(1)} %copy-done.14), channel_id=1, source_target_pairs={{1,0},{2,1},{3,2},{4,3},{5,4},{6,5},{7,6},{8,7},{9,8},{10,9},{11,1... | collective-permute-start | bytes 663560 | tf_op jit(solution)/shard_map/ppermute | solution.py:30
  33.7 0.7 %gather_fusion.1 = f32[32]{0:T(128)S(1)} fusion(f32[2048]{0:T(1024)S(1)} %copy-done.1, s32[1024]{0:T(1024)S(1)} %pad_clamp_fusion), kind=kCustom, calls=%fused_computation.1.clone | custom fusion | bytes 384 | tf_op jit(solution)/shard_map/jit(_take)/gather | solution.py:350
  34.4 0.7 %add_convert_fusion.edge_ref = s32[2]{0:T(128)} fusion(pred[1]{0:T(512)(128)(4,1)} %bitcast.1, pred[1]{0:T(512)(128)(4,1)} %bitcast), kind=kLoop, calls=%fused_computation.66 | loop fusion | flops 4 | bytes 10 | tf_op jit(solution)/shard_map/convert_element_type | solution.py:279
  35.6 0.3 reshape.509
  36.0 0.4 fusion.8
  36.5 2.3 %fusion.spread_ref = f32[9,2,24,8,128]{4,3,2,1,0:T(8,128)} fusion(f32[8,32]{1,0:T(8,128)S(1)} %fusion.32, f32[9,2,24,32]{3,2,1,0:T(8,128)S(1)} %maximum_maximum_fusion, s32[32]{0:T(128)S(1)} %get-tuple-element.60), kind=kOutput, calls=%fused_computation.2 | convolution fusion | flops 169984000 | bytes 1825920 | tf_op jit(solution)/shard_map/dot_general | solution.py:360
  38.8 3.1 %collective-permute-done.3.hyu_ref = f32[24,18,128]{2,1,0:T(8,128)S(1)} collective-permute-done((f32[24,18,128]{2,1,0:T(8,128)S(1)}, f32[24,18,128]{2,1,0:T(8,128)S(1)}, u32[]{:S(2)}, u32[]{:S(2)}) %collective-permute-start.3) | collective-permute-done | bytes 221216 | tf_op jit(solution)/shard_map/ppermute | solution.py:30
  41.9 0.7 %copy-done.7 = f32[24,18,128]{2,1,0:T(8,128)} copy-done((f32[24,18,128]{2,1,0:T(8,128)}, f32[24,18,128]{2,1,0:T(8,128)S(1)}, u32[]{:S(2)}) %copy-start.7) | copy-done | bytes 221208
  42.6 0.7 %copy-done.6 = f32[24,20,128]{2,1,0:T(8,128)} copy-done((f32[24,20,128]{2,1,0:T(8,128)}, f32[24,20,128]{2,1,0:T(8,128)S(1)}, u32[]{:S(2)}) %copy-start.6) | copy-done | bytes 245784
  43.3 7.5 %shard_map.203 = (f32[2,24,8,128]{3,2,1,0:T(8,128)}, f32[4,2,24,8,128]{4,3,2,1,0:T(8,128)}, f32[4,2,24,8,128]{4,3,2,1,0:T(8,128)}) custom-call(s32[2]{0:T(128)} %add_convert_fusion.edge_ref, f32[24,8,128]{2,1,0:T(8,128)} %pn_ref, f32[24,8,128]{2,1,0:T(8,128)} %sn_ref, f32[24,8,128]{2,1,0:T(8,128)} %so_ref.1, f32[24,8,128]{2,1,0:T(8,128)} %pore_ref.1, ...), custom_call_target="tpu_custom_call" | custom-call | flops 29491200 | bytes 9043968 | tf_op jit(solution)/shard_map/pallas_call | solution.py:377
  (65 shorter events, 1.2 us)
Async XLA Ops:
  0.6 1.6 %copy-start = (f32[2048]{0:T(1024)S(1)}, f32[2048]{0:T(1024)}, u32[]{:S(2)}) copy-start(f32[2048]{0:T(1024)} %param.38) | copy-start | bytes 24580
  0.6 8.5 %copy-start.3 = (f32[4,2,24,8,128]{4,3,2,1,0:T(8,128)S(1)}, f32[4,2,24,8,128]{4,3,2,1,0:T(8,128)}, u32[]{:S(2)}) copy-start(f32[4,2,24,8,128]{4,3,2,1,0:T(8,128)} %wn_ref) | copy-start | bytes 2359300
  0.7 8.2 %copy-start.5 = (f32[24,8,128]{2,1,0:T(8,128)S(1)}, f32[24,8,128]{2,1,0:T(8,128)}, u32[]{:S(2)}) copy-start(f32[24,8,128]{2,1,0:T(8,128)} %sn_ref) | copy-start | bytes 294916
  0.7 7.9 %copy-start.4 = (f32[24,8,128]{2,1,0:T(8,128)S(1)}, f32[24,8,128]{2,1,0:T(8,128)}, u32[]{:S(2)}) copy-start(f32[24,8,128]{2,1,0:T(8,128)} %pn_ref) | copy-start | bytes 294916
  2.9 7.0 %copy-start.2 = (f32[4,2,24,8,128]{4,3,2,1,0:T(8,128)S(1)}, f32[4,2,24,8,128]{4,3,2,1,0:T(8,128)}, u32[]{:S(2)}) copy-start(f32[4,2,24,8,128]{4,3,2,1,0:T(8,128)} %dn_ref) | copy-start | bytes 2359300
  3.6 7.0 %copy-start.11 = (s32[32]{0:T(128)S(1)}, s32[32]{0:T(128)}, u32[]{:S(2)}) copy-start(s32[32]{0:T(128)} %param.35) | copy-start | bytes 388
  3.6 7.0 %copy-start.17 = (s32[32]{0:T(128)S(1)}, s32[32]{0:T(128)}, u32[]{:S(2)}) copy-start(s32[32]{0:T(128)} %param.36) | copy-start | bytes 388
  3.6 7.0 %copy-start.10 = (f32[32]{0:T(128)S(1)}, f32[32]{0:T(128)}, u32[]{:S(2)}) copy-start(f32[32]{0:T(128)} %param.37) | copy-start | bytes 388
  9.2 13.2 %copy-start.15 = (f32[24,8,20]{2,1,0:T(8,128)S(1)}, f32[24,8,20]{2,1,0:T(8,128)}, u32[]{:S(2)}) copy-start(f32[24,8,20]{2,1,0:T(8,128)} %get-tuple-element.24) | copy-start | bytes 46084
  9.2 16.3 %copy-start.16 = (f32[24,8,18]{2,1,0:T(8,128)S(1)}, f32[24,8,18]{2,1,0:T(8,128)}, u32[]{:S(2)}) copy-start(f32[24,8,18]{2,1,0:T(8,128)} %get-tuple-element.25) | copy-start | bytes 41476
  9.2 18.5 %copy-start.13 = (f32[24,20,128]{2,1,0:T(8,128)S(1)}, f32[24,20,128]{2,1,0:T(8,128)}, u32[]{:S(2)}) copy-start(f32[24,20,128]{2,1,0:T(8,128)} %get-tuple-element.26) | copy-start | bytes 737284
  9.2 22.5 %copy-start.14 = (f32[24,18,128]{2,1,0:T(8,128)S(1)}, f32[24,18,128]{2,1,0:T(8,128)}, u32[]{:S(2)}) copy-start(f32[24,18,128]{2,1,0:T(8,128)} %get-tuple-element.27) | copy-start | bytes 663556
  9.2 24.4 %copy-start.1 = (f32[2048]{0:T(1024)S(1)}, f32[2048]{0:T(1024)}, u32[]{:S(2)}) copy-start(f32[2048]{0:T(1024)} %param.39) | copy-start | bytes 24580
  11.8 23.2 %all-to-all-start = ((f32[128,1,352]{2,1,0:T(1,128)}), f32[128,1,352]{2,1,0:T(1,128)S(1)}, u32[]{:S(2)}, u32[]{:S(2)}) async-start(f32[128,1,352]{2,1,0:T(1,128)} %broadcast_in_dim.34), calls=%async_computation | async-start | bytes 393216 | tf_op jit(solution)/shard_map/all_to_all | solution.py:22
  22.4 14.0 %copy-start.12 = (s32[32]{0:T(128)S(1)}, s32[32]{0:T(128)}, u32[]{:S(2)}) copy-start(s32[32]{0:T(128)} %param.33) | copy-start | bytes 388
  22.4 16.4 %collective-permute-start = (f32[24,8,20]{2,1,0:T(8,128)S(1)}, f32[24,8,20]{2,1,0:T(8,128)S(1)}, u32[]{:S(2)}, u32[]{:S(2)}) collective-permute-start(f32[24,8,20]{2,1,0:T(8,128)S(1)} %copy-done.15), channel_id=1, source_target_pairs={{0,32},{32,64},{64,96},{1,33},{33,65},{65,97},{2,34},{34,66},{66,9... | collective-permute-start | bytes 46088 | tf_op jit(solution)/shard_map/ppermute | solution.py:30
  25.5 13.3 %collective-permute-start.1 = (f32[24,8,18]{2,1,0:T(8,128)S(1)}, f32[24,8,18]{2,1,0:T(8,128)S(1)}, u32[]{:S(2)}, u32[]{:S(2)}) collective-permute-start(f32[24,8,18]{2,1,0:T(8,128)S(1)} %copy-done.16), channel_id=1, source_target_pairs={{32,0},{64,32},{96,64},{33,1},{65,33},{97,65},{34,2},{66,34},{98,6... | collective-permute-start | bytes 41480 | tf_op jit(solution)/shard_map/ppermute | solution.py:30
  27.7 14.2 %collective-permute-start.2 = (f32[24,20,128]{2,1,0:T(8,128)S(1)}, f32[24,20,128]{2,1,0:T(8,128)S(1)}, u32[]{:S(2)}, u32[]{:S(2)}) collective-permute-start(f32[24,20,128]{2,1,0:T(8,128)S(1)} %copy-done.13), channel_id=1, source_target_pairs={{0,1},{1,2},{2,3},{3,4},{4,5},{5,6},{6,7},{7,8},{8,9},{9,10},{10,1... | collective-permute-start | bytes 737288 | tf_op jit(solution)/shard_map/ppermute | solution.py:30
  31.7 10.2 %collective-permute-start.3 = (f32[24,18,128]{2,1,0:T(8,128)S(1)}, f32[24,18,128]{2,1,0:T(8,128)S(1)}, u32[]{:S(2)}, u32[]{:S(2)}) collective-permute-start(f32[24,18,128]{2,1,0:T(8,128)S(1)} %copy-done.14), channel_id=1, source_target_pairs={{1,0},{2,1},{3,2},{4,3},{5,4},{6,5},{7,6},{8,7},{9,8},{10,9},{11,1... | collective-permute-start | bytes 663560 | tf_op jit(solution)/shard_map/ppermute | solution.py:30
  38.8 3.1 %copy-start.9 = (f32[24,8,18]{2,1,0:T(8,128)}, f32[24,8,18]{2,1,0:T(8,128)S(1)}, u32[]{:S(2)}) copy-start(f32[24,8,18]{2,1,0:T(8,128)S(1)} %collective-permute-done.1.hxr_ref) | copy-start | bytes 41476
  38.8 3.1 %copy-start.8 = (f32[24,8,20]{2,1,0:T(8,128)}, f32[24,8,20]{2,1,0:T(8,128)S(1)}, u32[]{:S(2)}) copy-start(f32[24,8,20]{2,1,0:T(8,128)S(1)} %collective-permute-done.hxl_ref) | copy-start | bytes 46084
  41.9 0.7 %copy-start.7 = (f32[24,18,128]{2,1,0:T(8,128)}, f32[24,18,128]{2,1,0:T(8,128)S(1)}, u32[]{:S(2)}) copy-start(f32[24,18,128]{2,1,0:T(8,128)S(1)} %collective-permute-done.3.hyu_ref) | copy-start | bytes 663556
  42.6 0.7 %copy-start.6 = (f32[24,20,128]{2,1,0:T(8,128)}, f32[24,20,128]{2,1,0:T(8,128)S(1)}, u32[]{:S(2)}) copy-start(f32[24,20,128]{2,1,0:T(8,128)S(1)} %collective-permute-done.2.hyd_ref) | copy-start | bytes 737284

commit v8 on v7

--- a/solution.py
+++ b/solution.py
@@ -116,7 +116,6 @@
 
 
 def stencil_kernel(
-    edge_ref,
     p_ref,
     s_ref,
     so_ref,
@@ -153,8 +152,10 @@
     last_lane = lane == cols - 1
     first_sub = sub == 0
     last_sub = sub == rows - 1
-    cut_x = jnp.logical_and(last_lane, edge_ref[0] == 1)
-    cut_y = jnp.logical_and(last_sub, edge_ref[1] == 1)
+    last_x = lax.axis_index("gx") == lax.axis_size("gx") - 1
+    last_y = lax.axis_index(GY_WA) == lax.axis_size(GY_WA) - 1
+    cut_x = jnp.logical_and(last_lane, last_x)
+    cut_y = jnp.logical_and(last_sub, last_y)
     nf = 2 + 4 * ndir
 
     def cells_of(pr, sr, dr, wr, k):
@@ -274,9 +275,6 @@
     layers, rows, cols = pressure.shape
     spatial = (layers, rows, cols)
     ndir = directions.shape[0]
-    last_x = lax.axis_index("gx") == lax.axis_size("gx") - 1
-    last_y = lax.axis_index(GY_WA) == lax.axis_size(GY_WA) - 1
-    edge = jnp.stack([last_x, last_y]).astype(jnp.int32)
 
     nf = 2 + 4 * ndir
     vmem = pl.BlockSpec(memory_space=pltpu.VMEM)
@@ -320,7 +318,7 @@
         depth >= perf_top[None, :], depth < (perf_top + perf_span)[None, :]
     )
     weight = jnp.where(open_layer, perf_index[None, :], 0.0)
-    row_bhp = jnp.take(bhp, perf_well)
+    row_bhp, row_target = jnp.take(jnp.stack([bhp, target]), perf_well, axis=1)
     drive = p_cells - row_bhp
     mob = mobility(s_cells)
     slope = mobility_slope(s_cells)
@@ -347,7 +345,6 @@
     all_wells = everyone[:, -1].reshape(-1)
     same_well = (perf_well.astype(jnp.float32)[:, None] == all_wells[None, :]).astype(jnp.float32)
     row_totals = jnp.dot(all_sums, same_well.T, precision=lax.Precision.HIGHEST)
-    row_target = jnp.take(target, perf_well)
     row_factors = well_factors(row_totals, row_target)
     wells_res = rates - weight * mob * row_factors[0]
     wells_fwd = rate_tangent - (weight * mob)[None] * row_factors[1 : 1 + ndir][:, None, None, :]
@@ -382,8 +379,7 @@
             jax.ShapeDtypeStruct((ndir, 2) + spatial, jnp.float32),
             jax.ShapeDtypeStruct((ndir, 2) + spatial, jnp.float32),
         ],
-        in_specs=[pl.BlockSpec(memory_space=pltpu.SMEM)]
-        + [layer_block()] * 10
+        in_specs=[layer_block()] * 10
         + [layer_block(ndir, 2)] * 2
         + [next_layer()] * 2
         + [next_layer(ndir, 2)] * 2
@@ -403,7 +399,6 @@
             bytes_accessed=(10 + 4 * 4 * ndir + 2 + 2 * 2 * ndir) * layers * rows * cols * 4,
         ),
     )(
-        edge,
         pressure,
         saturation,
         sat_old,

time: 51.2 us -> 51.5 us (level)
  waiting for transfers between devices: 3.07 us -> 4.43 us
  other arithmetic: 3.16 us -> 2.52 us
    ppermute x4, waiting for transfers between devices: 3.07 us -> 4.43 us  [shift_along(): return lax.ppermute(block, axis, pairs)]
    and x0 -> x1, other arithmetic: none -> 0.81 us  [body(): row_bhp, row_target = jnp.take(jnp.stack([bhp, target]), perf_well, axis=1)]
    gather x2, local copies, waits for them, and re-layouts: 1.4 us -> 0.66 us  [body(): row_bhp, row_target = jnp.take(jnp.stack([bhp, target]), perf_well, axis=1)]
    select_n x1, other arithmetic: 0.73 us -> 0.01 us  [body(): row_bhp, row_target = jnp.take(jnp.stack([bhp, target]), perf_well, axis=1)]
    convert_element_type x1 -> x0, other arithmetic: 0.65 us -> none  [body(): edge = jnp.stack([last_x, last_y]).astype(jnp.int32)]
    unnamed x36 -> x34, local copies, waits for them, and re-layouts: 1.49 us -> 1.49 us
  transfers between devices with their start and end apart: 5 -> 5, of which waited for: 1 -> 1; matrix products, arithmetic and copies ran while one was open for 10% -> 7% of each run, Pallas kernels for 0% -> 0%
where the time goes in v8:
time: 51.5 us; the launch traced here: 51.1 us
  starting transfers between devices  21.7 us (42%)
  Pallas kernels  12.4 us (24%)
  matrix products  4.56 us (9%)
  waiting for transfers between devices  4.43 us (9%)
  local copies, waits for them, and re-layouts  4.41 us (9%)
  other arithmetic  2.52 us (5%)
  between operations  1.07 us (2%)
    ppermute x4, starting transfers between devices, shift_along(): return lax.ppermute(block, axis, pairs)  11.2 us
    all_to_all x1, starting transfers between devices, gather_everywhere(): lax.all_to_all(flat, GX_GY_WA, 0, 0, tiled=True)  10.5 us
    pallas_call x1, Pallas kernels, body(): pl.pallas_call(stencil_kernel, grid=(blocks,), out_shape=[jax.ShapeDtypeS...  7.44 us
    pallas_call x1, Pallas kernels, body(): pl.pallas_call(pack_kernel, out_shape=[jax.ShapeDtypeStruct((layers, rows...  4.93 us
    ppermute x4, waiting for transfers between devices, shift_along(): return lax.ppermute(block, axis, pairs)  4.43 us
    dot_general x1, matrix products, body(): spread = jnp.dot(by_row, lane_hit.T, precision=lax.Precision.HIGHEST)  2.27 us
    dot_general x4, matrix products, at_perfs(): by_lane = jnp.dot(field, lane_hit, precision=lax.Precision.HIGHEST)  1.88 us
    unnamed x34, local copies, waits for them, and re-layouts  1.49 us
  transfers between devices with their start and end apart: 5, of which 1 were waited for; matrix products, arithmetic and copies ran while one was open for 7% of the time, Pallas kernels for 0%

profile of v8, /device:TPU:27, one launch (start us, length us, event | category | flops | bytes accessed | tf_op | source)
XLA Modules:
  0.0 51.1 jit_solution(8192095638420830844)
XLA Ops:
  0.7 0.8 %compare_and_fusion = pred[32]{0:T(512)(128)(4,1)S(1)} fusion(s32[32]{0:T(128)} %param.31), kind=kLoop, calls=%fused_computation.66 | loop fusion | flops 192 | bytes 160 | tf_op jit(solution)/shard_map/jit(_take)/and | solution.py:321
  1.5 0.7 %fusion.43 = (f32[32]{0:T(128)S(1)}, f32[1,32]{1,0:T(1,128)S(1)}, s32[32]{0:T(128)S(1)}) fusion(s32[32]{0:T(128)} %param.31), kind=kLoop, calls=%fused_computation.87 | loop fusion | flops 128 | bytes 512 | tf_op jit(solution)/shard_map/convert_element_type | solution.py:340
  2.2 0.7 %and_select_fusion.1 = (s32[32]{0:T(128)S(1)}, s32[32]{0:T(128)S(1)}) fusion(s32[32]{0:T(128)} %param.32), kind=kLoop, calls=%fused_computation.68 | loop fusion | flops 608 | bytes 384 | tf_op jit(solution)/shard_map/jit(remainder)/select_n | solution.py:305
  2.9 4.9 %shard_map.202 = (f32[24,8,20]{2,1,0:T(8,128)}, f32[24,8,18]{2,1,0:T(8,128)}, f32[24,20,128]{2,1,0:T(8,128)}, f32[24,18,128]{2,1,0:T(8,128)}) custom-call(f32[24,8,128]{2,1,0:T(8,128)} %pn_ref, f32[24,8,128]{2,1,0:T(8,128)} %sn_ref, f32[4,2,24,8,128]{4,3,2,1,0:T(8,128)} %dn_ref, f32[4,2,24,8,128]{4,3,2,1,0:T(8,128)} %wn_ref, f32[24,8,128]{2,1,0:T(8,128)} %tx_ref.3, ...), custom_call_target="tpu_custom_call" | custom-call | flops 3932160 | bytes 2162688 | tf_op jit(solution)/shard_map/pallas_call | solution.py:281
  7.9 0.3 fusion.5
  8.2 0.3 fusion.4
  8.5 0.7 %fusion.3 = f32[4,2,24,32]{3,2,1,0:T(8,128)S(1)} fusion(f32[4,2,24,8,128]{4,3,2,1,0:T(8,128)S(1)} %copy-done.1, f32[8,32]{1,0:T(8,128)S(1)} %fusion.32, s32[32]{0:T(128)S(1)} %get-tuple-element.59), kind=kOutput, calls=%fused_computation.6 | convolution fusion | flops 75593728 | bytes 812160 | tf_op jit(solution)/shard_map/dot_general | solution.py:309
  9.2 0.7 %fusion.2 = f32[4,2,24,32]{3,2,1,0:T(8,128)S(1)} fusion(f32[4,2,24,8,128]{4,3,2,1,0:T(8,128)S(1)} %copy-done, f32[8,32]{1,0:T(8,128)S(1)} %fusion.32, s32[32]{0:T(128)S(1)} %get-tuple-element.59), kind=kOutput, calls=%fused_computation.5 | convolution fusion | flops 75593728 | bytes 812160 | tf_op jit(solution)/shard_map/dot_general | solution.py:309
  9.9 0.4 copy.28
  10.3 0.6 %gather_fusion = f32[32,2]{1,0:T(8,128)S(1)} fusion(f32[2,2048]{0,1:T(8,128)S(1)} %copy.28, s32[1024]{0:T(1024)S(1)} %pad_clamp_fusion), kind=kCustom, calls=%fused_computation | custom fusion | bytes 640 | tf_op jit(solution)/shard_map/jit(_take)/gather | solution.py:321
  11.4 0.8 %broadcast_in_dim.43 = f32[128,1,352]{2,1,0:T(1,128)} broadcast(f32[352]{0:T(512)S(1)} %broadcast_in_dim.42), dimensions={2} | broadcast | bytes 181632 | tf_op jit(solution)/shard_map/broadcast_in_dim | solution.py:21
  12.2 10.5 %all-to-all-start = ((f32[128,1,352]{2,1,0:T(1,128)}), f32[128,1,352]{2,1,0:T(1,128)S(1)}, u32[]{:S(2)}, u32[]{:S(2)}) async-start(f32[128,1,352]{2,1,0:T(1,128)} %broadcast_in_dim.43), calls=%async_computation | async-start | bytes 393216 | tf_op jit(solution)/shard_map/all_to_all | solution.py:22
  22.7 3.1 %collective-permute-start = (f32[24,8,20]{2,1,0:T(8,128)S(1)}, f32[24,8,20]{2,1,0:T(8,128)S(1)}, u32[]{:S(2)}, u32[]{:S(2)}) collective-permute-start(f32[24,8,20]{2,1,0:T(8,128)S(1)} %copy-done.14), channel_id=1, source_target_pairs={{0,32},{32,64},{64,96},{1,33},{33,65},{65,97},{2,34},{34,66},{66,9... | collective-permute-start | bytes 46088 | tf_op jit(solution)/shard_map/ppermute | solution.py:30
  25.9 2.2 %collective-permute-start.1 = (f32[24,8,18]{2,1,0:T(8,128)S(1)}, f32[24,8,18]{2,1,0:T(8,128)S(1)}, u32[]{:S(2)}, u32[]{:S(2)}) collective-permute-start(f32[24,8,18]{2,1,0:T(8,128)S(1)} %copy-done.15), channel_id=1, source_target_pairs={{32,0},{64,32},{96,64},{33,1},{65,33},{97,65},{34,2},{66,34},{98,6... | collective-permute-start | bytes 41480 | tf_op jit(solution)/shard_map/ppermute | solution.py:30
  28.1 4.0 %collective-permute-start.2 = (f32[24,20,128]{2,1,0:T(8,128)S(1)}, f32[24,20,128]{2,1,0:T(8,128)S(1)}, u32[]{:S(2)}, u32[]{:S(2)}) collective-permute-start(f32[24,20,128]{2,1,0:T(8,128)S(1)} %copy-done.12), channel_id=1, source_target_pairs={{0,1},{1,2},{2,3},{3,4},{4,5},{5,6},{6,7},{7,8},{8,9},{9,10},{10,1... | collective-permute-start | bytes 737288 | tf_op jit(solution)/shard_map/ppermute | solution.py:30
  32.1 1.9 %collective-permute-start.3 = (f32[24,18,128]{2,1,0:T(8,128)S(1)}, f32[24,18,128]{2,1,0:T(8,128)S(1)}, u32[]{:S(2)}, u32[]{:S(2)}) collective-permute-start(f32[24,18,128]{2,1,0:T(8,128)S(1)} %copy-done.13), channel_id=1, source_target_pairs={{1,0},{2,1},{3,2},{4,3},{5,4},{6,5},{7,6},{8,7},{9,8},{10,9},{11,1... | collective-permute-start | bytes 663560 | tf_op jit(solution)/shard_map/ppermute | solution.py:30
  34.4 0.2 copy.31
  34.6 0.3 reshape.530
  34.9 0.4 fusion.8
  35.5 2.3 %fusion.spread_ref = f32[9,2,24,8,128]{4,3,2,1,0:T(8,128)} fusion(f32[8,32]{1,0:T(8,128)S(1)} %fusion.32, f32[9,2,24,32]{3,2,1,0:T(8,128)S(1)} %maximum_maximum_fusion, s32[32]{0:T(128)S(1)} %get-tuple-element.59), kind=kOutput, calls=%fused_computation.1 | convolution fusion | flops 169984000 | bytes 1825920 | tf_op jit(solution)/shard_map/dot_general | solution.py:357
  37.8 4.4 %collective-permute-done.3.hyu_ref = f32[24,18,128]{2,1,0:T(8,128)S(1)} collective-permute-done((f32[24,18,128]{2,1,0:T(8,128)S(1)}, f32[24,18,128]{2,1,0:T(8,128)S(1)}, u32[]{:S(2)}, u32[]{:S(2)}) %collective-permute-start.3) | collective-permute-done | bytes 221216 | tf_op jit(solution)/shard_map/ppermute | solution.py:30
  42.2 0.7 %copy-done.5 = f32[24,18,128]{2,1,0:T(8,128)} copy-done((f32[24,18,128]{2,1,0:T(8,128)}, f32[24,18,128]{2,1,0:T(8,128)S(1)}, u32[]{:S(2)}) %copy-start.5) | copy-done | bytes 221208
  42.9 0.7 %copy-done.4 = f32[24,20,128]{2,1,0:T(8,128)} copy-done((f32[24,20,128]{2,1,0:T(8,128)}, f32[24,20,128]{2,1,0:T(8,128)S(1)}, u32[]{:S(2)}) %copy-start.4) | copy-done | bytes 245784
  43.7 7.4 %shard_map.203 = (f32[2,24,8,128]{3,2,1,0:T(8,128)}, f32[4,2,24,8,128]{4,3,2,1,0:T(8,128)}, f32[4,2,24,8,128]{4,3,2,1,0:T(8,128)}) custom-call(f32[24,8,128]{2,1,0:T(8,128)} %pn_ref, f32[24,8,128]{2,1,0:T(8,128)} %sn_ref, f32[24,8,128]{2,1,0:T(8,128)} %so_ref.1, f32[24,8,128]{2,1,0:T(8,128)} %pore_ref.1, f32[24,8,128]{2,1,0:T(8,128)} %tx_ref.3, ...), custom_call_target="tpu_custom_call" | custom-call | flops 29491200 | bytes 9043968 | tf_op jit(solution)/shard_map/pallas_call | solution.py:374
  (66 shorter events, 1.0 us)
Async XLA Ops:
  0.6 7.8 %copy-start.1 = (f32[4,2,24,8,128]{4,3,2,1,0:T(8,128)S(1)}, f32[4,2,24,8,128]{4,3,2,1,0:T(8,128)}, u32[]{:S(2)}) copy-start(f32[4,2,24,8,128]{4,3,2,1,0:T(8,128)} %wn_ref) | copy-start | bytes 2359300
  0.6 8.5 %copy-start = (f32[4,2,24,8,128]{4,3,2,1,0:T(8,128)S(1)}, f32[4,2,24,8,128]{4,3,2,1,0:T(8,128)}, u32[]{:S(2)}) copy-start(f32[4,2,24,8,128]{4,3,2,1,0:T(8,128)} %dn_ref) | copy-start | bytes 2359300
  0.7 7.5 %copy-start.3 = (f32[24,8,128]{2,1,0:T(8,128)S(1)}, f32[24,8,128]{2,1,0:T(8,128)}, u32[]{:S(2)}) copy-start(f32[24,8,128]{2,1,0:T(8,128)} %sn_ref) | copy-start | bytes 294916
  0.7 7.2 %copy-start.2 = (f32[24,8,128]{2,1,0:T(8,128)S(1)}, f32[24,8,128]{2,1,0:T(8,128)}, u32[]{:S(2)}) copy-start(f32[24,8,128]{2,1,0:T(8,128)} %pn_ref) | copy-start | bytes 294916
  2.9 7.0 %copy-start.8 = (f32[2048]{0:T(1024)S(1)}, f32[2048]{0:T(1024)}, u32[]{:S(2)}) copy-start(f32[2048]{0:T(1024)} %param.37) | copy-start | bytes 24580
  2.9 7.0 %copy-start.9 = (f32[2048]{0:T(1024)S(1)}, f32[2048]{0:T(1024)}, u32[]{:S(2)}) copy-start(f32[2048]{0:T(1024)} %param.36) | copy-start | bytes 24580
  7.9 3.1 %copy-start.11 = (s32[32]{0:T(128)S(1)}, s32[32]{0:T(128)}, u32[]{:S(2)}) copy-start(s32[32]{0:T(128)} %param.33) | copy-start | bytes 388
  7.9 3.1 %copy-start.16 = (s32[32]{0:T(128)S(1)}, s32[32]{0:T(128)}, u32[]{:S(2)}) copy-start(s32[32]{0:T(128)} %param.34) | copy-start | bytes 388
  7.9 3.1 %copy-start.10 = (f32[32]{0:T(128)S(1)}, f32[32]{0:T(128)}, u32[]{:S(2)}) copy-start(f32[32]{0:T(128)} %param.35) | copy-start | bytes 388
  9.2 13.6 %copy-start.14 = (f32[24,8,20]{2,1,0:T(8,128)S(1)}, f32[24,8,20]{2,1,0:T(8,128)}, u32[]{:S(2)}) copy-start(f32[24,8,20]{2,1,0:T(8,128)} %get-tuple-element.23) | copy-start | bytes 46084
  9.2 16.7 %copy-start.15 = (f32[24,8,18]{2,1,0:T(8,128)S(1)}, f32[24,8,18]{2,1,0:T(8,128)}, u32[]{:S(2)}) copy-start(f32[24,8,18]{2,1,0:T(8,128)} %get-tuple-element.24) | copy-start | bytes 41476
  9.2 18.9 %copy-start.12 = (f32[24,20,128]{2,1,0:T(8,128)S(1)}, f32[24,20,128]{2,1,0:T(8,128)}, u32[]{:S(2)}) copy-start(f32[24,20,128]{2,1,0:T(8,128)} %get-tuple-element.25) | copy-start | bytes 737284
  9.2 22.9 %copy-start.13 = (f32[24,18,128]{2,1,0:T(8,128)S(1)}, f32[24,18,128]{2,1,0:T(8,128)}, u32[]{:S(2)}) copy-start(f32[24,18,128]{2,1,0:T(8,128)} %get-tuple-element.26) | copy-start | bytes 663556
  12.2 21.8 %all-to-all-start = ((f32[128,1,352]{2,1,0:T(1,128)}), f32[128,1,352]{2,1,0:T(1,128)S(1)}, u32[]{:S(2)}, u32[]{:S(2)}) async-start(f32[128,1,352]{2,1,0:T(1,128)} %broadcast_in_dim.43), calls=%async_computation | async-start | bytes 393216 | tf_op jit(solution)/shard_map/all_to_all | solution.py:22
  22.7 15.0 %collective-permute-start = (f32[24,8,20]{2,1,0:T(8,128)S(1)}, f32[24,8,20]{2,1,0:T(8,128)S(1)}, u32[]{:S(2)}, u32[]{:S(2)}) collective-permute-start(f32[24,8,20]{2,1,0:T(8,128)S(1)} %copy-done.14), channel_id=1, source_target_pairs={{0,32},{32,64},{64,96},{1,33},{33,65},{65,97},{2,34},{34,66},{66,9... | collective-permute-start | bytes 46088 | tf_op jit(solution)/shard_map/ppermute | solution.py:30
  25.9 11.9 %collective-permute-start.1 = (f32[24,8,18]{2,1,0:T(8,128)S(1)}, f32[24,8,18]{2,1,0:T(8,128)S(1)}, u32[]{:S(2)}, u32[]{:S(2)}) collective-permute-start(f32[24,8,18]{2,1,0:T(8,128)S(1)} %copy-done.15), channel_id=1, source_target_pairs={{32,0},{64,32},{96,64},{33,1},{65,33},{97,65},{34,2},{66,34},{98,6... | collective-permute-start | bytes 41480 | tf_op jit(solution)/shard_map/ppermute | solution.py:30
  28.1 14.2 %collective-permute-start.2 = (f32[24,20,128]{2,1,0:T(8,128)S(1)}, f32[24,20,128]{2,1,0:T(8,128)S(1)}, u32[]{:S(2)}, u32[]{:S(2)}) collective-permute-start(f32[24,20,128]{2,1,0:T(8,128)S(1)} %copy-done.12), channel_id=1, source_target_pairs={{0,1},{1,2},{2,3},{3,4},{4,5},{5,6},{6,7},{7,8},{8,9},{9,10},{10,1... | collective-permute-start | bytes 737288 | tf_op jit(solution)/shard_map/ppermute | solution.py:30
  32.1 10.2 %collective-permute-start.3 = (f32[24,18,128]{2,1,0:T(8,128)S(1)}, f32[24,18,128]{2,1,0:T(8,128)S(1)}, u32[]{:S(2)}, u32[]{:S(2)}) collective-permute-start(f32[24,18,128]{2,1,0:T(8,128)S(1)} %copy-done.13), channel_id=1, source_target_pairs={{1,0},{2,1},{3,2},{4,3},{5,4},{6,5},{7,6},{8,7},{9,8},{10,9},{11,1... | collective-permute-start | bytes 663560 | tf_op jit(solution)/shard_map/ppermute | solution.py:30
  37.8 4.4 %copy-start.7 = (f32[24,8,18]{2,1,0:T(8,128)}, f32[24,8,18]{2,1,0:T(8,128)S(1)}, u32[]{:S(2)}) copy-start(f32[24,8,18]{2,1,0:T(8,128)S(1)} %collective-permute-done.1.hxr_ref) | copy-start | bytes 41476
  37.8 4.4 %copy-start.6 = (f32[24,8,20]{2,1,0:T(8,128)}, f32[24,8,20]{2,1,0:T(8,128)S(1)}, u32[]{:S(2)}) copy-start(f32[24,8,20]{2,1,0:T(8,128)S(1)} %collective-permute-done.hxl_ref) | copy-start | bytes 46084
  42.2 0.7 %copy-start.5 = (f32[24,18,128]{2,1,0:T(8,128)}, f32[24,18,128]{2,1,0:T(8,128)S(1)}, u32[]{:S(2)}) copy-start(f32[24,18,128]{2,1,0:T(8,128)S(1)} %collective-permute-done.3.hyu_ref) | copy-start | bytes 663556
  42.9 0.7 %copy-start.4 = (f32[24,20,128]{2,1,0:T(8,128)}, f32[24,20,128]{2,1,0:T(8,128)S(1)}, u32[]{:S(2)}) copy-start(f32[24,20,128]{2,1,0:T(8,128)S(1)} %collective-permute-done.2.hyd_ref) | copy-start | bytes 737284
